TPU v7x, 128 devices: a whole 4x4x4 slice. The times are simulated.
128 devices in a mesh: dp: 4 (over z), fsdp: 32 (over x, y, core).
Axes of the slice: x: 4, y: 4, z: 4, core: 2. Of those that a mesh axis runs over, the one named last changes fastest.
Arguments:
- frames: bfloat16 [131072, 1024], P(('dp', 'fsdp')), may hold values from -6 to 6
- llm_grad: bfloat16 [131072, 1024], P(('dp', 'fsdp')), may hold values from -6 to 6
- dest_rank: int32 [128, 128], P(('dp', 'fsdp')), may hold values from 0 to 127, as said below
- utt_lengths: int32 [128, 4], P(('dp', 'fsdp')), may hold values from 1 to 512, 1024 in all within a row
- valid: int32 [131072], P(('dp', 'fsdp')), may hold values 0 or 1
- norm_gain: float32 [1024], replicated, may hold values from 0.25 to 1.75
- up_weight: bfloat16 [1024, 2048], P('fsdp'), may hold values from -0.1875 to 0.1875
- kernel: float32 [9, 1024], replicated, may hold values from -2 to 2
- down_weight: bfloat16 [1024, 1024], P('fsdp'), may hold values from -0.1875 to 0.1875
Outputs:
- input_grad: bfloat16 [131072, 1024], P(('dp', 'fsdp'))
- up_grad: float32 [1024, 2048], P('fsdp')
- down_grad: float32 [1024, 1024], P('fsdp')
- kernel_grad: float32 [9, 1024], replicated
- gain_grad: float32 [1024], replicated
Inputs may be any that keep to these rules, and one draw needn't show every extreme that they name: `dest_rank`: each language-model rank sends its blocks in groups of 1 block, all of one group to one encoder rank and different groups to different ranks; every encoder block j is named by exactly one rank.
All inputs are finite; a program needn't handle non-finite values. No bound on the sum of `valid` on one device may be relied on, other than what follows from the above.
Results may differ from a plain program's by a relative error of at most 0.025.
Values may be sent and summed in bfloat16 or wider, within the bound.
No kernel may reach another device: no remote copies, remote signals or barrier semaphores. Data moves between devices by JAX's collectives and lax.ppermute only.
A program may use at most 256 MiB of HBM per device.

v0:
```python
import jax
import jax.numpy as jnp
from jax import lax
from jax.sharding import PartitionSpec as P

CAPB = 1


def shift_rows(values, offset, fill):
    rows = values.shape[0]
    if offset == 0:
        return values
    pad = jnp.full((abs(offset),) + values.shape[1:], fill, values.dtype)
    if offset > 0:
        return jnp.concatenate([values[offset:], pad], axis=0)
    return jnp.concatenate([pad, values[: rows + offset]], axis=0)


def segment_of(lengths, rows):
    ends = jnp.cumsum(lengths)
    place = jnp.arange(rows, dtype=jnp.int32)
    return jnp.sum((place[:, None] >= ends[None, :]).astype(jnp.int32), axis=1)


def contract_rows(left, right):
    return lax.dot_general(
        left, right, (((0,), (0,)), ((), ())), preferred_element_type=jnp.float32
    )


def on_device(
    frames, llm_grad, dest_rank, utt_lengths, valid, norm_gain, up_weight, kernel, down_weight
):
    rows, width = frames.shape
    n_data = lax.axis_size("dp")
    n_shard = lax.axis_size("fsdp")
    ranks = n_data * n_shard
    blocks_dev = dest_rank.shape[1]
    block_rows = rows // blocks_dev
    targets = dest_rank[0]
    slots = jnp.arange(blocks_dev, dtype=jnp.int32) % CAPB
    block_ids = jnp.arange(blocks_dev, dtype=jnp.int32)
    grad_blocks = llm_grad.reshape(blocks_dev, block_rows, width)
    outbox = (
        jnp.zeros((ranks, CAPB, block_rows, width), jnp.bfloat16)
        .at[targets, slots]
        .set(grad_blocks)
    )
    labels = jnp.full((ranks, CAPB), -1, jnp.int32).at[targets, slots].set(block_ids)
    got_rows, got_labels = (
        lax.all_to_all(
            outbox.reshape(ranks, CAPB * block_rows, width),
            ("dp", "fsdp"),
            split_axis=0,
            concat_axis=0,
            tiled=True,
        ),
        lax.all_to_all(labels, ("dp", "fsdp"), split_axis=0, concat_axis=0, tiled=True),
    )
    got_labels = got_labels.reshape(ranks * CAPB)
    places = jnp.where(got_labels >= 0, got_labels, blocks_dev)
    out_grad = (
        jnp.zeros((blocks_dev + 1, block_rows, width), jnp.bfloat16)
        .at[places]
        .set(got_rows)[:blocks_dev]
        .reshape(rows, width)
    )
    up_full = lax.all_gather(up_weight, "fsdp", axis=0, tiled=True)
    down_full = lax.all_gather(down_weight, "fsdp", axis=0, tiled=True)
    taps = kernel.shape[0]
    middle = (taps - 1) // 2
    seg = segment_of(utt_lengths[0], rows)
    xf = frames.astype(jnp.float32)
    mean = jnp.mean(xf, axis=1, keepdims=True)
    var = jnp.mean((xf - mean) ** 2, axis=1, keepdims=True)
    rstd = lax.rsqrt(var + 1e-05)
    normed = (xf - mean) * rstd
    hidden = (normed * norm_gain[None, :]).astype(jnp.bfloat16)
    up = jnp.dot(hidden, up_full, preferred_element_type=jnp.float32)
    value = up[:, :width]
    sig_b = jax.nn.sigmoid(up[:, width:])
    glu = (value * sig_b).astype(jnp.bfloat16)
    glu_f = glu.astype(jnp.float32)
    keep = valid.astype(jnp.float32)[:, None]
    sames = []
    conv = jnp.zeros((rows, width), jnp.float32)
    for k in range(taps):
        offset = k - middle
        same = (shift_rows(seg, offset, -1) == seg).astype(jnp.float32)[:, None]
        sames.append(same)
        conv = conv + kernel[k][None, :] * shift_rows(glu_f, offset, 0.0) * same
    conv = conv * keep
    sig_c = jax.nn.sigmoid(conv)
    act = (conv * sig_c).astype(jnp.bfloat16)
    act_grad = jnp.dot(out_grad, down_full.T, preferred_element_type=jnp.float32)
    conv_grad = act_grad * sig_c * (1.0 + conv * (1.0 - sig_c)) * keep
    kernel_rows = []
    glu_grad = jnp.zeros((rows, width), jnp.float32)
    for k in range(taps):
        offset = k - middle
        masked = conv_grad * sames[k]
        kernel_rows.append(jnp.sum(masked * shift_rows(glu_f, offset, 0.0), axis=0))
        glu_grad = glu_grad + kernel[k][None, :] * shift_rows(masked, -offset, 0.0)
    kernel_term = jnp.stack(kernel_rows, axis=0)
    value_grad = glu_grad * sig_b
    gate_grad = glu_grad * value * sig_b * (1.0 - sig_b)
    up_out_grad = jnp.concatenate([value_grad, gate_grad], axis=1).astype(jnp.bfloat16)
    hidden_grad = jnp.dot(up_out_grad, up_full.T, preferred_element_type=jnp.float32)
    gain_term = jnp.sum(hidden_grad * normed, axis=0)
    scaled = hidden_grad * norm_gain[None, :]
    input_grad = rstd * (
        scaled
        - jnp.mean(scaled, axis=1, keepdims=True)
        - normed * jnp.mean(scaled * normed, axis=1, keepdims=True)
    )
    left_hidden, left_act = (hidden, act)
    shard_sum = lax.psum_scatter(
        jnp.concatenate(
            [contract_rows(left_hidden, up_out_grad), contract_rows(left_act, out_grad)], axis=1
        ).astype(jnp.bfloat16),
        "fsdp",
        scatter_dimension=0,
        tiled=True,
    ).astype(jnp.float32)
    shard_sum = lax.psum(shard_sum.astype(jnp.bfloat16), "dp").astype(jnp.float32)
    kernel_grad, gain_grad = lax.psum((kernel_term, gain_term), ("dp", "fsdp"))
    return (
        input_grad.astype(jnp.bfloat16),
        shard_sum[:, : 2 * width],
        shard_sum[:, 2 * width :],
        kernel_grad,
        gain_grad,
    )


def solution(mesh):
    return jax.shard_map(
        on_device,
        mesh=mesh,
        in_specs=(
            P(("dp", "fsdp"), None),
            P(("dp", "fsdp"), None),
            P(("dp", "fsdp"), None),
            P(("dp", "fsdp"), None),
            P(("dp", "fsdp")),
            P(),
            P("fsdp", None),
            P(),
            P("fsdp", None),
        ),
        out_specs=(P(("dp", "fsdp"), None), P("fsdp", None), P("fsdp", None), P(), P()),
        check_vma=False,
    )
```

profile of v0, /device:TPU:0, one launch (start us, length us, event | category | flops | bytes accessed | tf_op | source)
XLA Modules:
  0.0 390.3 jit_solution(12550658970036619461)
XLA Ops:
  7.2 0.7 all-gather.5.cloned.1.call-update
  7.9 0.7 fusion.31
  8.6 1.0 scatter_custom_fusion
  9.6 0.7 copy.26
  10.3 11.2 %all-to-all-start = ((s32[128,1,1]{2,1,0:T(1,128)}), s32[128,1,1]{2,1,0:T(1,128)S(1)}, u32[]{:S(2)}, u32[]{:S(2)}) async-start(s32[128,1,1]{2,1,0:T(1,128)} %copy.26), calls=%async_computation | async-start | bytes 131072 | tf_op jit(solution)/shard_map/all_to_all | solution.py:58
  21.5 0.7 all-gather.3.cloned.1.call-update
  22.2 2.9 copy.25
  25.1 0.4 convert_reduce_fusion
  25.5 0.2 reduce-window.8
  25.7 1.6 broadcast.185
  27.2 17.7 %scatter_fusion = bf16[128,8,1024]{2,1,0:T(8,128)(2,1)} fusion(bf16[128,8,1024]{2,1,0:T(8,128)(2,1)} %broadcast.185, s32[128]{0:T(128)S(1)} %fusion.31, bf16[128,8,1024]{2,1,0:T(8,128)(2,1)} %bitcast.50), kind=kCustom, calls=%fused_computation.1 | custom fusion | bytes 6291968 | tf_op jit(solution)/shard_map/scatter | solution.py:47
  44.9 10.2 %all-to-all-start.1 = ((bf16[128,8,1024]{2,1,0:T(8,128)(2,1)}), bf16[128,8,1024]{2,1,0:T(8,128)(2,1)}, u32[]{:S(2)}, u32[]{:S(2)}) async-start(bf16[128,8,1024]{2,1,0:T(8,128)(2,1)} %scatter_fusion), calls=%async_computation.1 | async-start | bytes 4194304 | tf_op jit(solution)/shard_map/all_to_all | solution.py:51
  55.2 0.1 convert_reduce_fusion.1
  55.3 0.6 fusion.12
  56.3 2.4 reduce
  58.7 27.0 %all-to-all-done.1 = bf16[128,8,1024]{2,1,0:T(8,128)(2,1)} async-done(((bf16[128,8,1024]{2,1,0:T(8,128)(2,1)}), bf16[128,8,1024]{2,1,0:T(8,128)(2,1)}, u32[]{:S(2)}, u32[]{:S(2)}) %all-to-all-start.1) | async-done | bytes 2097184 | tf_op jit(solution)/shard_map/all_to_all | solution.py:51
  85.7 1.6 broadcast_in_dim.7
  87.4 17.9 %scatter_fusion.1 = bf16[129,8,1024]{2,1,0:T(8,128)(2,1)} fusion(bf16[129,8,1024]{2,1,0:T(8,128)(2,1)} %broadcast_in_dim.7, s32[128]{0:T(128)S(1)} %fusion.32, bf16[128,8,1024]{2,1,0:T(8,128)(2,1)} %all-to-all-done.1), kind=kCustom, calls=%fused_computation.2 | custom fusion | bytes 6291968 | tf_op jit(solution)/shard_map/scatter | solution.py:65
  105.3 6.7 %fusion.21 = f32[1024,2048]{1,0:T(8,128)S(1)} fusion(bf16[1024,2048]{1,0:T(8,128)(2,1)} %all-gather.5.cloned.1.call-done, bf16[1024,1024]{0,1:T(8,128)(2,1)S(1)} %copy.25, f32[1024]{0:T(1024)S(1)} %copy-done.16, f32[1024]{0:T(1024)S(1)} %add_rsqrt_fusion, f32[1024]{0:T(1024)S(1)} %broadcast_multiply_fusion.10), kind=kOutput, calls=%fused_computation.56 | convolution fusion | flops 4300210176 | bytes 14692352 | tf_op jit(solution)/shard_map/dot_general | solution.py:79
  112.0 1.5 fusion.17
  113.6 1.2 fusion.41
  114.8 4.7 %fusion.40 = (f32[1022,1024]{1,0:T(8,128)}, f32[1022,1024]{1,0:T(8,128)}) fusion(f32[1024,1024]{1,0:T(8,128)S(1)} %fusion.17), kind=kLoop, calls=%fused_computation.91 | loop fusion | bytes 16744448 | tf_op jit(solution)/shard_map/slice | solution.py:16
  119.5 4.4 %fusion.39 = (f32[1021,1024]{1,0:T(8,128)}, f32[1021,1024]{1,0:T(8,128)}) fusion(f32[1024,1024]{1,0:T(8,128)S(1)} %fusion.17), kind=kLoop, calls=%fused_computation.90 | loop fusion | bytes 16728064 | tf_op jit(solution)/shard_map/slice | solution.py:16
  124.0 4.1 %fusion.38 = (f32[1020,1024]{1,0:T(8,128)}, f32[1020,1024]{1,0:T(8,128)}) fusion(f32[1024,1024]{1,0:T(8,128)S(1)} %fusion.17), kind=kLoop, calls=%fused_computation.89 | loop fusion | bytes 16711680 | tf_op jit(solution)/shard_map/slice | solution.py:16
  128.1 11.8 %add_multiply_fusion = f32[1024,1024]{1,0:T(8,128)S(1)} fusion(f32[1020,1024]{1,0:T(8,128)} %get-tuple-element.65, f32[1021,1024]{1,0:T(8,128)} %get-tuple-element.67, f32[1022,1024]{1,0:T(8,128)} %get-tuple-element.69, f32[1023,1024]{1,0:T(8,128)S(1)} %get-tuple-element.71, f32[1023,1024]{1,0:T(8,128)S(1)} %get-tuple-element.70, ...), kind=kLoop, calls=%fused_computation.39 | loop fusion | flops 33554432 | bytes 46129152 | tf_op jit(solution)/shard_map/mul | solution.py:92
  139.9 1.9 copy-done.8
  141.8 3.9 %fusion.19 = bf16[1024,1024]{1,0:T(8,128)(2,1)} fusion(f32[1024,1024]{1,0:T(8,128)S(1)} %add_multiply_fusion, bf16[129,8,1024]{2,1,0:T(8,128)(2,1)S(1)} %copy-done.6), kind=kOutput, calls=%fused_computation.55 | convolution fusion | flops 2153775104 | bytes 8388608 | tf_op jit(solution)/shard_map/dot_general | solution.py:26
  145.8 28.1 %multiply_reduce_fusion.8 = (f32[1024]{0:T(1024)S(1)}, f32[1024,1024]{1,0:T(8,128)}, f32[1024]{0:T(1024)S(1)}, f32[1024]{0:T(1024)S(1)}, f32[1024,1024]{1,0:T(8,...) fusion(f32[1020,1024]{1,0:T(8,128)} %get-tuple-element.64, ...), kind=kOutput, calls=%fused_computation.32 | convolution fusion | flops 2184174592 | bytes 83877888 | tf_op jit(solution)/shard_map/dot_general | solution.py:95
  173.9 5.2 %slice.184 = f32[1020,1024]{1,0:T(8,128)} slice(f32[1024,1024]{1,0:T(8,128)} %get-tuple-element.45), slice={[4:1024], [0:1024]} | slice | bytes 8355840 | tf_op jit(solution)/shard_map/slice | solution.py:15
  179.1 2.6 slice.187
  181.7 1.1 copy-done.10
  182.8 2.6 slice.186
  185.4 1.1 copy-done.9
  186.5 2.6 slice.185
  189.1 1.1 copy-done.12
  190.2 17.6 %multiply_convert_fusion.2 = (bf16[1024,1024]{1,0:T(8,128)(2,1)}, f32[1024,1024]{1,0:T(8,128)}) fusion(f32[1024,2048]{1,0:T(8,128)} %copy-done.1, f32[1020,1024]{1,0:T(8,128)S(1)} %bitcast.46, f32[1024]{0:T(1024)S(1)} %bitcast.66, f32[1021,1024]{1,0:T(8,128)} %bitcast.47, f32[1024]{0:T(1024)S(1)} %bitcast.68, f32[1022,1024]{1,0:T(8,128)} %bitcast.48, ...), kind=kLoop, calls=%fused_computation.35 | loop fusion | flops 23068672 | bytes 48189440 | tf_op jit(solution)/shard_map/convert.2
  207.8 5.7 %multiply_convert_fusion.1 = bf16[1024,1024]{1,0:T(8,128)(2,1)S(1)} fusion(f32[1024,1024]{1,0:T(8,128)} %get-tuple-element.47, f32[1024,2048]{1,0:T(8,128)} %copy-done.1), kind=kLoop, calls=%fused_computation.34 | loop fusion | flops 8388608 | bytes 14680064 | tf_op jit(solution)/shard_map/convert.3
  213.5 1.3 copy-done.14
  214.8 4.9 %convolution_convert_fusion = bf16[1024,2048]{1,0:T(8,128)(2,1)S(1)} fusion(bf16[1024,1024]{1,0:T(8,128)(2,1)S(1)} %multiply_convert_fusion.1, bf16[1024,1024]{1,0:T(8,128)(2,1)S(1)} %copy-done.13, bf16[1024,1024]{0,1:T(8,128)(2,1)S(1)} %copy-done.5, f32[1024]{0:T(1024)S(1)} %copy-done.16, f32[1024]{0:T(1024)S(1)} %add_rsqrt_fusion, ...), kind=kOutput, calls=%fused_computation.41 | convolution fusion | flops 4310695936 | bytes 10498048 | tf_op jit(solution)/shard_map/dot_general | solution.py:26
  219.7 4.8 %pad_maximum_fusion = bf16[1024,3072]{1,0:T(8,128)(2,1)} fusion(bf16[1024,1024]{1,0:T(8,128)(2,1)} %fusion.19, bf16[1024,2048]{1,0:T(8,128)(2,1)S(1)} %convolution_convert_fusion), kind=kLoop, calls=%fused_computation.3 | loop fusion | flops 12582912 | bytes 12582912 | tf_op jit(solution)/shard_map/concatenate | solution.py:118
  224.6 0.3 all-reduce.26.cloned.1.call-start
  224.9 10.4 %fusion.11 = (f32[1024]{0:T(1024)S(1)}, f32[1024]{0:T(1024)S(1)}, f32[1024]{0:T(1024)S(1)}, f32[1024,1024]{0,1:T(8,128)}) fusion(bf16[1024,1024]{0,1:T(8,128)(2,1)S(1)} %copy-done.5, f32[1024]{0:T(1024)S(1)} %add_rsqrt_fusion, f32[1024]{0:T(1024)S(1)} %broadcast_multiply_fusion.10, f32[1024]{0:T(1024)S(1)} %copy-done.16, ...), kind=kOutput, calls=%fused_computation.17 | convolution fusion | flops 4312790016 | bytes 14704640 | tf_op jit(solution)/shard_map/dot_general | solution.py:108
  235.3 70.5 %reduce-scatter.2.cloned.1.call-done = bf16[32,3072]{1,0:T(8,128)(2,1)} async-done(((bf16[1024,3072]{1,0:T(8,128)(2,1)}), bf16[32,3072]{1,0:T(8,128)(2,1)}) %reduce-scatter.2.cloned.1.call-update) | async-done | bytes 196624 | tf_op jit(solution)/shard_map/reduce_scatter | solution.py:117
  305.9 4.7 %fusion.10 = bf16[1024,1024]{0,1:T(8,128)(2,1)} fusion(bf16[1024,1024]{0,1:T(8,128)(2,1)S(1)} %copy-done.5, f32[1024,1024]{0,1:T(8,128)} %get-tuple-element.98, f32[1024]{0:T(1024)S(1)} %get-tuple-element.99, f32[1024]{0:T(1024)S(1)} %get-tuple-element.100, f32[1024]{0:T(1024)S(1)} %copy-done.16, f32[1024]{0:T(1024)S(1)} %add_rsqrt_fusion, ...), kind=kLoop, calls=%fused_computation.16 | loop fusion | flops 9437184 | bytes 8409088 | tf_op jit(solution)/shard_map/convert_element_type | solution.py:128
  310.6 3.9 %copy.28 = bf16[1024,1024]{1,0:T(8,128)(2,1)} copy(bf16[1024,1024]{0,1:T(8,128)(2,1)} %fusion.10) | data formatting | bytes 4194304
  314.6 66.0 %all-reduce.23 = (f32[9,1024]{1,0:T(8,128)}, f32[1024]{0:T(1024)}) all-reduce(f32[9,1024]{1,0:T(8,128)S(1)} %stack.39, f32[1024]{0:T(1024)S(1)} %get-tuple-element.25), channel_id=1, replica_groups=mesh['dp'=4,'fsdp'=32] {'dp','fsdp'}, use_global_device_ids=true, to_apply=%region_20.21 | all-reduce | flops 10240 | bytes 81920 | tf_op jit(solution)/shard_map/psum | solution.py:126
  380.6 1.5 slice.193
  382.1 1.6 slice.192
  (55 shorter events, 0.7 us)
Async XLA Ops:
  7.2 18.3 %copy-start.18 = (s32[1,4]{1,0:T(1,128)S(1)}, s32[1,4]{1,0:T(1,128)}, u32[]{:S(2)}) copy-start(s32[1,4]{1,0:T(1,128)} %param.12) | copy-start | bytes 52
  7.2 98.1 %all-gather.5.cloned.1.call-start = ((), (), s32[]{:S(2)}) async-start(), calls=%async_computation.4 | async-start | bytes 4325376 | tf_op jit(solution)/shard_map/all_gather | solution.py:68
  10.3 34.6 %all-to-all-start = ((s32[128,1,1]{2,1,0:T(1,128)}), s32[128,1,1]{2,1,0:T(1,128)S(1)}, u32[]{:S(2)}, u32[]{:S(2)}) async-start(s32[128,1,1]{2,1,0:T(1,128)} %copy.26), calls=%async_computation | async-start | bytes 131072 | tf_op jit(solution)/shard_map/all_to_all | solution.py:58
  21.5 124.3 %all-gather.3.cloned.1.call-start = ((), (), s32[]{:S(2)}) async-start(), calls=%async_computation.3 | async-start | bytes 2162688 | tf_op jit(solution)/shard_map/all_gather | solution.py:69
  25.1 80.2 %copy-start.4 = (bf16[1024,1024]{0,1:T(8,128)(2,1)}, bf16[1024,1024]{0,1:T(8,128)(2,1)S(1)}, u32[]{:S(2)}) copy-start(bf16[1024,1024]{0,1:T(8,128)(2,1)S(1)} %copy.25) | copy-start | bytes 6291460
  27.2 28.1 %copy-start.17 = (s32[1024]{0:T(1024)S(1)}, s32[1024]{0:T(1024)}, u32[]{:S(2)}) copy-start(s32[1024]{0:T(1024)} %param.13) | copy-start | bytes 12292
  44.9 11.4 %copy-start.15 = (f32[9,1024]{1,0:T(8,128)S(1)}, f32[9,1024]{1,0:T(8,128)}, u32[]{:S(2)}) copy-start(f32[9,1024]{1,0:T(8,128)} %param.16) | copy-start | bytes 110596
  44.9 40.8 %all-to-all-start.1 = ((bf16[128,8,1024]{2,1,0:T(8,128)(2,1)}), bf16[128,8,1024]{2,1,0:T(8,128)(2,1)}, u32[]{:S(2)}, u32[]{:S(2)}) async-start(bf16[128,8,1024]{2,1,0:T(8,128)(2,1)} %scatter_fusion), calls=%async_computation.1 | async-start | bytes 4194304 | tf_op jit(solution)/shard_map/all_to_all | solution.py:51
  55.2 250.7 %reduce-scatter.2.cloned.1.call-start = ((), (), s32[]{:S(2)}) async-start(), calls=%async_computation.5 | async-start | bytes 6488064 | tf_op jit(solution)/shard_map/reduce_scatter | solution.py:117
  58.7 46.6 %copy-start.16 = (f32[1024]{0:T(1024)S(1)}, f32[1024]{0:T(1024)}, u32[]{:S(2)}) copy-start(f32[1024]{0:T(1024)} %param.14) | copy-start | bytes 12292
  112.0 16.0 %copy-start.1 = (f32[1024,2048]{1,0:T(8,128)}, f32[1024,2048]{1,0:T(8,128)S(1)}, u32[]{:S(2)}) copy-start(f32[1024,2048]{1,0:T(8,128)S(1)} %fusion.21) | copy-start | bytes 25165828
  113.6 10.4 %copy-start = (f32[1024,1024]{1,0:T(8,128)}, f32[1024,1024]{1,0:T(8,128)S(1)}, u32[]{:S(2)}) copy-start(f32[1024,1024]{1,0:T(8,128)S(1)} %fusion.17) | copy-start | bytes 12582916
  114.8 13.2 %copy-start.2 = (f32[1023,1024]{1,0:T(8,128)}, f32[1023,1024]{1,0:T(8,128)S(1)}, u32[]{:S(2)}) copy-start(f32[1023,1024]{1,0:T(8,128)S(1)} %get-tuple-element.70) | copy-start | bytes 12570628
  114.8 13.2 %copy-start.3 = (f32[1023,1024]{1,0:T(8,128)}, f32[1023,1024]{1,0:T(8,128)S(1)}, u32[]{:S(2)}) copy-start(f32[1023,1024]{1,0:T(8,128)S(1)} %get-tuple-element.71) | copy-start | bytes 12570628
  128.0 13.8 %copy-start.6 = (bf16[129,8,1024]{2,1,0:T(8,128)(2,1)S(1)}, bf16[129,8,1024]{2,1,0:T(8,128)(2,1)}, u32[]{:S(2)}) copy-start(bf16[129,8,1024]{2,1,0:T(8,128)(2,1)} %scatter_fusion.1) | copy-start | bytes 6340612
  139.9 2.0 copy-start.8
  141.8 3.9 %copy-start.7 = (bf16[129,8,1024]{2,1,0:T(8,128)(2,1)S(1)}, bf16[129,8,1024]{2,1,0:T(8,128)(2,1)}, u32[]{:S(2)}) copy-start(bf16[129,8,1024]{2,1,0:T(8,128)(2,1)} %scatter_fusion.1) | copy-start | bytes 6340612
  173.9 5.2 %copy-start.11 = (f32[1024,1024]{1,0:T(8,128)S(1)}, f32[1024,1024]{1,0:T(8,128)}, u32[]{:S(2)}) copy-start(f32[1024,1024]{1,0:T(8,128)} %get-tuple-element.59) | copy-start | bytes 12582916
  179.1 3.7 copy-start.10
  182.8 3.7 copy-start.9
  186.5 3.7 copy-start.12
  207.8 7.0 %copy-start.5 = (bf16[1024,1024]{0,1:T(8,128)(2,1)S(1)}, bf16[1024,1024]{0,1:T(8,128)(2,1)}, u32[]{:S(2)}) copy-start(bf16[1024,1024]{0,1:T(8,128)(2,1)} %copy-done.4) | copy-start | bytes 6291460
  207.8 7.0 %copy-start.13 = (bf16[1024,1024]{1,0:T(8,128)(2,1)S(1)}, bf16[1024,1024]{1,0:T(8,128)(2,1)}, u32[]{:S(2)}) copy-start(bf16[1024,1024]{1,0:T(8,128)(2,1)} %get-tuple-element.46) | copy-start | bytes 6291460
  213.5 1.3 copy-start.14
  224.6 156.0 %all-reduce.26.cloned.1.call-start = ((), (), s32[]{:S(2)}) async-start(), calls=%async_computation.6 | async-start | bytes 393216 | tf_op jit(solution)/shard_map/psum | solution.py:125
Sparse Core Ops, SparseCore 0:
  10.2 48.4 all-gather.4
  61.0 46.8 all-gather.2
  224.7 81.1 reduce-scatter.1
  308.0 41.3 all-reduce.25
where the time goes:
time: 391 us; the launch traced here: 390 us
  waiting for transfers between devices  99 us (25%)
  local copies, waits for them, and re-layouts  84.9 us (22%)
  blocking collectives  66 us (17%)
  matrix products  54.1 us (14%)
  other arithmetic  50.5 us (13%)
  starting transfers between devices  21.8 us (6%)
  between operations  14 us (4%)
    reduce_scatter x1, waiting for transfers between devices, on_device(): lax.psum_scatter(jnp.concatenate([contract_rows(left_hidden, up_out_grad)...  70.5 us
    psum x1, blocking collectives, on_device(): kernel_grad, gain_grad = lax.psum((kernel_term, gain_term), ('dp', 'fsdp'))  66 us
    dot_general x1, matrix products, on_device(): jnp.dot(out_grad, down_full.T, preferred_element_type=jnp.float32)  28.1 us
    all_to_all x1, waiting for transfers between devices, on_device(): lax.all_to_all(outbox.reshape(ranks, CAPB * block_rows, width), ('dp', 'f...  27 us
    another operation x3, other arithmetic  23.4 us
    scatter x1, local copies, waits for them, and re-layouts, on_device(): out_grad = jnp.zeros((blocks_dev + 1, block_rows, width), jnp.bfloat16).a...  17.9 us
    scatter x1, local copies, waits for them, and re-layouts, on_device(): outbox = jnp.zeros((ranks, CAPB, block_rows, width), jnp.bfloat16).at[tar...  17.7 us
    slice x8, local copies, waits for them, and re-layouts, shift_rows(): return jnp.concatenate([pad, values[:rows + offset]], axis=0)  14.7 us
  transfers between devices with their start and end apart: 6, of which 2 were waited for; matrix products, arithmetic and copies ran while one was open for 27% of the time, Pallas kernels for 0%

commit v1 on v0

--- a/solution.py
+++ b/solution.py
@@ -28,6 +28,42 @@
     )
 
 
+def butterfly(x, axis):
+    size = lax.axis_size(axis)
+    if size & (size - 1):
+        return lax.psum(x, axis)
+    m = 1
+    while m < size:
+        x = x + lax.ppermute(x, axis, [(i, i ^ m) for i in range(size)])
+        m *= 2
+    return x
+
+
+def route(llm_grad, dest_rank, ranks):
+    rows, width = llm_grad.shape
+    blocks_dev = dest_rank.shape[1]
+    block_rows = rows // blocks_dev
+    targets = dest_rank[0]
+    grad_blocks = llm_grad.reshape(blocks_dev, block_rows, width)
+    tags = jnp.broadcast_to(
+        (jnp.arange(blocks_dev, dtype=jnp.float32) + 1.0)[:, None, None], (blocks_dev, 1, width)
+    ).astype(jnp.bfloat16)
+    tagged = jnp.concatenate([grad_blocks, tags], axis=1)
+    send_sel = (targets[None, :] == jnp.arange(ranks, dtype=jnp.int32)[:, None]).astype(jnp.bfloat16)
+    outbox = jnp.einsum(
+        "dj,jrc->drc", send_sel, tagged, preferred_element_type=jnp.float32
+    ).astype(jnp.bfloat16)
+    inbox = lax.all_to_all(outbox, ("dp", "fsdp"), split_axis=0, concat_axis=0, tiled=True)
+    tag_in = inbox[:, block_rows, 0].astype(jnp.float32)
+    recv_sel = (
+        tag_in[None, :] == (jnp.arange(blocks_dev, dtype=jnp.float32) + 1.0)[:, None]
+    ).astype(jnp.bfloat16)
+    placed = jnp.einsum(
+        "js,src->jrc", recv_sel, inbox[:, :block_rows, :], preferred_element_type=jnp.float32
+    ).astype(jnp.bfloat16)
+    return placed.reshape(rows, width)
+
+
 def on_device(
     frames, llm_grad, dest_rank, utt_lengths, valid, norm_gain, up_weight, kernel, down_weight
 ):
@@ -35,36 +71,7 @@
     n_data = lax.axis_size("dp")
     n_shard = lax.axis_size("fsdp")
     ranks = n_data * n_shard
-    blocks_dev = dest_rank.shape[1]
-    block_rows = rows // blocks_dev
-    targets = dest_rank[0]
-    slots = jnp.arange(blocks_dev, dtype=jnp.int32) % CAPB
-    block_ids = jnp.arange(blocks_dev, dtype=jnp.int32)
-    grad_blocks = llm_grad.reshape(blocks_dev, block_rows, width)
-    outbox = (
-        jnp.zeros((ranks, CAPB, block_rows, width), jnp.bfloat16)
-        .at[targets, slots]
-        .set(grad_blocks)
-    )
-    labels = jnp.full((ranks, CAPB), -1, jnp.int32).at[targets, slots].set(block_ids)
-    got_rows, got_labels = (
-        lax.all_to_all(
-            outbox.reshape(ranks, CAPB * block_rows, width),
-            ("dp", "fsdp"),
-            split_axis=0,
-            concat_axis=0,
-            tiled=True,
-        ),
-        lax.all_to_all(labels, ("dp", "fsdp"), split_axis=0, concat_axis=0, tiled=True),
-    )
-    got_labels = got_labels.reshape(ranks * CAPB)
-    places = jnp.where(got_labels >= 0, got_labels, blocks_dev)
-    out_grad = (
-        jnp.zeros((blocks_dev + 1, block_rows, width), jnp.bfloat16)
-        .at[places]
-        .set(got_rows)[:blocks_dev]
-        .reshape(rows, width)
-    )
+    out_grad = route(llm_grad, dest_rank, ranks)
     up_full = lax.all_gather(up_weight, "fsdp", axis=0, tiled=True)
     down_full = lax.all_gather(down_weight, "fsdp", axis=0, tiled=True)
     taps = kernel.shape[0]
@@ -113,23 +120,23 @@
         - jnp.mean(scaled, axis=1, keepdims=True)
         - normed * jnp.mean(scaled * normed, axis=1, keepdims=True)
     )
-    left_hidden, left_act = (hidden, act)
     shard_sum = lax.psum_scatter(
         jnp.concatenate(
-            [contract_rows(left_hidden, up_out_grad), contract_rows(left_act, out_grad)], axis=1
+            [contract_rows(hidden, up_out_grad), contract_rows(act, out_grad)], axis=1
         ).astype(jnp.bfloat16),
         "fsdp",
         scatter_dimension=0,
         tiled=True,
     ).astype(jnp.float32)
-    shard_sum = lax.psum(shard_sum.astype(jnp.bfloat16), "dp").astype(jnp.float32)
-    kernel_grad, gain_grad = lax.psum((kernel_term, gain_term), ("dp", "fsdp"))
+    shard_sum = butterfly(shard_sum, "dp")
+    small = jnp.concatenate([kernel_term, gain_term[None, :]], axis=0)
+    small = butterfly(butterfly(small, "fsdp"), "dp")
     return (
         input_grad.astype(jnp.bfloat16),
         shard_sum[:, : 2 * width],
         shard_sum[:, 2 * width :],
-        kernel_grad,
-        gain_grad,
+        small[:taps],
+        small[taps],
     )
 
 

time: 391 us -> 346 us (0.88)
  blocking collectives: 66 us -> 0 us
  waiting for transfers between devices: 99 us -> 143 us
  local copies, waits for them, and re-layouts: 84.9 us -> 49.1 us
  matrix products: 54.1 us -> 59.6 us
  starting transfers between devices: 21.8 us -> 27.2 us
    psum x1 -> x0, blocking collectives: 66 us -> none  [on_device(): kernel_grad, gain_grad = lax.psum((kernel_term, gain_term), ('dp', 'fsdp'))]
    scatter x3 -> x0, local copies, waits for them, and re-layouts: 36.5 us -> none  [the longest x1 17.9 us: on_device(): out_grad = jnp.zeros((blocks_dev + 1, block_rows, width), jnp.bfloat16).a...]
    all_to_all x2 -> x1, waiting for transfers between devices: 27 us -> 52.9 us  [route(): lax.all_to_all(outbox, ('dp', 'fsdp'), split_axis=0, concat_axis=0, tiled...]
    ppermute x0 -> x9, waiting for transfers between devices: none -> 16 us  [butterfly(): x = x + lax.ppermute(x, axis, [(i, i ^ m) for i in range(size)])]
    ppermute x0 -> x9, starting transfers between devices: none -> 15.2 us  [butterfly(): x = x + lax.ppermute(x, axis, [(i, i ^ m) for i in range(size)])]
    all_to_all x2 -> x1, starting transfers between devices: 21.4 us -> 11.7 us  [route(): lax.all_to_all(outbox, ('dp', 'fsdp'), split_axis=0, concat_axis=0, tiled...]
    dot_general x0 -> x2, matrix products: none -> 4.84 us  [the longest x1 4.08 us: route(): jnp.einsum('js,src->jrc', recv_sel, inbox[:, :block_rows, :], preferred_e...]
    unnamed x40 -> x42, local copies, waits for them, and re-layouts: 13.4 us -> 11.2 us
  transfers between devices with their start and end apart: 6 -> 13, of which waited for: 2 -> 7; matrix products, arithmetic and copies ran while one was open for 27% -> 24% of each run, Pallas kernels for 0% -> 0%
where the time goes in v1:
time: 346 us; the launch traced here: 342 us
  waiting for transfers between devices  143 us (41%)
  matrix products  59.6 us (17%)
  other arithmetic  49.2 us (14%)
  local copies, waits for them, and re-layouts  49.1 us (14%)
  starting transfers between devices  27.2 us (8%)
  between operations  14.3 us (4%)
    reduce_scatter x1, waiting for transfers between devices, on_device(): lax.psum_scatter(jnp.concatenate([contract_rows(hidden, up_out_grad), con...  72.7 us
    all_to_all x1, waiting for transfers between devices, route(): lax.all_to_all(outbox, ('dp', 'fsdp'), split_axis=0, concat_axis=0, tiled...  52.9 us
    dot_general x1, matrix products, on_device(): jnp.dot(out_grad, down_full.T, preferred_element_type=jnp.float32)  28.4 us
    another operation x3, other arithmetic  22.3 us
    ppermute x9, waiting for transfers between devices, butterfly(): x = x + lax.ppermute(x, axis, [(i, i ^ m) for i in range(size)])  16 us
    ppermute x9, starting transfers between devices, butterfly(): x = x + lax.ppermute(x, axis, [(i, i ^ m) for i in range(size)])  15.2 us
    slice x8, local copies, waits for them, and re-layouts, shift_rows(): return jnp.concatenate([pad, values[:rows + offset]], axis=0)  14.9 us
    slice x4, local copies, waits for them, and re-layouts, shift_rows(): return jnp.concatenate([values[offset:], pad], axis=0)  12.8 us
  transfers between devices with their start and end apart: 13, of which 7 were waited for; matrix products, arithmetic and copies ran while one was open for 24% of the time, Pallas kernels for 0%

profile of v1, /device:TPU:0, one launch (start us, length us, event | category | flops | bytes accessed | tf_op | source)
XLA Modules:
  0.0 342.2 jit_solution(10935425352825855576)
XLA Ops:
  7.9 2.7 copy.30
  10.8 0.8 fusion.27
  11.5 3.5 %copy.31 = bf16[128,9,1024]{2,1,0:T(8,128)(2,1)} copy(bf16[128,9,1024]{2,0,1:T(8,128)(2,1)S(1)} %fusion.27) | data formatting | bytes 4718592 | tf_op jit(solution)/shard_map/convert_element_type | solution.py:55
  15.1 11.7 %all-to-all-start = ((bf16[128,9,1024]{2,1,0:T(8,128)(2,1)}), bf16[128,9,1024]{2,1,0:T(8,128)(2,1)}, u32[]{:S(2)}, u32[]{:S(2)}) async-start(bf16[128,9,1024]{2,1,0:T(8,128)(2,1)} %copy.31), calls=%async_computation | async-start | bytes 8388608 | tf_op jit(solution)/shard_map/all_to_all | solution.py:56
  28.1 2.9 copy.29
  32.4 52.9 %all-to-all-done = bf16[128,9,1024]{2,1,0:T(8,128)(2,1)} async-done(((bf16[128,9,1024]{2,1,0:T(8,128)(2,1)}), bf16[128,9,1024]{2,1,0:T(8,128)(2,1)}, u32[]{:S(2)}, u32[]{:S(2)}) %all-to-all-start) | async-done | bytes 2359328 | tf_op jit(solution)/shard_map/all_to_all | solution.py:56
  85.3 2.0 fusion.41
  87.3 1.8 slice.182
  89.0 4.1 %fusion.33 = bf16[128,8,1024]{2,0,1:T(8,128)(2,1)} fusion(bf16[128,8,1024]{2,1,0:T(8,128)(2,1)S(1)} %slice.182, f32[128]{0:T(128)S(1)} %fusion.41, f32[128]{0:T(128)S(1)} %iota_add_fusion), kind=kOutput, calls=%fused_computation.61 | convolution fusion | flops 269500416 | bytes 4195328 | tf_op jit(solution)/shard_map/js,src->jrc/dot_general | solution.py:61
  93.1 6.7 %fusion.39 = f32[1024,2048]{1,0:T(8,128)S(1)} fusion(bf16[1024,2048]{1,0:T(8,128)(2,1)} %all-gather.5.cloned.1.call-done, bf16[1024,1024]{0,1:T(8,128)(2,1)S(1)} %copy.29, f32[1024]{0:T(1024)S(1)} %copy-done.16, f32[1024]{0:T(1024)S(1)} %add_rsqrt_fusion, f32[1024]{0:T(1024)S(1)} %broadcast_multiply_fusion.10), kind=kOutput, calls=%fused_computation.64 | convolution fusion | flops 4300210176 | bytes 14692352 | tf_op jit(solution)/shard_map/dot_general | solution.py:86
  99.9 1.5 fusion.21
  101.4 1.2 fusion.65
  102.7 4.7 %fusion.64 = (f32[1022,1024]{1,0:T(8,128)}, f32[1022,1024]{1,0:T(8,128)}) fusion(f32[1024,1024]{1,0:T(8,128)S(1)} %fusion.21), kind=kLoop, calls=%fused_computation.105 | loop fusion | bytes 16744448 | tf_op jit(solution)/shard_map/slice | solution.py:16
  107.4 4.6 %fusion.63 = (f32[1021,1024]{1,0:T(8,128)}, f32[1021,1024]{1,0:T(8,128)}) fusion(f32[1024,1024]{1,0:T(8,128)S(1)} %fusion.21), kind=kLoop, calls=%fused_computation.104 | loop fusion | bytes 16728064 | tf_op jit(solution)/shard_map/slice | solution.py:16
  112.0 4.1 %fusion.62 = (f32[1020,1024]{1,0:T(8,128)}, f32[1020,1024]{1,0:T(8,128)}) fusion(f32[1024,1024]{1,0:T(8,128)S(1)} %fusion.21), kind=kLoop, calls=%fused_computation.103 | loop fusion | bytes 16711680 | tf_op jit(solution)/shard_map/slice | solution.py:16
  116.1 12.3 %add_multiply_fusion = f32[1024,1024]{1,0:T(8,128)S(1)} fusion(f32[1020,1024]{1,0:T(8,128)} %get-tuple-element.63, f32[1021,1024]{1,0:T(8,128)} %get-tuple-element.65, f32[1022,1024]{1,0:T(8,128)} %get-tuple-element.67, f32[1023,1024]{1,0:T(8,128)S(1)} %get-tuple-element.69, f32[1023,1024]{1,0:T(8,128)S(1)} %get-tuple-element.68, ...), kind=kLoop, calls=%fused_computation.36 | loop fusion | flops 33554432 | bytes 46129152 | tf_op jit(solution)/shard_map/mul | solution.py:99
  128.4 1.9 copy-done.6
  130.3 4.4 %fusion.30 = bf16[1024,1024]{1,0:T(8,128)(2,1)} fusion(f32[1024,1024]{1,0:T(8,128)S(1)} %add_multiply_fusion, bf16[128,8,1024]{2,0,1:T(8,128)(2,1)S(1)} %copy-done.9), kind=kOutput, calls=%fused_computation.60 | convolution fusion | flops 2153775104 | bytes 8388608 | tf_op jit(solution)/shard_map/dot_general | solution.py:26
  134.6 28.4 %multiply_reduce_fusion.8 = (f32[1024]{0:T(1024)S(1)}, f32[1024,1024]{1,0:T(8,128)}, f32[1024]{0:T(1024)S(1)}, f32[1024]{0:T(1024)S(1)}, f32[1024,1024]{1,0:T(8,...) fusion(f32[1020,1024]{1,0:T(8,128)} %get-tuple-element.62, ...), kind=kOutput, calls=%fused_computation.29 | convolution fusion | flops 2184174592 | bytes 83877888 | tf_op jit(solution)/shard_map/dot_general | solution.py:102
  163.0 5.3 %slice.193 = f32[1020,1024]{1,0:T(8,128)} slice(f32[1024,1024]{1,0:T(8,128)} %get-tuple-element.43), slice={[4:1024], [0:1024]} | slice | bytes 8355840 | tf_op jit(solution)/shard_map/slice | solution.py:15
  168.3 2.6 slice.196
  171.0 1.1 copy-done.7
  172.0 2.4 slice.195
  174.4 2.4 slice.194
  176.9 17.6 %multiply_convert_fusion.2 = (bf16[1024,1024]{1,0:T(8,128)(2,1)}, f32[1024,1024]{1,0:T(8,128)S(1)}) fusion(f32[1024,2048]{1,0:T(8,128)} %copy-done.1, f32[1020,1024]{1,0:T(8,128)} %bitcast.47, f32[1024]{0:T(1024)S(1)} %bitcast.68, f32[1021,1024]{1,0:T(8,128)} %bitcast.48, f32[1024]{0:T(1024)S(1)} %bitcast.70, f32[1022,1024]{1,0:T(8,128)} %bitcast.49, ...), kind=kLoop, calls=%fused_computation.32 | loop fusion | flops 23068672 | bytes 48189440 | tf_op jit(solution)/shard_map/convert.3
  194.5 4.4 %multiply_convert_fusion.1 = bf16[1024,1024]{1,0:T(8,128)(2,1)S(1)} fusion(f32[1024,1024]{1,0:T(8,128)S(1)} %get-tuple-element.45, f32[1024,2048]{1,0:T(8,128)} %copy-done.1), kind=kLoop, calls=%fused_computation.31 | loop fusion | flops 8388608 | bytes 14680064 | tf_op jit(solution)/shard_map/convert.4
  199.0 1.3 copy-done.12
  200.3 4.9 %convolution_convert_fusion = bf16[1024,2048]{1,0:T(8,128)(2,1)S(1)} fusion(bf16[1024,1024]{1,0:T(8,128)(2,1)S(1)} %multiply_convert_fusion.1, bf16[1024,1024]{1,0:T(8,128)(2,1)S(1)} %copy-done.11, bf16[1024,1024]{0,1:T(8,128)(2,1)S(1)} %copy-done.5, f32[1024]{0:T(1024)S(1)} %copy-done.16, f32[1024]{0:T(1024)S(1)} %add_rsqrt_fusion, ...), kind=kOutput, calls=%fused_computation.38 | convolution fusion | flops 4310695936 | bytes 10498048 | tf_op jit(solution)/shard_map/dot_general | solution.py:26
  205.3 3.2 pad_maximum_fusion
  208.5 10.3 %fusion.11 = (f32[1024]{0:T(1024)S(1)}, f32[1024]{0:T(1024)S(1)}, f32[1024]{0:T(1024)S(1)}, f32[1024,1024]{0,1:T(8,128)}) fusion(bf16[1024,1024]{0,1:T(8,128)(2,1)S(1)} %copy-done.5, f32[1024]{0:T(1024)S(1)} %add_rsqrt_fusion, f32[1024]{0:T(1024)S(1)} %broadcast_multiply_fusion.10, f32[1024]{0:T(1024)S(1)} %copy-done.16, ...), kind=kOutput, calls=%fused_computation.14 | convolution fusion | flops 4312790016 | bytes 14704640 | tf_op jit(solution)/shard_map/dot_general | solution.py:115
  219.0 72.7 %reduce-scatter.2.cloned.1.call-done = bf16[32,3072]{1,0:T(8,128)(2,1)} async-done(((bf16[1024,3072]{1,0:T(8,128)(2,1)}), bf16[32,3072]{1,0:T(8,128)(2,1)}) %reduce-scatter.2.cloned.1.call-update) | async-done | bytes 196624 | tf_op jit(solution)/shard_map/reduce_scatter | solution.py:123
  291.7 1.0 convert_element_type.109
  292.6 1.6 collective-permute-start
  294.3 1.3 collective-permute-start.3
  295.6 3.2 collective-permute-done.3
  298.8 3.0 collective-permute-start.4
  301.8 2.8 collective-permute-done.4
  304.6 1.7 collective-permute-start.5
  306.3 2.8 collective-permute-done.5
  309.2 3.2 collective-permute-start.6
  312.4 2.6 collective-permute-done.6
  315.6 4.5 %collective-permute-done.7 = f32[10,1024]{1,0:T(8,128)S(1)} collective-permute-done((f32[10,1024]{1,0:T(8,128)S(1)}, f32[10,1024]{1,0:T(8,128)S(1)}, u32[]{:S(2)}, u32[]{:S(2)}) %collective-permute-start.7) | collective-permute-done | bytes 40992 | tf_op jit(solution)/shard_map/ppermute | solution.py:37
  320.1 2.9 collective-permute-start.8
  322.9 1.0 convert_add_fusion
  323.9 0.8 collective-permute-start.1
  324.7 4.7 %fusion.10 = bf16[1024,1024]{0,1:T(8,128)(2,1)} fusion(bf16[1024,1024]{0,1:T(8,128)(2,1)S(1)} %copy-done.5, f32[1024,1024]{0,1:T(8,128)} %get-tuple-element.96, f32[1024]{0:T(1024)S(1)} %get-tuple-element.97, f32[1024]{0:T(1024)S(1)} %get-tuple-element.98, f32[1024]{0:T(1024)S(1)} %copy-done.16, f32[1024]{0:T(1024)S(1)} %add_rsqrt_fusion, ...), kind=kLoop, calls=%fused_computation.13 | loop fusion | flops 9437184 | bytes 8409088 | tf_op jit(solution)/shard_map/convert_element_type | solution.py:135
  329.5 3.9 %copy.35 = bf16[1024,1024]{1,0:T(8,128)(2,1)} copy(bf16[1024,1024]{0,1:T(8,128)(2,1)} %fusion.10) | data formatting | bytes 4194304
  334.7 0.7 slice.201
  (79 shorter events, 5.6 us)
Async XLA Ops:
  7.2 3.6 %copy-start.18 = (s32[1,128]{1,0:T(1,128)S(1)}, s32[1,128]{1,0:T(1,128)}, u32[]{:S(2)}) copy-start(s32[1,128]{1,0:T(1,128)} %param.11) | copy-start | bytes 1540
  7.2 85.9 %all-gather.5.cloned.1.call-start = ((), (), s32[]{:S(2)}) async-start(), calls=%async_computation.3 | async-start | bytes 4325376 | tf_op jit(solution)/shard_map/all_gather | solution.py:75
  15.1 12.7 %copy-start.19 = (s32[1,4]{1,0:T(1,128)S(1)}, s32[1,4]{1,0:T(1,128)}, u32[]{:S(2)}) copy-start(s32[1,4]{1,0:T(1,128)} %param.12) | copy-start | bytes 52
  15.1 13.0 %copy-start.17 = (s32[1024]{0:T(1024)S(1)}, s32[1024]{0:T(1024)}, u32[]{:S(2)}) copy-start(s32[1024]{0:T(1024)} %param.13) | copy-start | bytes 12292
  15.1 70.2 %all-to-all-start = ((bf16[128,9,1024]{2,1,0:T(8,128)(2,1)}), bf16[128,9,1024]{2,1,0:T(8,128)(2,1)}, u32[]{:S(2)}, u32[]{:S(2)}) async-start(bf16[128,9,1024]{2,1,0:T(8,128)(2,1)} %copy.31), calls=%async_computation | async-start | bytes 8388608 | tf_op jit(solution)/shard_map/all_to_all | solution.py:56
  26.8 107.9 %all-gather.3.cloned.1.call-start = ((), (), s32[]{:S(2)}) async-start(), calls=%async_computation.2 | async-start | bytes 2162688 | tf_op jit(solution)/shard_map/all_gather | solution.py:76
  27.5 264.1 %reduce-scatter.2.cloned.1.call-start = ((), (), s32[]{:S(2)}) async-start(), calls=%async_computation.4 | async-start | bytes 6488064 | tf_op jit(solution)/shard_map/reduce_scatter | solution.py:123
  28.0 4.3 %copy-start.15 = (f32[9,1024]{1,0:T(8,128)S(1)}, f32[9,1024]{1,0:T(8,128)}, u32[]{:S(2)}) copy-start(f32[9,1024]{1,0:T(8,128)} %param.16) | copy-start | bytes 110596
  31.0 62.2 %copy-start.4 = (bf16[1024,1024]{0,1:T(8,128)(2,1)}, bf16[1024,1024]{0,1:T(8,128)(2,1)S(1)}, u32[]{:S(2)}) copy-start(bf16[1024,1024]{0,1:T(8,128)(2,1)S(1)} %copy.29) | copy-start | bytes 6291460
  87.3 5.9 %copy-start.16 = (f32[1024]{0:T(1024)S(1)}, f32[1024]{0:T(1024)}, u32[]{:S(2)}) copy-start(f32[1024]{0:T(1024)} %param.14) | copy-start | bytes 12292
  99.9 16.2 %copy-start.1 = (f32[1024,2048]{1,0:T(8,128)}, f32[1024,2048]{1,0:T(8,128)S(1)}, u32[]{:S(2)}) copy-start(f32[1024,2048]{1,0:T(8,128)S(1)} %fusion.39) | copy-start | bytes 25165828
  101.4 10.6 %copy-start = (f32[1024,1024]{1,0:T(8,128)}, f32[1024,1024]{1,0:T(8,128)S(1)}, u32[]{:S(2)}) copy-start(f32[1024,1024]{1,0:T(8,128)S(1)} %fusion.21) | copy-start | bytes 12582916
  102.7 13.4 %copy-start.2 = (f32[1023,1024]{1,0:T(8,128)}, f32[1023,1024]{1,0:T(8,128)S(1)}, u32[]{:S(2)}) copy-start(f32[1023,1024]{1,0:T(8,128)S(1)} %get-tuple-element.68) | copy-start | bytes 12570628
  102.7 13.4 %copy-start.3 = (f32[1023,1024]{1,0:T(8,128)}, f32[1023,1024]{1,0:T(8,128)S(1)}, u32[]{:S(2)}) copy-start(f32[1023,1024]{1,0:T(8,128)S(1)} %get-tuple-element.69) | copy-start | bytes 12570628
  116.1 14.2 %copy-start.9 = (bf16[128,8,1024]{2,0,1:T(8,128)(2,1)S(1)}, bf16[128,8,1024]{2,0,1:T(8,128)(2,1)}, u32[]{:S(2)}) copy-start(bf16[128,8,1024]{2,0,1:T(8,128)(2,1)} %fusion.33) | copy-start | bytes 6291460
  128.3 1.9 copy-start.6
  130.3 4.4 %copy-start.10 = (bf16[128,8,1024]{2,0,1:T(8,128)(2,1)S(1)}, bf16[128,8,1024]{2,0,1:T(8,128)(2,1)}, u32[]{:S(2)}) copy-start(bf16[128,8,1024]{2,0,1:T(8,128)(2,1)} %fusion.33) | copy-start | bytes 6291460
  163.0 5.3 %copy-start.8 = (f32[1024,1024]{1,0:T(8,128)S(1)}, f32[1024,1024]{1,0:T(8,128)}, u32[]{:S(2)}) copy-start(f32[1024,1024]{1,0:T(8,128)} %get-tuple-element.57) | copy-start | bytes 12582916
  168.3 3.7 %copy-start.7 = (f32[1024,1024]{1,0:T(8,128)S(1)}, f32[1024,1024]{1,0:T(8,128)}, u32[]{:S(2)}) copy-start(f32[1024,1024]{1,0:T(8,128)} %get-tuple-element.59) | copy-start | bytes 12582916
  194.5 5.8 %copy-start.5 = (bf16[1024,1024]{0,1:T(8,128)(2,1)S(1)}, bf16[1024,1024]{0,1:T(8,128)(2,1)}, u32[]{:S(2)}) copy-start(bf16[1024,1024]{0,1:T(8,128)(2,1)} %copy-done.4) | copy-start | bytes 6291460
  194.5 5.8 %copy-start.11 = (bf16[1024,1024]{1,0:T(8,128)(2,1)S(1)}, bf16[1024,1024]{1,0:T(8,128)(2,1)}, u32[]{:S(2)}) copy-start(bf16[1024,1024]{1,0:T(8,128)(2,1)} %get-tuple-element.44) | copy-start | bytes 6291460
  199.0 1.3 copy-start.12
  200.3 4.9 %copy-start.13 = (bf16[1024,1024]{1,0:T(8,128)(2,1)S(1)}, bf16[1024,1024]{1,0:T(8,128)(2,1)}, u32[]{:S(2)}) copy-start(bf16[1024,1024]{1,0:T(8,128)(2,1)} %fusion.30) | copy-start | bytes 6291460
  218.9 75.3 %collective-permute-start.2 = (f32[10,1024]{1,0:T(8,128)S(1)}, f32[10,1024]{1,0:T(8,128)S(1)}, u32[]{:S(2)}, u32[]{:S(2)}) collective-permute-start(f32[10,1024]{1,0:T(8,128)S(1)} %concatenate.129), channel_id=1, source_target_pairs={{0,1},{1,0},{2,3},{3,2},{4,5},{5,4},{6,7},{7,6},{8,9},{9,8},{10,11... | collective-permute-start | bytes 122888 | tf_op jit(solution)/shard_map/ppermute | solution.py:37
  292.6 30.3 %collective-permute-start = (f32[32,3072]{1,0:T(8,128)S(1)}, f32[32,3072]{1,0:T(8,128)S(1)}, u32[]{:S(2)}, u32[]{:S(2)}) collective-permute-start(f32[32,3072]{1,0:T(8,128)S(1)} %convert_element_type.109), channel_id=1, source_target_pairs={{0,32},{32,0},{64,96},{96,64},{1,33},{33,1},{65,97},{97,65},{2,34}... | collective-permute-start | bytes 1179656 | tf_op jit(solution)/shard_map/ppermute | solution.py:37
  294.3 4.5 %collective-permute-start.3 = (f32[10,1024]{1,0:T(8,128)S(1)}, f32[10,1024]{1,0:T(8,128)S(1)}, u32[]{:S(2)}, u32[]{:S(2)}) collective-permute-start(f32[10,1024]{1,0:T(8,128)S(1)} %add.181), channel_id=1, source_target_pairs={{0,2},{1,3},{2,0},{3,1},{4,6},{5,7},{6,4},{7,5},{8,10},{9,11},{10,... | collective-permute-start | bytes 122888 | tf_op jit(solution)/shard_map/ppermute | solution.py:37
  298.8 5.8 %collective-permute-start.4 = (f32[10,1024]{1,0:T(8,128)S(1)}, f32[10,1024]{1,0:T(8,128)S(1)}, u32[]{:S(2)}, u32[]{:S(2)}) collective-permute-start(f32[10,1024]{1,0:T(8,128)S(1)} %add.182), channel_id=1, source_target_pairs={{0,4},{1,5},{2,6},{3,7},{4,0},{5,1},{6,2},{7,3},{8,12},{9,13},{10,... | collective-permute-start | bytes 122888 | tf_op jit(solution)/shard_map/ppermute | solution.py:37
  304.6 4.5 %collective-permute-start.5 = (f32[10,1024]{1,0:T(8,128)S(1)}, f32[10,1024]{1,0:T(8,128)S(1)}, u32[]{:S(2)}, u32[]{:S(2)}) collective-permute-start(f32[10,1024]{1,0:T(8,128)S(1)} %add.183), channel_id=1, source_target_pairs={{0,8},{1,9},{2,10},{3,11},{4,12},{5,13},{6,14},{7,15},{8,0},{9,1},... | collective-permute-start | bytes 122888 | tf_op jit(solution)/shard_map/ppermute | solution.py:37
  309.2 5.8 %collective-permute-start.6 = (f32[10,1024]{1,0:T(8,128)S(1)}, f32[10,1024]{1,0:T(8,128)S(1)}, u32[]{:S(2)}, u32[]{:S(2)}) collective-permute-start(f32[10,1024]{1,0:T(8,128)S(1)} %add.184), channel_id=1, source_target_pairs={{0,16},{1,17},{2,18},{3,19},{4,20},{5,21},{6,22},{7,23},{8,24},{9,... | collective-permute-start | bytes 122888 | tf_op jit(solution)/shard_map/ppermute | solution.py:37
  315.0 5.0 %collective-permute-start.7 = (f32[10,1024]{1,0:T(8,128)S(1)}, f32[10,1024]{1,0:T(8,128)S(1)}, u32[]{:S(2)}, u32[]{:S(2)}) collective-permute-start(f32[10,1024]{1,0:T(8,128)S(1)} %add.185), channel_id=1, source_target_pairs={{0,32},{32,0},{64,96},{96,64},{1,33},{33,1},{65,97},{97,65},{2,34}... | collective-permute-start | bytes 122888 | tf_op jit(solution)/shard_map/ppermute | solution.py:37
  320.1 13.3 %collective-permute-start.8 = (f32[10,1024]{1,0:T(8,128)S(1)}, f32[10,1024]{1,0:T(8,128)S(1)}, u32[]{:S(2)}, u32[]{:S(2)}) collective-permute-start(f32[10,1024]{1,0:T(8,128)S(1)} %add.186), channel_id=1, source_target_pairs={{0,64},{32,96},{64,0},{96,32},{1,65},{33,97},{65,1},{97,33},{2,66}... | collective-permute-start | bytes 122888 | tf_op jit(solution)/shard_map/ppermute | solution.py:37
  323.9 10.1 %collective-permute-start.1 = (f32[32,3072]{1,0:T(8,128)S(1)}, f32[32,3072]{1,0:T(8,128)S(1)}, u32[]{:S(2)}, u32[]{:S(2)}) collective-permute-start(f32[32,3072]{1,0:T(8,128)S(1)} %convert_add_fusion), channel_id=1, source_target_pairs={{0,64},{32,96},{64,0},{96,32},{1,65},{33,97},{65,1},{97,33},{2,66}... | collective-permute-start | bytes 1179656 | tf_op jit(solution)/shard_map/ppermute | solution.py:37
  333.4 2.1 copy-start.14
Sparse Core Ops, SparseCore 0:
  10.2 77.3 all-gather.4
  89.9 42.1 all-gather.2
  208.6 82.9 reduce-scatter.1

commit v2 on v1

--- a/solution.py
+++ b/solution.py
@@ -28,14 +28,26 @@
     )
 
 
-def butterfly(x, axis):
+def group_sum(x, axis):
     size = lax.axis_size(axis)
     if size & (size - 1):
         return lax.psum(x, axis)
-    m = 1
-    while m < size:
-        x = x + lax.ppermute(x, axis, [(i, i ^ m) for i in range(size)])
-        m *= 2
+    bits = size.bit_length() - 1
+    shift = 0
+    me = lax.axis_index(axis)
+    while shift < bits:
+        width = 1 if (shift == 0 and bits % 2) else 2
+        n = 1 << width
+        got = [x] + [
+            lax.ppermute(x, axis, [(i, i ^ (d << shift)) for i in range(size)]) for d in range(1, n)
+        ]
+        stack = jnp.stack(got)
+        mine = (me >> shift) & (n - 1)
+        total = stack[mine]
+        for m in range(1, n):
+            total = total + stack[m ^ mine]
+        x = total
+        shift += width
     return x
 
 
@@ -71,8 +83,9 @@
     n_data = lax.axis_size("dp")
     n_shard = lax.axis_size("fsdp")
     ranks = n_data * n_shard
+    up_full = lax.all_gather(up_weight, "fsdp", axis=0, tiled=True)
+    llm_grad, up_full = lax.optimization_barrier((llm_grad, up_full))
     out_grad = route(llm_grad, dest_rank, ranks)
-    up_full = lax.all_gather(up_weight, "fsdp", axis=0, tiled=True)
     down_full = lax.all_gather(down_weight, "fsdp", axis=0, tiled=True)
     taps = kernel.shape[0]
     middle = (taps - 1) // 2
@@ -112,27 +125,28 @@
     value_grad = glu_grad * sig_b
     gate_grad = glu_grad * value * sig_b * (1.0 - sig_b)
     up_out_grad = jnp.concatenate([value_grad, gate_grad], axis=1).astype(jnp.bfloat16)
+    down_sum = lax.psum_scatter(
+        contract_rows(act, out_grad).astype(jnp.bfloat16), "fsdp", scatter_dimension=0, tiled=True
+    )
+    up_out_grad, down_sum = lax.optimization_barrier((up_out_grad, down_sum))
     hidden_grad = jnp.dot(up_out_grad, up_full.T, preferred_element_type=jnp.float32)
     gain_term = jnp.sum(hidden_grad * normed, axis=0)
+    small = group_sum(jnp.concatenate([kernel_term, gain_term[None, :]], axis=0), "fsdp")
+    small = group_sum(small, "dp")
     scaled = hidden_grad * norm_gain[None, :]
     input_grad = rstd * (
         scaled
         - jnp.mean(scaled, axis=1, keepdims=True)
         - normed * jnp.mean(scaled * normed, axis=1, keepdims=True)
     )
-    shard_sum = lax.psum_scatter(
-        jnp.concatenate(
-            [contract_rows(hidden, up_out_grad), contract_rows(act, out_grad)], axis=1
-        ).astype(jnp.bfloat16),
-        "fsdp",
-        scatter_dimension=0,
-        tiled=True,
-    ).astype(jnp.float32)
-    shard_sum = butterfly(shard_sum, "dp")
-    small = jnp.concatenate([kernel_term, gain_term[None, :]], axis=0)
-    small = butterfly(butterfly(small, "fsdp"), "dp")
+    input_grad = input_grad.astype(jnp.bfloat16)
+    up_term = contract_rows(hidden, up_out_grad).astype(jnp.bfloat16)
+    up_term, small, input_grad = lax.optimization_barrier((up_term, small, input_grad))
+    up_sum = lax.psum_scatter(up_term, "fsdp", scatter_dimension=0, tiled=True)
+    shard_sum = jnp.concatenate([up_sum, down_sum], axis=1).astype(jnp.float32)
+    shard_sum = group_sum(shard_sum, "dp")
     return (
-        input_grad.astype(jnp.bfloat16),
+        input_grad,
         shard_sum[:, : 2 * width],
         shard_sum[:, 2 * width :],
         small[:taps],

time: 346 us -> 400 us (1.16); the launches traced: 342 us -> 392 us
  waiting for transfers between devices: 143 us -> 182 us
  local copies, waits for them, and re-layouts: 49.1 us -> 56.7 us
    all_gather x1, waiting for transfers between devices: 0.01 us -> 44.6 us  [on_device(): up_full = lax.all_gather(up_weight, 'fsdp', axis=0, tiled=True)]
    all_to_all x1, waiting for transfers between devices: 52.9 us -> 25.1 us  [route(): lax.all_to_all(outbox, ('dp', 'fsdp'), split_axis=0, concat_axis=0, tiled...]
    reduce_scatter x1 -> x2, waiting for transfers between devices: 72.7 us -> 84.6 us  [the longest x1 78.2 us: on_device(): up_sum = lax.psum_scatter(up_term, 'fsdp', scatter_dimension=0, tiled=True)]
    ppermute x9 -> x13, waiting for transfers between devices: 16 us -> 26 us  [group_sum(): lax.ppermute(x, axis, [(i, i ^ d << shift) for i in range(size)])]
    slice x8, local copies, waits for them, and re-layouts: 14.9 us -> 22.8 us  [shift_rows(): return jnp.concatenate([pad, values[:rows + offset]], axis=0)]
    ppermute x9 -> x13, starting transfers between devices: 15.2 us -> 19.1 us  [group_sum(): lax.ppermute(x, axis, [(i, i ^ d << shift) for i in range(size)])]
    unnamed x42 -> x48, local copies, waits for them, and re-layouts: 11.2 us -> 12.4 us
    another operation x3 -> x7, other arithmetic: 22.3 us -> 23.3 us
  transfers between devices with their start and end apart: 13 -> 18, of which waited for: 7 -> 13; matrix products, arithmetic and copies ran while one was open for 24% -> 36% of each run, Pallas kernels for 0% -> 0%
where the time goes in v2:
time: 400 us; the launch traced here: 392 us
  waiting for transfers between devices  182 us (46%)
  matrix products  60.1 us (15%)
  local copies, waits for them, and re-layouts  56.7 us (14%)
  other arithmetic  50 us (12%)
  starting transfers between devices  28.4 us (7%)
  between operations  14.7 us (4%)
    reduce_scatter x1, waiting for transfers between devices, on_device(): up_sum = lax.psum_scatter(up_term, 'fsdp', scatter_dimension=0, tiled=True)  78.2 us
    all_gather x1, waiting for transfers between devices, on_device(): up_full = lax.all_gather(up_weight, 'fsdp', axis=0, tiled=True)  44.6 us
    dot_general x1, matrix products, on_device(): jnp.dot(out_grad, down_full.T, preferred_element_type=jnp.float32)  28.7 us
    ppermute x13, waiting for transfers between devices, group_sum(): lax.ppermute(x, axis, [(i, i ^ d << shift) for i in range(size)])  26 us
    all_to_all x1, waiting for transfers between devices, route(): lax.all_to_all(outbox, ('dp', 'fsdp'), split_axis=0, concat_axis=0, tiled...  25.1 us
    another operation x3, other arithmetic  23.1 us
    slice x8, local copies, waits for them, and re-layouts, shift_rows(): return jnp.concatenate([pad, values[:rows + offset]], axis=0)  22.8 us
    ppermute x13, starting transfers between devices, group_sum(): lax.ppermute(x, axis, [(i, i ^ d << shift) for i in range(size)])  19.1 us
  transfers between devices with their start and end apart: 18, of which 13 were waited for; matrix products, arithmetic and copies ran while one was open for 36% of the time, Pallas kernels for 0%

profile of v2, /device:TPU:0, one launch (start us, length us, event | category | flops | bytes accessed | tf_op | source)
XLA Modules:
  0.0 391.6 jit_solution(9065369719693428825)
XLA Ops:
  10.0 2.9 copy.26
  14.1 44.6 %all-gather.3.cloned.1.call-done = bf16[1024,2048]{1,0:T(8,128)(2,1)} async-done(((bf16[32,2048]{1,0:T(8,128)(2,1)}), bf16[1024,2048]{1,0:T(8,128)(2,1)}) %all-gather.3.cloned.1.call-update) | async-done | bytes 4194320 | tf_op jit(solution)/shard_map/all_gather | solution.py:86
  58.7 6.7 %fusion.38 = f32[1024,2048]{1,0:T(8,128)S(1)} fusion(bf16[1024,2048]{1,0:T(8,128)(2,1)} %all-gather.3.cloned.1.call-done, bf16[1024,1024]{0,1:T(8,128)(2,1)S(1)} %copy.26, f32[1024]{0:T(1024)S(1)} %copy-done.18, f32[1024]{0:T(1024)S(1)} %add_rsqrt_fusion, f32[1024]{0:T(1024)S(1)} %broadcast_multiply_fusion.10), kind=kOutput, calls=%fused_computation.64 | convolution fusion | flops 4300210176 | bytes 14692352 | tf_op jit(solution)/shard_map/dot_general | solution.py:99
  65.4 3.2 copy-done.2
  69.7 4.4 %fusion.62 = (f32[1020,1024]{1,0:T(8,128)}, f32[1020,1024]{1,0:T(8,128)}) fusion(f32[1024,1024]{1,0:T(8,128)S(1)} %fusion.20), kind=kLoop, calls=%fused_computation.115 | loop fusion | bytes 16711680 | tf_op jit(solution)/shard_map/slice | solution.py:16
  74.2 4.1 %fusion.63 = (f32[1021,1024]{1,0:T(8,128)}, f32[1021,1024]{1,0:T(8,128)}) fusion(f32[1024,1024]{1,0:T(8,128)S(1)} %fusion.20), kind=kLoop, calls=%fused_computation.116 | loop fusion | bytes 16728064 | tf_op jit(solution)/shard_map/slice | solution.py:16
  80.3 3.5 copy.28
  83.8 8.7 %all-to-all-start = ((bf16[128,9,1024]{2,1,0:T(8,128)(2,1)}), bf16[128,9,1024]{2,1,0:T(8,128)(2,1)}, u32[]{:S(2)}, u32[]{:S(2)}) async-start(bf16[128,9,1024]{2,1,0:T(8,128)(2,1)} %copy.28), calls=%async_computation | async-start | bytes 8388608 | tf_op jit(solution)/shard_map/all_to_all | solution.py:68
  92.8 9.0 %fusion.64 = (f32[1022,1024]{1,0:T(8,128)}, f32[1022,1024]{1,0:T(8,128)}) fusion(f32[1024,1024]{1,0:T(8,128)} %copy-done), kind=kLoop, calls=%fused_computation.117 | loop fusion | bytes 16744448 | tf_op jit(solution)/shard_map/slice | solution.py:16
  101.8 5.0 %fusion.65 = (f32[1023,1024]{1,0:T(8,128)}, f32[1023,1024]{1,0:T(8,128)}) fusion(f32[1024,1024]{1,0:T(8,128)S(1)} %copy-done.1), kind=kLoop, calls=%fused_computation.118 | loop fusion | bytes 16760832 | tf_op jit(solution)/shard_map/slice | solution.py:16
  106.8 1.4 copy-done.3
  109.4 13.4 %add_multiply_fusion = f32[1024,1024]{1,0:T(8,128)} fusion(f32[1020,1024]{1,0:T(8,128)S(1)} %copy-done.4, f32[1021,1024]{1,0:T(8,128)} %get-tuple-element.79, f32[1022,1024]{1,0:T(8,128)} %get-tuple-element.81, f32[1023,1024]{1,0:T(8,128)} %get-tuple-element.83, f32[1023,1024]{1,0:T(8,128)} %get-tuple-element.82, f32[1022,1024]{1,0:T(8,128)} %get-tuple-element.80, ...), kind=kLoop, calls=%fused_computation.35 | loop fusion | flops 33554432 | bytes 46129152 | tf_op jit(solution)/shard_map/mul | solution.py:112
  122.7 25.1 %all-to-all-done = bf16[128,9,1024]{2,1,0:T(8,128)(2,1)} async-done(((bf16[128,9,1024]{2,1,0:T(8,128)(2,1)}), bf16[128,9,1024]{2,1,0:T(8,128)(2,1)}, u32[]{:S(2)}, u32[]{:S(2)}) %all-to-all-start) | async-done | bytes 2359328 | tf_op jit(solution)/shard_map/all_to_all | solution.py:68
  147.8 1.9 slice.182
  149.7 2.0 fusion.43
  151.7 2.7 fusion.32
  154.5 4.2 %fusion.29 = bf16[1024,1024]{1,0:T(8,128)(2,1)} fusion(f32[1024,1024]{1,0:T(8,128)S(1)} %copy-done.7, bf16[128,8,1024]{2,0,1:T(8,128)(2,1)S(1)} %fusion.32), kind=kOutput, calls=%fused_computation.58 | convolution fusion | flops 2153775104 | bytes 8388608 | tf_op jit(solution)/shard_map/dot_general | solution.py:26
  159.0 28.7 %multiply_reduce_fusion.8 = (f32[1024]{0:T(1024)S(1)}, f32[1024,1024]{1,0:T(8,128)}, f32[1024]{0:T(1024)S(1)}, f32[1024]{0:T(1024)S(1)}, f32[1024,1024]{1,0:T(8,...) fusion(f32[1020,1024]{1,0:T(8,128)} %get-tuple-element.76, ...), kind=kOutput, calls=%fused_computation.28 | convolution fusion | flops 2184174592 | bytes 83877888 | tf_op jit(solution)/shard_map/dot_general | solution.py:115
  187.8 5.2 %slice.193 = f32[1020,1024]{1,0:T(8,128)} slice(f32[1024,1024]{1,0:T(8,128)} %get-tuple-element.57), slice={[4:1024], [0:1024]} | slice | bytes 8355840 | tf_op jit(solution)/shard_map/slice | solution.py:15
  193.0 2.6 slice.194
  196.7 2.5 slice.195
  199.1 2.5 slice.196
  201.6 17.6 %multiply_convert_fusion.2 = (bf16[1024,1024]{1,0:T(8,128)(2,1)}, f32[1024,1024]{1,0:T(8,128)S(1)}) fusion(f32[1024,2048]{1,0:T(8,128)} %copy-done.2, f32[1020,1024]{1,0:T(8,128)} %bitcast.76, f32[1024]{0:T(1024)S(1)} %bitcast.116, f32[1021,1024]{1,0:T(8,128)} %bitcast.77, f32[1024]{0:T(1024)S(1)} %bitcast.118, f32[1022,1024]{1,0:T(8,128)} %bitcast.78, ...), kind=kLoop, calls=%fused_computation.31 | loop fusion | flops 23068672 | bytes 48189440 | tf_op jit(solution)/shard_map/convert.1
  219.2 4.7 %multiply_convert_fusion.1 = bf16[1024,1024]{1,0:T(8,128)(2,1)S(1)} fusion(f32[1024,1024]{1,0:T(8,128)S(1)} %get-tuple-element.59, f32[1024,2048]{1,0:T(8,128)} %copy-done.2), kind=kLoop, calls=%fused_computation.30 | loop fusion | flops 8388608 | bytes 14680064 | tf_op jit(solution)/shard_map/convert.2
  223.9 2.4 pad_maximum_fusion
  226.3 6.3 %reduce-scatter.3.cloned.1.call-done = bf16[32,1024]{1,0:T(8,128)(2,1)} async-done(((bf16[1024,1024]{1,0:T(8,128)(2,1)}), bf16[32,1024]{1,0:T(8,128)(2,1)}) %reduce-scatter.3.cloned.1.call-update) | async-done | bytes 65552 | tf_op jit(solution)/shard_map/reduce_scatter | solution.py:128
  232.7 10.5 %fusion.8 = (f32[1024]{0:T(1024)S(1)}, f32[1024]{0:T(1024)S(1)}, f32[1024]{0:T(1024)S(1)}, f32[1024,1024]{0,1:T(8,128)}) fusion(bf16[1024,1024]{0,1:T(8,128)(2,1)S(1)} %copy-done.6, f32[1024]{0:T(1024)S(1)} %copy-done.18, f32[1024]{0:T(1024)S(1)} %add_rsqrt_fusion, f32[1024]{0:T(1024)S(1)} %broadcast_multiply_fusion.10, ...), kind=kOutput, calls=%fused_computation.10 | convolution fusion | flops 4304401408 | bytes 14704640 | tf_op jit(solution)/shard_map/dot_general | solution.py:132
  243.2 6.4 %convolution_convert_fusion = bf16[1024,2048]{1,0:T(8,128)(2,1)} fusion(bf16[1024,2048]{1,0:T(8,128)(2,1)S(1)} %copy-done.12, bf16[1024,1024]{0,1:T(8,128)(2,1)S(1)} %copy-done.6, f32[1024]{0:T(1024)S(1)} %copy-done.18, f32[1024]{0:T(1024)S(1)} %add_rsqrt_fusion, f32[1024]{0:T(1024)S(1)} %broadcast_multiply_fusion.10), kind=kOutput, calls=%fused_computation.37 | convolution fusion | flops 4302307328 | bytes 10498048 | tf_op jit(solution)/shard_map/dot_general | solution.py:26
  249.8 1.2 collective-permute-done
  251.0 1.3 collective-permute-start.1
  252.3 2.7 collective-permute-start.2
  255.8 4.7 %fusion.11 = bf16[1024,1024]{0,1:T(8,128)(2,1)} fusion(bf16[1024,1024]{0,1:T(8,128)(2,1)S(1)} %copy-done.6, f32[1024,1024]{0,1:T(8,128)} %get-tuple-element.110, f32[1024]{0:T(1024)S(1)} %get-tuple-element.111, f32[1024]{0:T(1024)S(1)} %get-tuple-element.112, f32[1024]{0:T(1024)S(1)} %copy-done.18, f32[1024]{0:T(1024)S(1)} %add_rsqrt_fusion, ...), kind=kLoop, calls=%fused_computation.13 | loop fusion | flops 9437184 | bytes 8409088 | tf_op jit(solution)/shard_map/convert_element_type | solution.py:142
  260.6 1.3 collective-permute-start.4
  261.8 2.7 collective-permute-start.5
  265.5 2.2 collective-permute-done.5
  267.7 2.4 collective-permute-done.6
  270.1 1.6 collective-permute-start.7
  271.7 2.9 collective-permute-start.8
  274.9 2.6 collective-permute-done.8
  277.5 2.5 collective-permute-done.9
  280.1 78.2 %reduce-scatter.5.cloned.1.call-done = bf16[32,2048]{1,0:T(8,128)(2,1)} async-done(((bf16[1024,2048]{1,0:T(8,128)(2,1)}), bf16[32,2048]{1,0:T(8,128)(2,1)}) %reduce-scatter.5.cloned.1.call-update) | async-done | bytes 131088 | tf_op jit(solution)/shard_map/reduce_scatter | solution.py:145
  358.3 1.7 maximum_convert_fusion.1
  360.1 1.5 collective-permute-start.10
  361.6 2.8 collective-permute-start.11
  364.8 2.5 copy.31
  368.0 4.3 %collective-permute-done.10 = f32[32,3072]{1,0:T(8,128)S(1)} collective-permute-done((f32[32,3072]{1,0:T(8,128)}, f32[32,3072]{1,0:T(8,128)S(1)}, u32[]{:S(2)}, u32[]{:S(2)}) %collective-permute-start.10) | collective-permute-done | bytes 393248 | tf_op jit(solution)/shard_map/ppermute | solution.py:42
  372.3 8.1 %collective-permute-done.11 = f32[32,3072]{1,0:T(8,128)S(1)} collective-permute-done((f32[32,3072]{1,0:T(8,128)}, f32[32,3072]{1,0:T(8,128)S(1)}, u32[]{:S(2)}, u32[]{:S(2)}) %collective-permute-start.11) | collective-permute-done | bytes 393248 | tf_op jit(solution)/shard_map/ppermute | solution.py:42
  380.4 2.6 collective-permute-done.12
  (100 shorter events, 14.7 us)
Async XLA Ops:
  7.2 51.5 %all-gather.3.cloned.1.call-start = ((), (), s32[]{:S(2)}) async-start(), calls=%async_computation.3 | async-start | bytes 4325376 | tf_op jit(solution)/shard_map/all_gather | solution.py:86
  7.9 151.1 %all-gather.5.cloned.1.call-start = ((), (), s32[]{:S(2)}) async-start(), calls=%async_computation.4 | async-start | bytes 2162688 | tf_op jit(solution)/shard_map/all_gather | solution.py:89
  9.9 3.9 %copy-start.17 = (f32[9,1024]{1,0:T(8,128)S(1)}, f32[9,1024]{1,0:T(8,128)}, u32[]{:S(2)}) copy-start(f32[9,1024]{1,0:T(8,128)} %param.16) | copy-start | bytes 110596
  9.9 4.0 %copy-start.19 = (s32[1024]{0:T(1024)S(1)}, s32[1024]{0:T(1024)}, u32[]{:S(2)}) copy-start(s32[1024]{0:T(1024)} %param.13) | copy-start | bytes 12292
  9.9 48.7 %copy-start.18 = (f32[1024]{0:T(1024)S(1)}, f32[1024]{0:T(1024)}, u32[]{:S(2)}) copy-start(f32[1024]{0:T(1024)} %param.14) | copy-start | bytes 12292
  12.8 52.5 %copy-start.5 = (bf16[1024,1024]{0,1:T(8,128)(2,1)}, bf16[1024,1024]{0,1:T(8,128)(2,1)S(1)}, u32[]{:S(2)}) copy-start(bf16[1024,1024]{0,1:T(8,128)(2,1)S(1)} %copy.26) | copy-start | bytes 6291460
  65.4 3.2 copy-start.2
  69.7 4.5 %copy-start = (f32[1024,1024]{1,0:T(8,128)}, f32[1024,1024]{1,0:T(8,128)S(1)}, u32[]{:S(2)}) copy-start(f32[1024,1024]{1,0:T(8,128)S(1)} %fusion.20) | copy-start | bytes 12582916
  74.2 4.1 %copy-start.13 = (bf16[1024,1024]{1,0:T(8,128)(2,1)S(1)}, bf16[1024,1024]{1,0:T(8,128)(2,1)}, u32[]{:S(2)}) copy-start(bf16[1024,1024]{1,0:T(8,128)(2,1)} %param.10) | copy-start | bytes 6291460
  78.3 1.3 copy-start.20
  83.8 64.0 %all-to-all-start = ((bf16[128,9,1024]{2,1,0:T(8,128)(2,1)}), bf16[128,9,1024]{2,1,0:T(8,128)(2,1)}, u32[]{:S(2)}, u32[]{:S(2)}) async-start(bf16[128,9,1024]{2,1,0:T(8,128)(2,1)} %copy.28), calls=%async_computation | async-start | bytes 8388608 | tf_op jit(solution)/shard_map/all_to_all | solution.py:68
  92.6 140.1 %reduce-scatter.3.cloned.1.call-start = ((), (), s32[]{:S(2)}) async-start(), calls=%async_computation.5 | async-start | bytes 2162688 | tf_op jit(solution)/shard_map/reduce_scatter | solution.py:128
  92.8 9.0 %copy-start.1 = (f32[1024,1024]{1,0:T(8,128)S(1)}, f32[1024,1024]{1,0:T(8,128)}, u32[]{:S(2)}) copy-start(f32[1024,1024]{1,0:T(8,128)} %copy-done) | copy-start | bytes 12582916
  92.8 14.0 %slice-start = ((s8[8388608]{0:T(1024)(128)(4,1)}), s8[4194304]{0:T(1024)(128)(4,1)S(1)}, s32[]{:S(2)}) async-start(s8[8388608]{0:T(1024)(128)(4,1)} %bitcast.74), calls=%async_computation.7 | async-start | bytes 8388608
  101.8 5.0 %slice-start.1 = ((s8[8388608]{0:T(1024)(128)(4,1)}), s8[4194304]{0:T(1024)(128)(4,1)S(1)}, s32[]{:S(2)}) async-start(s8[8388608]{0:T(1024)(128)(4,1)} %bitcast.74), calls=%async_computation.8 | async-start | bytes 8388608
  101.8 6.4 %copy-start.3 = (f32[1020,1024]{1,0:T(8,128)S(1)}, f32[1020,1024]{1,0:T(8,128)}, u32[]{:S(2)}) copy-start(f32[1020,1024]{1,0:T(8,128)} %get-tuple-element.76) | copy-start | bytes 12533764
  101.8 7.6 %copy-start.4 = (f32[1020,1024]{1,0:T(8,128)S(1)}, f32[1020,1024]{1,0:T(8,128)}, u32[]{:S(2)}) copy-start(f32[1020,1024]{1,0:T(8,128)} %get-tuple-element.77) | copy-start | bytes 12533764
  147.8 6.6 %copy-start.7 = (f32[1024,1024]{1,0:T(8,128)S(1)}, f32[1024,1024]{1,0:T(8,128)}, u32[]{:S(2)}) copy-start(f32[1024,1024]{1,0:T(8,128)} %add_multiply_fusion) | copy-start | bytes 12582916
  158.7 199.6 %reduce-scatter.5.cloned.1.call-start = ((), (), s32[]{:S(2)}) async-start(), calls=%async_computation.6 | async-start | bytes 4325376 | tf_op jit(solution)/shard_map/reduce_scatter | solution.py:145
  187.8 5.2 %copy-start.9 = (f32[1024,1024]{1,0:T(8,128)S(1)}, f32[1024,1024]{1,0:T(8,128)}, u32[]{:S(2)}) copy-start(f32[1024,1024]{1,0:T(8,128)} %get-tuple-element.75) | copy-start | bytes 12582916
  192.9 3.7 copy-start.8
  219.2 4.8 %copy-start.10 = (bf16[1024,1024]{1,0:T(8,128)(2,1)S(1)}, bf16[1024,1024]{1,0:T(8,128)(2,1)}, u32[]{:S(2)}) copy-start(bf16[1024,1024]{1,0:T(8,128)(2,1)} %get-tuple-element.58) | copy-start | bytes 6291460
  223.9 8.7 %copy-start.6 = (bf16[1024,1024]{0,1:T(8,128)(2,1)S(1)}, bf16[1024,1024]{0,1:T(8,128)(2,1)}, u32[]{:S(2)}) copy-start(bf16[1024,1024]{0,1:T(8,128)(2,1)} %copy-done.5) | copy-start | bytes 6291460
  232.7 10.5 %copy-start.12 = (bf16[1024,2048]{1,0:T(8,128)(2,1)S(1)}, bf16[1024,2048]{1,0:T(8,128)(2,1)}, u32[]{:S(2)}) copy-start(bf16[1024,2048]{1,0:T(8,128)(2,1)} %pad_maximum_fusion) | copy-start | bytes 12582916
  249.6 1.3 collective-permute-start
  251.0 9.5 %collective-permute-start.1 = (f32[10,1024]{1,0:T(8,128)S(1)}, f32[10,1024]{1,0:T(8,128)S(1)}, u32[]{:S(2)}, u32[]{:S(2)}) collective-permute-start(f32[10,1024]{1,0:T(8,128)S(1)} %bitcast.87), channel_id=1, source_target_pairs={{0,2},{1,3},{2,0},{3,1},{4,6},{5,7},{6,4},{7,5},{8,10},{9,11},{10,... | collective-permute-start | bytes 122888 | tf_op jit(solution)/shard_map/ppermute | solution.py:42
  252.3 8.2 %collective-permute-start.2 = (f32[10,1024]{1,0:T(8,128)S(1)}, f32[10,1024]{1,0:T(8,128)S(1)}, u32[]{:S(2)}, u32[]{:S(2)}) collective-permute-start(f32[10,1024]{1,0:T(8,128)S(1)} %bitcast.88), channel_id=1, source_target_pairs={{0,4},{1,5},{2,6},{3,7},{4,0},{5,1},{6,2},{7,3},{8,12},{9,13},{10,... | collective-permute-start | bytes 122888 | tf_op jit(solution)/shard_map/ppermute | solution.py:42
  255.0 5.5 %collective-permute-start.3 = (f32[10,1024]{1,0:T(8,128)S(1)}, f32[10,1024]{1,0:T(8,128)S(1)}, u32[]{:S(2)}, u32[]{:S(2)}) collective-permute-start(f32[10,1024]{1,0:T(8,128)S(1)} %bitcast.89), channel_id=1, source_target_pairs={{0,6},{1,7},{2,4},{3,5},{4,2},{5,3},{6,0},{7,1},{8,14},{9,15},{10,... | collective-permute-start | bytes 122888 | tf_op jit(solution)/shard_map/ppermute | solution.py:42
  260.5 97.9 %copy-start.15 = (bf16[32,1024]{1,0:T(8,128)(2,1)S(1)}, bf16[32,1024]{1,0:T(8,128)(2,1)}, u32[]{:S(2)}) copy-start(bf16[32,1024]{1,0:T(8,128)(2,1)} %reduce-scatter.3.cloned.1.call-done) | copy-start | bytes 196612
  260.5 104.3 %copy-start.11 = (bf16[1024,1024]{0,1:T(8,128)(2,1)S(1)}, bf16[1024,1024]{0,1:T(8,128)(2,1)}, u32[]{:S(2)}) copy-start(bf16[1024,1024]{0,1:T(8,128)(2,1)} %fusion.11) | copy-start | bytes 6291460
  260.6 4.9 %collective-permute-start.4 = (f32[10,1024]{1,0:T(8,128)S(1)}, f32[10,1024]{1,0:T(8,128)S(1)}, u32[]{:S(2)}, u32[]{:S(2)}) collective-permute-start(f32[10,1024]{1,0:T(8,128)S(1)} %fusion.77), channel_id=1, source_target_pairs={{0,8},{1,9},{2,10},{3,11},{4,12},{5,13},{6,14},{7,15},{8,0},{9,1},... | collective-permute-start | bytes 122888 | tf_op jit(solution)/shard_map/ppermute | solution.py:42
  261.8 5.8 %collective-permute-start.5 = (f32[10,1024]{1,0:T(8,128)S(1)}, f32[10,1024]{1,0:T(8,128)S(1)}, u32[]{:S(2)}, u32[]{:S(2)}) collective-permute-start(f32[10,1024]{1,0:T(8,128)S(1)} %fusion.77), channel_id=1, source_target_pairs={{0,16},{1,17},{2,18},{3,19},{4,20},{5,21},{6,22},{7,23},{8,24},{9,... | collective-permute-start | bytes 122888 | tf_op jit(solution)/shard_map/ppermute | solution.py:42
  264.5 5.5 %collective-permute-start.6 = (f32[10,1024]{1,0:T(8,128)S(1)}, f32[10,1024]{1,0:T(8,128)S(1)}, u32[]{:S(2)}, u32[]{:S(2)}) collective-permute-start(f32[10,1024]{1,0:T(8,128)S(1)} %fusion.77), channel_id=1, source_target_pairs={{0,24},{1,25},{2,26},{3,27},{4,28},{5,29},{6,30},{7,31},{8,16},{9,... | collective-permute-start | bytes 122888 | tf_op jit(solution)/shard_map/ppermute | solution.py:42
  270.1 4.8 %collective-permute-start.7 = (f32[10,1024]{1,0:T(8,128)S(1)}, f32[10,1024]{1,0:T(8,128)S(1)}, u32[]{:S(2)}, u32[]{:S(2)}) collective-permute-start(f32[10,1024]{1,0:T(8,128)S(1)} %fusion.76), channel_id=1, source_target_pairs={{0,32},{32,0},{64,96},{96,64},{1,33},{33,1},{65,97},{97,65},{2,34}... | collective-permute-start | bytes 122888 | tf_op jit(solution)/shard_map/ppermute | solution.py:42
  271.7 5.8 %collective-permute-start.8 = (f32[10,1024]{1,0:T(8,128)S(1)}, f32[10,1024]{1,0:T(8,128)S(1)}, u32[]{:S(2)}, u32[]{:S(2)}) collective-permute-start(f32[10,1024]{1,0:T(8,128)S(1)} %fusion.76), channel_id=1, source_target_pairs={{0,64},{32,96},{64,0},{96,32},{1,65},{33,97},{65,1},{97,33},{2,66}... | collective-permute-start | bytes 122888 | tf_op jit(solution)/shard_map/ppermute | solution.py:42
  274.5 5.5 %collective-permute-start.9 = (f32[10,1024]{1,0:T(8,128)S(1)}, f32[10,1024]{1,0:T(8,128)S(1)}, u32[]{:S(2)}, u32[]{:S(2)}) collective-permute-start(f32[10,1024]{1,0:T(8,128)S(1)} %fusion.76), channel_id=1, source_target_pairs={{0,96},{32,64},{64,32},{96,0},{1,97},{33,65},{65,33},{97,1},{2,98}... | collective-permute-start | bytes 122888 | tf_op jit(solution)/shard_map/ppermute | solution.py:42
  280.1 87.2 %copy-start.16 = (f32[10,1024]{1,0:T(8,128)}, f32[10,1024]{1,0:T(8,128)S(1)}, u32[]{:S(2)}) copy-start(f32[10,1024]{1,0:T(8,128)S(1)} %add_bitcast_fusion.1) | copy-start | bytes 122884
  358.3 9.6 %copy-start.14 = (bf16[32,2048]{1,0:T(8,128)(2,1)S(1)}, bf16[32,2048]{1,0:T(8,128)(2,1)}, u32[]{:S(2)}) copy-start(bf16[32,2048]{1,0:T(8,128)(2,1)} %reduce-scatter.5.cloned.1.call-done) | copy-start | bytes 393220
  360.1 12.2 %collective-permute-start.10 = (f32[32,3072]{1,0:T(8,128)}, f32[32,3072]{1,0:T(8,128)S(1)}, u32[]{:S(2)}, u32[]{:S(2)}) collective-permute-start(f32[32,3072]{1,0:T(8,128)} %maximum_convert_fusion.1), channel_id=1, source_target_pairs={{0,32},{32,0},{64,96},{96,64},{1,33},{33,1},{65,97},{97,65},{2,34}... | collective-permute-start | bytes 1179656 | tf_op jit(solution)/shard_map/ppermute | solution.py:42
  361.6 18.8 %collective-permute-start.11 = (f32[32,3072]{1,0:T(8,128)}, f32[32,3072]{1,0:T(8,128)S(1)}, u32[]{:S(2)}, u32[]{:S(2)}) collective-permute-start(f32[32,3072]{1,0:T(8,128)} %maximum_convert_fusion.1), channel_id=1, source_target_pairs={{0,64},{32,96},{64,0},{96,32},{1,65},{33,97},{65,1},{97,33},{2,66}... | collective-permute-start | bytes 1179656 | tf_op jit(solution)/shard_map/ppermute | solution.py:42
  364.5 18.5 %collective-permute-start.12 = (f32[32,3072]{1,0:T(8,128)}, f32[32,3072]{1,0:T(8,128)S(1)}, u32[]{:S(2)}, u32[]{:S(2)}) collective-permute-start(f32[32,3072]{1,0:T(8,128)} %maximum_convert_fusion.1), channel_id=1, source_target_pairs={{0,96},{32,64},{64,32},{96,0},{1,97},{33,65},{65,33},{97,1},{2,98}... | collective-permute-start | bytes 1179656 | tf_op jit(solution)/shard_map/ppermute | solution.py:42
Sparse Core Ops, SparseCore 0:
  10.2 48.3 all-gather.2
  60.9 58.9 all-gather.4
  158.9 73.7 reduce-scatter.2
  280.2 78.0 reduce-scatter.4

commit v3 on v2

--- a/solution.py
+++ b/solution.py
@@ -26,6 +26,17 @@
     return lax.dot_general(
         left, right, (((0,), (0,)), ((), ())), preferred_element_type=jnp.float32
     )
+
+
+def butterfly(x, axis):
+    size = lax.axis_size(axis)
+    if size & (size - 1):
+        return lax.psum(x, axis)
+    m = 1
+    while m < size:
+        x = x + lax.ppermute(x, axis, [(i, i ^ m) for i in range(size)])
+        m *= 2
+    return x
 
 
 def group_sum(x, axis):
@@ -83,9 +94,8 @@
     n_data = lax.axis_size("dp")
     n_shard = lax.axis_size("fsdp")
     ranks = n_data * n_shard
+    out_grad = route(llm_grad, dest_rank, ranks)
     up_full = lax.all_gather(up_weight, "fsdp", axis=0, tiled=True)
-    llm_grad, up_full = lax.optimization_barrier((llm_grad, up_full))
-    out_grad = route(llm_grad, dest_rank, ranks)
     down_full = lax.all_gather(down_weight, "fsdp", axis=0, tiled=True)
     taps = kernel.shape[0]
     middle = (taps - 1) // 2
@@ -114,39 +124,40 @@
     act = (conv * sig_c).astype(jnp.bfloat16)
     act_grad = jnp.dot(out_grad, down_full.T, preferred_element_type=jnp.float32)
     conv_grad = act_grad * sig_c * (1.0 + conv * (1.0 - sig_c)) * keep
-    kernel_rows = []
     glu_grad = jnp.zeros((rows, width), jnp.float32)
     for k in range(taps):
         offset = k - middle
         masked = conv_grad * sames[k]
-        kernel_rows.append(jnp.sum(masked * shift_rows(glu_f, offset, 0.0), axis=0))
         glu_grad = glu_grad + kernel[k][None, :] * shift_rows(masked, -offset, 0.0)
-    kernel_term = jnp.stack(kernel_rows, axis=0)
     value_grad = glu_grad * sig_b
     gate_grad = glu_grad * value * sig_b * (1.0 - sig_b)
     up_out_grad = jnp.concatenate([value_grad, gate_grad], axis=1).astype(jnp.bfloat16)
-    down_sum = lax.psum_scatter(
-        contract_rows(act, out_grad).astype(jnp.bfloat16), "fsdp", scatter_dimension=0, tiled=True
+    weight_terms = jnp.concatenate(
+        [contract_rows(hidden, up_out_grad), contract_rows(act, out_grad)], axis=1
+    ).astype(jnp.bfloat16)
+    weight_terms, conv_grad, up_out_grad = lax.optimization_barrier(
+        (weight_terms, conv_grad, up_out_grad)
     )
-    up_out_grad, down_sum = lax.optimization_barrier((up_out_grad, down_sum))
+    shard_sum = lax.psum_scatter(weight_terms, "fsdp", scatter_dimension=0, tiled=True)
+    kernel_rows = []
+    for k in range(taps):
+        offset = k - middle
+        masked = conv_grad * sames[k]
+        kernel_rows.append(jnp.sum(masked * shift_rows(glu_f, offset, 0.0), axis=0))
+    kernel_term = jnp.stack(kernel_rows, axis=0)
     hidden_grad = jnp.dot(up_out_grad, up_full.T, preferred_element_type=jnp.float32)
     gain_term = jnp.sum(hidden_grad * normed, axis=0)
-    small = group_sum(jnp.concatenate([kernel_term, gain_term[None, :]], axis=0), "fsdp")
-    small = group_sum(small, "dp")
     scaled = hidden_grad * norm_gain[None, :]
     input_grad = rstd * (
         scaled
         - jnp.mean(scaled, axis=1, keepdims=True)
         - normed * jnp.mean(scaled * normed, axis=1, keepdims=True)
     )
-    input_grad = input_grad.astype(jnp.bfloat16)
-    up_term = contract_rows(hidden, up_out_grad).astype(jnp.bfloat16)
-    up_term, small, input_grad = lax.optimization_barrier((up_term, small, input_grad))
-    up_sum = lax.psum_scatter(up_term, "fsdp", scatter_dimension=0, tiled=True)
-    shard_sum = jnp.concatenate([up_sum, down_sum], axis=1).astype(jnp.float32)
-    shard_sum = group_sum(shard_sum, "dp")
+    small = jnp.concatenate([kernel_term, gain_term[None, :]], axis=0)
+    small = group_sum(group_sum(small, "fsdp"), "dp")
+    shard_sum = butterfly(shard_sum.astype(jnp.float32), "dp")
     return (
-        input_grad,
+        input_grad.astype(jnp.bfloat16),
         shard_sum[:, : 2 * width],
         shard_sum[:, 2 * width :],
         small[:taps],

time: 400 us -> 310 us (0.78); the launches traced: 392 us -> 306 us
  waiting for transfers between devices: 182 us -> 103 us
  other arithmetic: 50 us -> 75.8 us
  matrix products: 60.1 us -> 40.2 us
  local copies, waits for them, and re-layouts: 56.7 us -> 42.2 us
    reduce_scatter x2 -> x1, waiting for transfers between devices: 84.6 us -> 38.9 us  [on_device(): lax.psum_scatter(weight_terms, 'fsdp', scatter_dimension=0, tiled=True)]
    all_gather x1, waiting for transfers between devices: 44.6 us -> 0.01 us  [on_device(): up_full = lax.all_gather(up_weight, 'fsdp', axis=0, tiled=True)]
    all_to_all x1, waiting for transfers between devices: 25.1 us -> 50.6 us  [route(): lax.all_to_all(outbox, ('dp', 'fsdp'), split_axis=0, concat_axis=0, tiled...]
    ppermute x13 -> x10, waiting for transfers between devices: 26 us -> 2.05 us  [group_sum(): lax.ppermute(x, axis, [(i, i ^ d << shift) for i in range(size)])]
    dot_general x1, matrix products: 28.7 us -> 6.42 us  [on_device(): jnp.dot(out_grad, down_full.T, preferred_element_type=jnp.float32)]
    mul x0 -> x4, other arithmetic: none -> 18.4 us  [on_device(): masked = conv_grad * sames[k]]
    reduce_sum x0 -> x1, other arithmetic: none -> 12.2 us  [on_device(): kernel_rows.append(jnp.sum(masked * shift_rows(glu_f, offset, 0.0), axis=0))]
    ppermute x0 -> x2, waiting for transfers between devices: none -> 10.5 us  [butterfly(): x = x + lax.ppermute(x, axis, [(i, i ^ m) for i in range(size)])]
  transfers between devices with their start and end apart: 18 -> 16, of which waited for: 13 -> 6; matrix products, arithmetic and copies ran while one was open for 36% -> 32% of each run, Pallas kernels for 0% -> 0%
where the time goes in v3:
time: 310 us; the launch traced here: 306 us
  waiting for transfers between devices  103 us (33%)
  other arithmetic  75.8 us (24%)
  local copies, waits for them, and re-layouts  42.2 us (14%)
  matrix products  40.2 us (13%)
  starting transfers between devices  29.7 us (10%)
  between operations  14.8 us (5%)
    all_to_all x1, waiting for transfers between devices, route(): lax.all_to_all(outbox, ('dp', 'fsdp'), split_axis=0, concat_axis=0, tiled...  50.6 us
    reduce_scatter x1, waiting for transfers between devices, on_device(): lax.psum_scatter(weight_terms, 'fsdp', scatter_dimension=0, tiled=True)  38.9 us
    mul x4, other arithmetic, on_device(): masked = conv_grad * sames[k]  18.4 us
    slice x8, local copies, waits for them, and re-layouts, shift_rows(): return jnp.concatenate([pad, values[:rows + offset]], axis=0)  16.8 us
    another operation x3, other arithmetic  15.7 us
    mul x1, other arithmetic, on_device(): conv = conv * keep  12.9 us
    ppermute x10, starting transfers between devices, group_sum(): lax.ppermute(x, axis, [(i, i ^ d << shift) for i in range(size)])  12.6 us
    reduce_sum x1, other arithmetic, on_device(): kernel_rows.append(jnp.sum(masked * shift_rows(glu_f, offset, 0.0), axis=0))  12.2 us
  transfers between devices with their start and end apart: 16, of which 6 were waited for; matrix products, arithmetic and copies ran while one was open for 32% of the time, Pallas kernels for 0%

profile of v3, /device:TPU:0, one launch (start us, length us, event | category | flops | bytes accessed | tf_op | source)
XLA Modules:
  0.0 306.0 jit_solution(7725852677004967752)
XLA Ops:
  7.9 2.7 copy.36
  11.5 3.6 %copy.37 = bf16[128,9,1024]{2,1,0:T(8,128)(2,1)} copy(bf16[128,9,1024]{2,0,1:T(8,128)(2,1)S(1)} %fusion.26) | data formatting | bytes 4718592 | tf_op jit(solution)/shard_map/convert_element_type | solution.py:78
  15.1 11.7 %all-to-all-start = ((bf16[128,9,1024]{2,1,0:T(8,128)(2,1)}), bf16[128,9,1024]{2,1,0:T(8,128)(2,1)}, u32[]{:S(2)}, u32[]{:S(2)}) async-start(bf16[128,9,1024]{2,1,0:T(8,128)(2,1)} %copy.37), calls=%async_computation | async-start | bytes 8388608 | tf_op jit(solution)/shard_map/all_to_all | solution.py:79
  28.0 2.9 copy.35
  35.3 50.6 %all-to-all-done = bf16[128,9,1024]{2,1,0:T(8,128)(2,1)} async-done(((bf16[128,9,1024]{2,1,0:T(8,128)(2,1)}), bf16[128,9,1024]{2,1,0:T(8,128)(2,1)}, u32[]{:S(2)}, u32[]{:S(2)}) %all-to-all-start) | async-done | bytes 2359328 | tf_op jit(solution)/shard_map/all_to_all | solution.py:79
  85.9 1.8 slice.187
  87.7 2.0 fusion.43
  89.7 4.0 %fusion.32 = bf16[128,8,1024]{2,0,1:T(8,128)(2,1)} fusion(bf16[128,8,1024]{2,1,0:T(8,128)(2,1)S(1)} %slice.187, f32[128]{0:T(128)S(1)} %fusion.43, f32[128]{0:T(128)S(1)} %iota_add_fusion), kind=kOutput, calls=%fused_computation.60 | convolution fusion | flops 269500416 | bytes 4195328 | tf_op jit(solution)/shard_map/js,src->jrc/dot_general | solution.py:84
  93.7 7.5 %fusion.38 = f32[1024,2048]{0,1:T(8,128)S(1)} fusion(bf16[1024,2048]{1,0:T(8,128)(2,1)} %all-gather.5.cloned.1.call-done, bf16[1024,1024]{0,1:T(8,128)(2,1)S(1)} %copy.35, f32[1024]{0:T(1024)S(1)} %copy-done.32, f32[1024]{0:T(1024)S(1)} %add_rsqrt_fusion, f32[1024]{0:T(1024)S(1)} %broadcast_multiply_fusion.2), kind=kOutput, calls=%fused_computation.63 | convolution fusion | flops 4300210176 | bytes 14692352 | tf_op jit(solution)/shard_map/dot_general | solution.py:109
  101.2 1.5 fusion.20
  102.7 1.7 fusion.62
  104.4 5.3 %fusion.63 = (f32[1021,1024]{0,1:T(8,128)}, f32[1021,1024]{0,1:T(8,128)}) fusion(f32[1024,1024]{0,1:T(8,128)S(1)} %fusion.20), kind=kLoop, calls=%fused_computation.115 | loop fusion | bytes 16728064 | tf_op jit(solution)/shard_map/slice | solution.py:16
  109.7 4.7 %fusion.64 = (f32[1022,1024]{0,1:T(8,128)}, f32[1022,1024]{0,1:T(8,128)}) fusion(f32[1024,1024]{0,1:T(8,128)S(1)} %fusion.20), kind=kLoop, calls=%fused_computation.116 | loop fusion | bytes 16744448 | tf_op jit(solution)/shard_map/slice | solution.py:16
  114.5 4.9 %fusion.65 = (f32[1023,1024]{0,1:T(8,128)}, f32[1023,1024]{0,1:T(8,128)}) fusion(f32[1024,1024]{0,1:T(8,128)S(1)} %fusion.20), kind=kLoop, calls=%fused_computation.117 | loop fusion | bytes 16760832 | tf_op jit(solution)/shard_map/slice | solution.py:16
  119.4 12.9 %add_multiply_fusion = f32[1024,1024]{0,1:T(8,128)S(1)} fusion(f32[1020,1024]{0,1:T(8,128)S(1)} %get-tuple-element.54, f32[1021,1024]{0,1:T(8,128)} %get-tuple-element.56, f32[1022,1024]{0,1:T(8,128)} %get-tuple-element.58, f32[1023,1024]{0,1:T(8,128)} %get-tuple-element.60, f32[1023,1024]{0,1:T(8,128)} %get-tuple-element.59, ...), kind=kLoop, calls=%fused_computation.44 | loop fusion | flops 33554432 | bytes 46129152 | tf_op jit(solution)/shard_map/mul | solution.py:122
  132.3 2.0 copy-done.14
  134.3 4.0 %fusion.29 = bf16[1024,1024]{1,0:T(8,128)(2,1)} fusion(f32[1024,1024]{0,1:T(8,128)S(1)} %add_multiply_fusion, bf16[128,8,1024]{2,0,1:T(8,128)(2,1)S(1)} %copy-done.15), kind=kOutput, calls=%fused_computation.59 | convolution fusion | flops 2153775104 | bytes 8388608 | tf_op jit(solution)/shard_map/dot_general | solution.py:26
  138.3 6.4 %multiply_multiply_fusion = f32[1024,1024]{0,1:T(8,128)S(1)} fusion(f32[1024,1024]{0,1:T(8,128)} %copy-done.14, bf16[1024,1024]{1,0:T(8,128)(2,1)} %all-gather.3.cloned.1.call-done, f32[1024]{0:T(1024)S(1)} %convert_element_type.106, bf16[128,8,1024]{2,0,1:T(8,128)(2,1)S(1)} %copy-done.15), kind=kOutput, calls=%fused_computation.42 | convolution fusion | flops 2156920832 | bytes 12587008 | tf_op jit(solution)/shard_map/dot_general | solution.py:125
  144.8 3.6 %slice_multiply_fusion.7 = (f32[1020,1024]{0,1:T(8,128)S(1)}, f32[1020,1024]{0,1:T(8,128)}) fusion(f32[1024,1024]{0,1:T(8,128)S(1)} %multiply_multiply_fusion, f32[1020]{0:T(1024)S(1)} %copy-done.31, f32[1020]{0:T(1024)S(1)} %bitcast.80), kind=kLoop, calls=%fused_computation.23 | loop fusion | flops 2088960 | bytes 16719840 | tf_op jit(solution)/shard_map/mul | solution.py:130
  148.3 4.9 %slice_multiply_fusion.6 = (f32[1021,1024]{0,1:T(8,128)}, f32[1021,1024]{0,1:T(8,128)}) fusion(f32[1024,1024]{0,1:T(8,128)S(1)} %multiply_multiply_fusion, f32[1021]{0:T(1024)S(1)} %copy-done.30, f32[1021]{0:T(1024)S(1)} %bitcast.81), kind=kLoop, calls=%fused_computation.22 | loop fusion | flops 2091008 | bytes 16736232 | tf_op jit(solution)/shard_map/mul | solution.py:130
  153.2 4.8 %slice_multiply_fusion.5 = (f32[1022,1024]{0,1:T(8,128)}, f32[1022,1024]{0,1:T(8,128)}) fusion(f32[1024,1024]{0,1:T(8,128)S(1)} %multiply_multiply_fusion, f32[1022]{0:T(1024)S(1)} %copy-done.29, f32[1022]{0:T(1024)S(1)} %bitcast.82), kind=kLoop, calls=%fused_computation.21 | loop fusion | flops 2093056 | bytes 16752624 | tf_op jit(solution)/shard_map/mul | solution.py:130
  158.0 5.1 %slice_multiply_fusion.4 = (f32[1023,1024]{0,1:T(8,128)}, f32[1023,1024]{0,1:T(8,128)}) fusion(f32[1024,1024]{0,1:T(8,128)S(1)} %multiply_multiply_fusion, f32[1023]{0:T(1024)S(1)} %copy-done.28, f32[1023]{0:T(1024)S(1)} %bitcast.83), kind=kLoop, calls=%fused_computation.20 | loop fusion | flops 2095104 | bytes 16769016 | tf_op jit(solution)/shard_map/mul | solution.py:130
  163.2 13.8 %multiply_convert_fusion.2 = (bf16[1024,1024]{0,1:T(8,128)(2,1)}, f32[1024,1024]{0,1:T(8,128)S(1)}) fusion(f32[1024,2048]{0,1:T(8,128)S(1)} %bitcast.64, f32[1020,1024]{0,1:T(8,128)} %get-tuple-element.46, f32[1024]{0:T(1024)} %bitcast.99, f32[1021,1024]{0,1:T(8,128)} %get-tuple-element.48, f32[1024]{0:T(1024)} %bitcast.101, ...), kind=kLoop, calls=%fused_computation.40 | loop fusion | flops 23068672 | bytes 48189440 | tf_op jit(solution)/shard_map/convert.3
  177.1 1.7 multiply_convert_fusion.1
  179.2 6.2 %convolution_convert_fusion = bf16[1024,2048]{1,0:T(8,128)(2,1)S(1)} fusion(bf16[1024,1024]{0,1:T(8,128)(2,1)S(1)} %copy-done.12, f32[1024]{0:T(1024)S(1)} %copy-done.33, f32[1024]{0:T(1024)S(1)} %copy-done.27, f32[1024]{0:T(1024)S(1)} %broadcast_multiply_fusion.2, bf16[1024,1024]{0,1:T(8,128)(2,1)S(1)} %multiply_convert_fusion.1, ...), kind=kOutput, calls=%fused_computation.46 | convolution fusion | flops 4310695936 | bytes 10498048 | tf_op jit(solution)/shard_map/dot_general | solution.py:26
  185.5 2.5 pad_maximum_fusion.1
  188.0 3.3 %pad_maximum_fusion = bf16[1024,3072]{1,0:T(8,128)(2,1)} fusion(bf16[1024,1024]{1,0:T(8,128)(2,1)S(1)} %copy-done.16, bf16[1024,2048]{1,0:T(8,128)(2,1)S(1)} %convolution_convert_fusion), kind=kLoop, calls=%fused_computation | loop fusion | flops 12582912 | bytes 12582912 | tf_op jit(solution)/shard_map/concatenate | solution.py:135
  191.4 11.3 %fusion.11 = (f32[1024]{0:T(1024)S(1)}, f32[1024]{0:T(1024)S(1)}, f32[1024]{0:T(1024)S(1)}, f32[1024,1024]{0,1:T(8,128)}) fusion(bf16[1024,1024]{0,1:T(8,128)(2,1)} %copy-done.11, f32[1024]{0:T(1024)S(1)} %copy-done.27, f32[1024]{0:T(1024)S(1)} %broadcast_multiply_fusion.2, f32[1024]{0:T(1024)S(1)} %copy-done.33, ...), kind=kOutput, calls=%fused_computation.14 | convolution fusion | flops 4304401408 | bytes 14704640 | tf_op jit(solution)/shard_map/dot_general | solution.py:148
  202.7 1.0 copy-done.8
  203.7 1.4 copy-done.9
  205.1 1.4 copy-done.10
  206.4 12.2 %multiply_reduce_fusion = (f32[1024]{0:T(1024)S(1)}, f32[1024]{0:T(1024)S(1)}, f32[1024]{0:T(1024)S(1)}, f32[1024]{0:T(1024)S(1)}, f32[1024]{0:T(1024)S(1)}, /*i...) fusion(f32[1024,1024]{0,1:T(8,128)S(1)} %copy-done.1, f32[1020,1024]{0,1:T(8,128)S(1)} %copy-done.6, ...), kind=kLoop, calls=%fused_computation.29 | loop fusion | flops 33545216 | bytes 46125056 | tf_op jit(solution)/shard_map/reduce_sum | solution.py:146
  218.8 1.2 collective-permute-done.2
  220.2 1.7 collective-permute-start.4
  221.9 2.4 collective-permute-start.3
  224.2 4.0 %fusion.10 = bf16[1024,1024]{0,1:T(8,128)(2,1)S(1)} fusion(bf16[1024,1024]{0,1:T(8,128)(2,1)} %copy-done.11, f32[1024,1024]{0,1:T(8,128)} %get-tuple-element.86, f32[1024]{0:T(1024)S(1)} %get-tuple-element.87, f32[1024]{0:T(1024)S(1)} %get-tuple-element.88, f32[1024]{0:T(1024)S(1)} %copy-done.33, f32[1024]{0:T(1024)S(1)} %copy-done.27, ...), kind=kLoop, calls=%fused_computation.13 | loop fusion | flops 9437184 | bytes 8409088 | tf_op jit(solution)/shard_map/convert_element_type | solution.py:160
  228.3 2.6 copy.43
  230.9 3.0 collective-permute-start.8
  233.9 1.1 collective-permute-start.7
  235.1 38.9 %reduce-scatter.2.cloned.1.call-done = bf16[32,3072]{1,0:T(8,128)(2,1)} async-done(((bf16[1024,3072]{1,0:T(8,128)(2,1)}), bf16[32,3072]{1,0:T(8,128)(2,1)}) %reduce-scatter.2.cloned.1.call-update) | async-done | bytes 196624 | tf_op jit(solution)/shard_map/reduce_scatter | solution.py:141
  274.0 1.0 convert_element_type.109
  274.9 1.6 collective-permute-start
  276.6 2.2 collective-permute-start.11
  279.7 1.1 collective-permute-start.9
  280.8 4.7 %collective-permute-done = f32[32,3072]{1,0:T(8,128)S(1)} collective-permute-done((f32[32,3072]{1,0:T(8,128)S(1)}, f32[32,3072]{1,0:T(8,128)S(1)}, u32[]{:S(2)}, u32[]{:S(2)}) %collective-permute-start) | collective-permute-done | bytes 393248 | tf_op jit(solution)/shard_map/ppermute | solution.py:37
  285.5 1.0 convert_add_fusion
  286.5 3.4 %collective-permute-start.1 = (f32[32,3072]{1,0:T(8,128)S(1)}, f32[32,3072]{1,0:T(8,128)S(1)}, u32[]{:S(2)}, u32[]{:S(2)}) collective-permute-start(f32[32,3072]{1,0:T(8,128)S(1)} %convert_add_fusion), channel_id=1, source_target_pairs={{0,64},{32,96},{64,0},{96,32},{1,65},{33,97},{65,1},{97,33},{2,66}... | collective-permute-start | bytes 1179656 | tf_op jit(solution)/shard_map/ppermute | solution.py:37
  292.0 5.8 %collective-permute-done.1 = f32[32,3072]{1,0:T(8,128)S(1)} collective-permute-done((f32[32,3072]{1,0:T(8,128)S(1)}, f32[32,3072]{1,0:T(8,128)S(1)}, u32[]{:S(2)}, u32[]{:S(2)}) %collective-permute-start.1) | collective-permute-done | bytes 393248 | tf_op jit(solution)/shard_map/ppermute | solution.py:37
  (133 shorter events, 12.4 us)
Async XLA Ops:
  7.2 3.6 %copy-start.35 = (s32[1,128]{1,0:T(1,128)S(1)}, s32[1,128]{1,0:T(1,128)}, u32[]{:S(2)}) copy-start(s32[1,128]{1,0:T(1,128)} %param.11) | copy-start | bytes 1540
  7.2 86.5 %all-gather.5.cloned.1.call-start = ((), (), s32[]{:S(2)}) async-start(), calls=%async_computation.3 | async-start | bytes 4325376 | tf_op jit(solution)/shard_map/all_gather | solution.py:98
  15.1 70.8 %all-to-all-start = ((bf16[128,9,1024]{2,1,0:T(8,128)(2,1)}), bf16[128,9,1024]{2,1,0:T(8,128)(2,1)}, u32[]{:S(2)}, u32[]{:S(2)}) async-start(bf16[128,9,1024]{2,1,0:T(8,128)(2,1)} %copy.37), calls=%async_computation | async-start | bytes 8388608 | tf_op jit(solution)/shard_map/all_to_all | solution.py:79
  26.8 4.0 %copy-start.34 = (s32[1024]{0:T(1024)S(1)}, s32[1024]{0:T(1024)}, u32[]{:S(2)}) copy-start(s32[1024]{0:T(1024)} %param.13) | copy-start | bytes 12292
  26.8 4.0 %copy-start.36 = (s32[1,4]{1,0:T(1,128)S(1)}, s32[1,4]{1,0:T(1,128)}, u32[]{:S(2)}) copy-start(s32[1,4]{1,0:T(1,128)} %param.12) | copy-start | bytes 52
  26.9 111.4 %all-gather.3.cloned.1.call-start = ((), (), s32[]{:S(2)}) async-start(), calls=%async_computation.2 | async-start | bytes 2162688 | tf_op jit(solution)/shard_map/all_gather | solution.py:99
  27.6 7.6 %copy-start.25 = (f32[9,1024]{1,0:T(8,128)S(1)}, f32[9,1024]{1,0:T(8,128)}, u32[]{:S(2)}) copy-start(f32[9,1024]{1,0:T(8,128)} %param.16) | copy-start | bytes 110596
  27.6 246.3 %reduce-scatter.2.cloned.1.call-start = ((), (), s32[]{:S(2)}) async-start(), calls=%async_computation.4 | async-start | bytes 6488064 | tf_op jit(solution)/shard_map/reduce_scatter | solution.py:141
  30.8 62.9 %copy-start.11 = (bf16[1024,1024]{0,1:T(8,128)(2,1)}, bf16[1024,1024]{0,1:T(8,128)(2,1)S(1)}, u32[]{:S(2)}) copy-start(bf16[1024,1024]{0,1:T(8,128)(2,1)S(1)} %copy.35) | copy-start | bytes 6291460
  35.2 58.5 %copy-start.26 = (f32[1024]{0:T(1024)}, f32[1024]{0:T(1024)S(1)}, u32[]{:S(2)}) copy-start(f32[1024]{0:T(1024)S(1)} %add_rsqrt_fusion) | copy-start | bytes 12292
  35.2 84.1 %copy-start.17 = (f32[1,1024]{1,0:T(1,128)}, f32[1,1024]{1,0:T(1,128)S(1)}, u32[]{:S(2)}) copy-start(f32[1,1024]{1,0:T(1,128)S(1)} %get-tuple-element.62) | copy-start | bytes 12292
  35.2 84.1 %copy-start.18 = (f32[1,1024]{1,0:T(1,128)}, f32[1,1024]{1,0:T(1,128)S(1)}, u32[]{:S(2)}) copy-start(f32[1,1024]{1,0:T(1,128)S(1)} %get-tuple-element.63) | copy-start | bytes 12292
  35.2 84.1 %copy-start.19 = (f32[1,1024]{1,0:T(1,128)}, f32[1,1024]{1,0:T(1,128)S(1)}, u32[]{:S(2)}) copy-start(f32[1,1024]{1,0:T(1,128)S(1)} %get-tuple-element.64) | copy-start | bytes 12292
  35.2 84.1 %copy-start.20 = (f32[1,1024]{1,0:T(1,128)}, f32[1,1024]{1,0:T(1,128)S(1)}, u32[]{:S(2)}) copy-start(f32[1,1024]{1,0:T(1,128)S(1)} %get-tuple-element.65) | copy-start | bytes 12292
  35.3 84.1 %copy-start.21 = (f32[1,1024]{1,0:T(1,128)}, f32[1,1024]{1,0:T(1,128)S(1)}, u32[]{:S(2)}) copy-start(f32[1,1024]{1,0:T(1,128)S(1)} %get-tuple-element.66) | copy-start | bytes 12292
  35.3 84.1 %copy-start.22 = (f32[1,1024]{1,0:T(1,128)}, f32[1,1024]{1,0:T(1,128)S(1)}, u32[]{:S(2)}) copy-start(f32[1,1024]{1,0:T(1,128)S(1)} %get-tuple-element.67) | copy-start | bytes 12292
  35.3 84.1 %copy-start.23 = (f32[1,1024]{1,0:T(1,128)}, f32[1,1024]{1,0:T(1,128)S(1)}, u32[]{:S(2)}) copy-start(f32[1,1024]{1,0:T(1,128)S(1)} %get-tuple-element.68) | copy-start | bytes 12292
  35.3 84.1 %copy-start.24 = (f32[1,1024]{1,0:T(1,128)}, f32[1,1024]{1,0:T(1,128)S(1)}, u32[]{:S(2)}) copy-start(f32[1,1024]{1,0:T(1,128)S(1)} %get-tuple-element.69) | copy-start | bytes 12292
  35.3 58.4 %copy-start.32 = (f32[1024]{0:T(1024)S(1)}, f32[1024]{0:T(1024)}, u32[]{:S(2)}) copy-start(f32[1024]{0:T(1024)} %param.14) | copy-start | bytes 12292
  101.2 18.2 %copy-start.2 = (f32[1024,2048]{0,1:T(8,128)}, f32[1024,2048]{0,1:T(8,128)S(1)}, u32[]{:S(2)}) copy-start(f32[1024,2048]{0,1:T(8,128)S(1)} %fusion.38) | copy-start | bytes 25165828
  104.4 15.0 %copy-start.3 = (f32[1020,1024]{0,1:T(8,128)}, f32[1020,1024]{0,1:T(8,128)S(1)}, u32[]{:S(2)}) copy-start(f32[1020,1024]{0,1:T(8,128)S(1)} %get-tuple-element.53) | copy-start | bytes 12533764
  104.4 15.0 %copy-start.5 = (f32[1020,1024]{0,1:T(8,128)}, f32[1020,1024]{0,1:T(8,128)S(1)}, u32[]{:S(2)}) copy-start(f32[1020,1024]{0,1:T(8,128)S(1)} %get-tuple-element.54) | copy-start | bytes 12533764
  119.4 14.9 %copy-start.15 = (bf16[128,8,1024]{2,0,1:T(8,128)(2,1)S(1)}, bf16[128,8,1024]{2,0,1:T(8,128)(2,1)}, u32[]{:S(2)}) copy-start(bf16[128,8,1024]{2,0,1:T(8,128)(2,1)} %fusion.32) | copy-start | bytes 6291460
  138.3 6.4 %copy-start.31 = (f32[1020]{0:T(1024)S(1)}, f32[1020]{0:T(1024)}, u32[]{:S(2)}) copy-start(f32[1020]{0:T(1024)} %slice.199) | copy-start | bytes 12244
  144.7 18.4 %copy-start = (f32[1024,1024]{0,1:T(8,128)}, f32[1024,1024]{0,1:T(8,128)S(1)}, u32[]{:S(2)}) copy-start(f32[1024,1024]{0,1:T(8,128)S(1)} %multiply_multiply_fusion) | copy-start | bytes 12582916
  148.3 4.9 %copy-start.29 = (f32[1022]{0:T(1024)S(1)}, f32[1022]{0:T(1024)}, u32[]{:S(2)}) copy-start(f32[1022]{0:T(1024)} %slice.203) | copy-start | bytes 12268
  153.2 4.8 %copy-start.28 = (f32[1023]{0:T(1024)S(1)}, f32[1023]{0:T(1024)}, u32[]{:S(2)}) copy-start(f32[1023]{0:T(1024)} %slice.205) | copy-start | bytes 12280
  153.2 10.0 %slice-start = ((s8[8388608]{0:T(1024)(128)(4,1)}), s8[4194304]{0:T(1024)(128)(4,1)S(1)}, s32[]{:S(2)}) async-start(s8[8388608]{0:T(1024)(128)(4,1)} %bitcast.63), calls=%async_computation.5 | async-start | bytes 8388608
  158.0 5.1 %slice-start.1 = ((s8[8388608]{0:T(1024)(128)(4,1)}), s8[4194304]{0:T(1024)(128)(4,1)S(1)}, s32[]{:S(2)}) async-start(s8[8388608]{0:T(1024)(128)(4,1)} %bitcast.63), calls=%async_computation.6 | async-start | bytes 8388608
  191.3 11.3 %copy-start.1 = (f32[1024,1024]{0,1:T(8,128)S(1)}, f32[1024,1024]{0,1:T(8,128)}, u32[]{:S(2)}) copy-start(f32[1024,1024]{0,1:T(8,128)} %copy-done) | copy-start | bytes 12582916
  191.4 11.3 %copy-start.4 = (f32[1020,1024]{0,1:T(8,128)S(1)}, f32[1020,1024]{0,1:T(8,128)}, u32[]{:S(2)}) copy-start(f32[1020,1024]{0,1:T(8,128)} %copy-done.3) | copy-start | bytes 12533764
  191.4 11.3 %copy-start.6 = (f32[1020,1024]{0,1:T(8,128)S(1)}, f32[1020,1024]{0,1:T(8,128)}, u32[]{:S(2)}) copy-start(f32[1020,1024]{0,1:T(8,128)} %copy-done.5) | copy-start | bytes 12533764
  191.4 11.3 %copy-start.7 = (f32[1021,1024]{0,1:T(8,128)S(1)}, f32[1021,1024]{0,1:T(8,128)}, u32[]{:S(2)}) copy-start(f32[1021,1024]{0,1:T(8,128)} %get-tuple-element.55) | copy-start | bytes 12546052
  191.4 12.3 %copy-start.8 = (f32[1021,1024]{0,1:T(8,128)S(1)}, f32[1021,1024]{0,1:T(8,128)}, u32[]{:S(2)}) copy-start(f32[1021,1024]{0,1:T(8,128)} %get-tuple-element.56) | copy-start | bytes 12546052
  191.4 13.7 %copy-start.9 = (f32[1022,1024]{0,1:T(8,128)S(1)}, f32[1022,1024]{0,1:T(8,128)}, u32[]{:S(2)}) copy-start(f32[1022,1024]{0,1:T(8,128)} %get-tuple-element.57) | copy-start | bytes 12558340
  191.4 15.0 %copy-start.10 = (f32[1022,1024]{0,1:T(8,128)S(1)}, f32[1022,1024]{0,1:T(8,128)}, u32[]{:S(2)}) copy-start(f32[1022,1024]{0,1:T(8,128)} %get-tuple-element.58) | copy-start | bytes 12558340
  218.7 1.3 collective-permute-start.2
  220.1 10.8 %collective-permute-start.5 = (f32[10,1024]{1,0:T(8,128)S(1)}, f32[10,1024]{1,0:T(8,128)S(1)}, u32[]{:S(2)}, u32[]{:S(2)}) collective-permute-start(f32[10,1024]{1,0:T(8,128)S(1)} %bitcast.67), channel_id=1, source_target_pairs={{0,6},{1,7},{2,4},{3,5},{4,2},{5,3},{6,0},{7,1},{8,14},{9,15},{10,... | collective-permute-start | bytes 122888 | tf_op jit(solution)/shard_map/ppermute | solution.py:53
  220.2 10.7 %collective-permute-start.4 = (f32[10,1024]{1,0:T(8,128)S(1)}, f32[10,1024]{1,0:T(8,128)S(1)}, u32[]{:S(2)}, u32[]{:S(2)}) collective-permute-start(f32[10,1024]{1,0:T(8,128)S(1)} %bitcast.68), channel_id=1, source_target_pairs={{0,4},{1,5},{2,6},{3,7},{4,0},{5,1},{6,2},{7,3},{8,12},{9,13},{10,... | collective-permute-start | bytes 122888 | tf_op jit(solution)/shard_map/ppermute | solution.py:53
  221.9 8.9 %collective-permute-start.3 = (f32[10,1024]{1,0:T(8,128)S(1)}, f32[10,1024]{1,0:T(8,128)S(1)}, u32[]{:S(2)}, u32[]{:S(2)}) collective-permute-start(f32[10,1024]{1,0:T(8,128)S(1)} %bitcast.69), channel_id=1, source_target_pairs={{0,2},{1,3},{2,0},{3,1},{4,6},{5,7},{6,4},{7,5},{8,10},{9,11},{10,... | collective-permute-start | bytes 122888 | tf_op jit(solution)/shard_map/ppermute | solution.py:53
  230.9 45.6 %collective-permute-start.8 = (f32[10,1024]{1,0:T(8,128)S(1)}, f32[10,1024]{1,0:T(8,128)S(1)}, u32[]{:S(2)}, u32[]{:S(2)}) collective-permute-start(f32[10,1024]{1,0:T(8,128)S(1)} %fusion.76), channel_id=1, source_target_pairs={{0,24},{1,25},{2,26},{3,27},{4,28},{5,29},{6,30},{7,31},{8,16},{9,... | collective-permute-start | bytes 122888 | tf_op jit(solution)/shard_map/ppermute | solution.py:53
  233.9 42.6 %collective-permute-start.7 = (f32[10,1024]{1,0:T(8,128)S(1)}, f32[10,1024]{1,0:T(8,128)S(1)}, u32[]{:S(2)}, u32[]{:S(2)}) collective-permute-start(f32[10,1024]{1,0:T(8,128)S(1)} %fusion.76), channel_id=1, source_target_pairs={{0,16},{1,17},{2,18},{3,19},{4,20},{5,21},{6,22},{7,23},{8,24},{9,... | collective-permute-start | bytes 122888 | tf_op jit(solution)/shard_map/ppermute | solution.py:53
  235.0 41.6 %collective-permute-start.6 = (f32[10,1024]{1,0:T(8,128)S(1)}, f32[10,1024]{1,0:T(8,128)S(1)}, u32[]{:S(2)}, u32[]{:S(2)}) collective-permute-start(f32[10,1024]{1,0:T(8,128)S(1)} %fusion.76), channel_id=1, source_target_pairs={{0,8},{1,9},{2,10},{3,11},{4,12},{5,13},{6,14},{7,15},{8,0},{9,1},... | collective-permute-start | bytes 122888 | tf_op jit(solution)/shard_map/ppermute | solution.py:53
  274.9 10.6 %collective-permute-start = (f32[32,3072]{1,0:T(8,128)S(1)}, f32[32,3072]{1,0:T(8,128)S(1)}, u32[]{:S(2)}, u32[]{:S(2)}) collective-permute-start(f32[32,3072]{1,0:T(8,128)S(1)} %convert_element_type.109), channel_id=1, source_target_pairs={{0,32},{32,0},{64,96},{96,64},{1,33},{33,1},{65,97},{97,65},{2,34}... | collective-permute-start | bytes 1179656 | tf_op jit(solution)/shard_map/ppermute | solution.py:37
  276.6 13.3 %collective-permute-start.11 = (f32[10,1024]{1,0:T(8,128)S(1)}, f32[10,1024]{1,0:T(8,128)S(1)}, u32[]{:S(2)}, u32[]{:S(2)}) collective-permute-start(f32[10,1024]{1,0:T(8,128)S(1)} %fusion.75), channel_id=1, source_target_pairs={{0,96},{32,64},{64,32},{96,0},{1,97},{33,65},{65,33},{97,1},{2,98}... | collective-permute-start | bytes 122888 | tf_op jit(solution)/shard_map/ppermute | solution.py:53
  278.9 11.8 %collective-permute-start.10 = (f32[10,1024]{1,0:T(8,128)S(1)}, f32[10,1024]{1,0:T(8,128)S(1)}, u32[]{:S(2)}, u32[]{:S(2)}) collective-permute-start(f32[10,1024]{1,0:T(8,128)S(1)} %fusion.75), channel_id=1, source_target_pairs={{0,64},{32,96},{64,0},{96,32},{1,65},{33,97},{65,1},{97,33},{2,66}... | collective-permute-start | bytes 122888 | tf_op jit(solution)/shard_map/ppermute | solution.py:53
  279.7 11.1 %collective-permute-start.9 = (f32[10,1024]{1,0:T(8,128)S(1)}, f32[10,1024]{1,0:T(8,128)S(1)}, u32[]{:S(2)}, u32[]{:S(2)}) collective-permute-start(f32[10,1024]{1,0:T(8,128)S(1)} %fusion.75), channel_id=1, source_target_pairs={{0,32},{32,0},{64,96},{96,64},{1,33},{33,1},{65,97},{97,65},{2,34}... | collective-permute-start | bytes 122888 | tf_op jit(solution)/shard_map/ppermute | solution.py:53
  286.5 11.2 %collective-permute-start.1 = (f32[32,3072]{1,0:T(8,128)S(1)}, f32[32,3072]{1,0:T(8,128)S(1)}, u32[]{:S(2)}, u32[]{:S(2)}) collective-permute-start(f32[32,3072]{1,0:T(8,128)S(1)} %convert_add_fusion), channel_id=1, source_target_pairs={{0,64},{32,96},{64,0},{96,32},{1,65},{33,97},{65,1},{97,33},{2,66}... | collective-permute-start | bytes 1179656 | tf_op jit(solution)/shard_map/ppermute | solution.py:37
  (7 other events, 16.5 us)
Sparse Core Ops, SparseCore 0:
  10.2 76.8 all-gather.4
  89.4 42.7 all-gather.2
  191.4 82.5 reduce-scatter.1

commit v4 on v3

--- a/solution.py
+++ b/solution.py
@@ -66,25 +66,36 @@
     rows, width = llm_grad.shape
     blocks_dev = dest_rank.shape[1]
     block_rows = rows // blocks_dev
+    lanes = 128
+    col_tiles = width // lanes
+    body = block_rows * col_tiles
     targets = dest_rank[0]
-    grad_blocks = llm_grad.reshape(blocks_dev, block_rows, width)
+    grad_tiles = (
+        llm_grad.reshape(blocks_dev, block_rows, col_tiles, lanes)
+        .transpose(0, 2, 1, 3)
+        .reshape(blocks_dev, body, lanes)
+    )
     tags = jnp.broadcast_to(
-        (jnp.arange(blocks_dev, dtype=jnp.float32) + 1.0)[:, None, None], (blocks_dev, 1, width)
+        (jnp.arange(blocks_dev, dtype=jnp.float32) + 1.0)[:, None, None], (blocks_dev, 16, lanes)
     ).astype(jnp.bfloat16)
-    tagged = jnp.concatenate([grad_blocks, tags], axis=1)
+    tagged = jnp.concatenate([grad_tiles, tags], axis=1)
     send_sel = (targets[None, :] == jnp.arange(ranks, dtype=jnp.int32)[:, None]).astype(jnp.bfloat16)
     outbox = jnp.einsum(
-        "dj,jrc->drc", send_sel, tagged, preferred_element_type=jnp.float32
+        "dj,jqc->dqc", send_sel, tagged, preferred_element_type=jnp.float32
     ).astype(jnp.bfloat16)
     inbox = lax.all_to_all(outbox, ("dp", "fsdp"), split_axis=0, concat_axis=0, tiled=True)
-    tag_in = inbox[:, block_rows, 0].astype(jnp.float32)
+    tag_in = inbox[:, body, 0].astype(jnp.float32)
     recv_sel = (
         tag_in[None, :] == (jnp.arange(blocks_dev, dtype=jnp.float32) + 1.0)[:, None]
     ).astype(jnp.bfloat16)
     placed = jnp.einsum(
-        "js,src->jrc", recv_sel, inbox[:, :block_rows, :], preferred_element_type=jnp.float32
+        "js,sqc->jqc", recv_sel, inbox[:, :body, :], preferred_element_type=jnp.float32
     ).astype(jnp.bfloat16)
-    return placed.reshape(rows, width)
+    return (
+        placed.reshape(blocks_dev, col_tiles, block_rows, lanes)
+        .transpose(0, 2, 1, 3)
+        .reshape(rows, width)
+    )
 
 
 def on_device(

time: 310 us -> 292 us (0.942)
  waiting for transfers between devices: 103 us -> 85.4 us
    all_to_all x1, waiting for transfers between devices: 50.6 us -> 28.4 us  [route(): lax.all_to_all(outbox, ('dp', 'fsdp'), split_axis=0, concat_axis=0, tiled...]
  transfers between devices with their start and end apart: 16 -> 16, of which waited for: 6 -> 7; matrix products, arithmetic and copies ran while one was open for 32% -> 34% of each run, Pallas kernels for 0% -> 0%
where the time goes in v4:
time: 292 us; the launch traced here: 288 us
  waiting for transfers between devices  85.4 us (29%)
  other arithmetic  75.9 us (26%)
  local copies, waits for them, and re-layouts  44.3 us (15%)
  matrix products  37.4 us (13%)
  starting transfers between devices  29.8 us (10%)
  between operations  14.7 us (5%)
    reduce_scatter x1, waiting for transfers between devices, on_device(): lax.psum_scatter(weight_terms, 'fsdp', scatter_dimension=0, tiled=True)  41.9 us
    all_to_all x1, waiting for transfers between devices, route(): lax.all_to_all(outbox, ('dp', 'fsdp'), split_axis=0, concat_axis=0, tiled...  28.4 us
    mul x4, other arithmetic, on_device(): masked = conv_grad * sames[k]  18.2 us
    slice x8, local copies, waits for them, and re-layouts, shift_rows(): return jnp.concatenate([pad, values[:rows + offset]], axis=0)  16.8 us
    another operation x3, other arithmetic  15.9 us
    ppermute x10, starting transfers between devices, group_sum(): lax.ppermute(x, axis, [(i, i ^ d << shift) for i in range(size)])  12.8 us
    mul x1, other arithmetic, on_device(): conv = conv * keep  12.7 us
    reduce_sum x1, other arithmetic, on_device(): kernel_rows.append(jnp.sum(masked * shift_rows(glu_f, offset, 0.0), axis=0))  12.2 us
  transfers between devices with their start and end apart: 16, of which 7 were waited for; matrix products, arithmetic and copies ran while one was open for 34% of the time, Pallas kernels for 0%

profile of v4, /device:TPU:0, one launch (start us, length us, event | category | flops | bytes accessed | tf_op | source)
XLA Modules:
  0.0 287.5 jit_solution(16903129414494926409)
XLA Ops:
  7.9 2.9 %copy.37 = bf16[128,8,8,128]{3,0,1,2:T(8,128)(2,1)S(1)} copy(bf16[128,8,8,128]{3,1,2,0:T(8,128)(2,1)} %bitcast.76) | data formatting | bytes 4194304 | tf_op jit(solution)/shard_map/reshape | solution.py:74
  11.9 3.2 %copy.38 = bf16[128,80,128]{2,1,0:T(8,128)(2,1)} copy(bf16[128,80,128]{2,0,1:T(8,128)(2,1)S(1)} %fusion.26) | data formatting | bytes 5242880 | tf_op jit(solution)/shard_map/convert_element_type | solution.py:85
  15.1 11.6 %all-to-all-start = ((bf16[128,80,128]{2,1,0:T(8,128)(2,1)}), bf16[128,80,128]{2,1,0:T(8,128)(2,1)}, u32[]{:S(2)}, u32[]{:S(2)}) async-start(bf16[128,80,128]{2,1,0:T(8,128)(2,1)} %copy.38), calls=%async_computation | async-start | bytes 5242880 | tf_op jit(solution)/shard_map/all_to_all | solution.py:86
  27.9 2.9 copy.36
  35.2 28.4 %all-to-all-done = bf16[128,80,128]{2,1,0:T(8,128)(2,1)} async-done(((bf16[128,80,128]{2,1,0:T(8,128)(2,1)}), bf16[128,80,128]{2,1,0:T(8,128)(2,1)}, u32[]{:S(2)}, u32[]{:S(2)}) %all-to-all-start) | async-done | bytes 2621472 | tf_op jit(solution)/shard_map/all_to_all | solution.py:86
  63.6 1.8 slice.187
  65.4 2.0 fusion.43
  67.4 1.7 fusion.29
  69.1 2.7 copy.62
  71.8 7.5 %fusion.38 = f32[1024,2048]{0,1:T(8,128)S(1)} fusion(bf16[1024,2048]{1,0:T(8,128)(2,1)} %all-gather.5.cloned.1.call-done, bf16[1024,1024]{0,1:T(8,128)(2,1)S(1)} %copy.36, f32[1024]{0:T(1024)S(1)} %copy-done.32, f32[1024]{0:T(1024)S(1)} %add_rsqrt_fusion, f32[1024]{0:T(1024)S(1)} %broadcast_multiply_fusion.2), kind=kOutput, calls=%fused_computation.64 | convolution fusion | flops 4300210176 | bytes 14692352 | tf_op jit(solution)/shard_map/dot_general | solution.py:120
  79.3 1.5 fusion.20
  80.9 1.7 fusion.62
  82.5 5.3 %fusion.63 = (f32[1021,1024]{0,1:T(8,128)}, f32[1021,1024]{0,1:T(8,128)}) fusion(f32[1024,1024]{0,1:T(8,128)S(1)} %fusion.20), kind=kLoop, calls=%fused_computation.116 | loop fusion | bytes 16728064 | tf_op jit(solution)/shard_map/slice | solution.py:16
  87.8 4.7 %fusion.64 = (f32[1022,1024]{0,1:T(8,128)}, f32[1022,1024]{0,1:T(8,128)}) fusion(f32[1024,1024]{0,1:T(8,128)S(1)} %fusion.20), kind=kLoop, calls=%fused_computation.117 | loop fusion | bytes 16744448 | tf_op jit(solution)/shard_map/slice | solution.py:16
  92.6 4.9 %fusion.65 = (f32[1023,1024]{0,1:T(8,128)}, f32[1023,1024]{0,1:T(8,128)}) fusion(f32[1024,1024]{0,1:T(8,128)S(1)} %fusion.20), kind=kLoop, calls=%fused_computation.118 | loop fusion | bytes 16760832 | tf_op jit(solution)/shard_map/slice | solution.py:16
  97.5 12.7 %add_multiply_fusion = f32[1024,1024]{0,1:T(8,128)S(1)} fusion(f32[1020,1024]{0,1:T(8,128)S(1)} %get-tuple-element.54, f32[1021,1024]{0,1:T(8,128)} %get-tuple-element.56, f32[1022,1024]{0,1:T(8,128)} %get-tuple-element.58, f32[1023,1024]{0,1:T(8,128)} %get-tuple-element.60, f32[1023,1024]{0,1:T(8,128)} %get-tuple-element.59, ...), kind=kLoop, calls=%fused_computation.44 | loop fusion | flops 33554432 | bytes 46129152 | tf_op jit(solution)/shard_map/mul | solution.py:133
  110.3 2.0 copy-done.14
  112.2 3.7 %fusion.32 = bf16[1024,1024]{1,0:T(8,128)(2,1)} fusion(f32[1024,1024]{0,1:T(8,128)S(1)} %add_multiply_fusion, bf16[128,8,8,128]{3,2,1,0:T(8,128)(2,1)S(1)} %bitcast.77), kind=kOutput, calls=%fused_computation.61 | convolution fusion | flops 2153775104 | bytes 8388608 | tf_op jit(solution)/shard_map/dot_general | solution.py:26
  115.9 1.2 all-gather.3.cloned.1.call-done
  117.1 6.2 %multiply_multiply_fusion = f32[1024,1024]{0,1:T(8,128)S(1)} fusion(f32[1024,1024]{0,1:T(8,128)} %copy-done.14, bf16[1024,1024]{1,0:T(8,128)(2,1)} %all-gather.3.cloned.1.call-done, f32[1024]{0:T(1024)S(1)} %convert_element_type.101, bf16[128,8,8,128]{3,2,1,0:T(8,128)(2,1)S(1)} %bitcast.78), kind=kOutput, calls=%fused_computation.42 | convolution fusion | flops 2156920832 | bytes 12587008 | tf_op jit(solution)/shard_map/dot_general | solution.py:136
  123.3 3.6 %slice_multiply_fusion.7 = (f32[1020,1024]{0,1:T(8,128)S(1)}, f32[1020,1024]{0,1:T(8,128)}) fusion(f32[1024,1024]{0,1:T(8,128)S(1)} %multiply_multiply_fusion, f32[1020]{0:T(1024)S(1)} %copy-done.31, f32[1020]{0:T(1024)S(1)} %bitcast.93), kind=kLoop, calls=%fused_computation.23 | loop fusion | flops 2088960 | bytes 16719840 | tf_op jit(solution)/shard_map/mul | solution.py:141
  126.9 4.9 %slice_multiply_fusion.6 = (f32[1021,1024]{0,1:T(8,128)}, f32[1021,1024]{0,1:T(8,128)}) fusion(f32[1024,1024]{0,1:T(8,128)S(1)} %multiply_multiply_fusion, f32[1021]{0:T(1024)S(1)} %copy-done.30, f32[1021]{0:T(1024)S(1)} %bitcast.94), kind=kLoop, calls=%fused_computation.22 | loop fusion | flops 2091008 | bytes 16736232 | tf_op jit(solution)/shard_map/mul | solution.py:141
  131.8 4.8 %slice_multiply_fusion.5 = (f32[1022,1024]{0,1:T(8,128)}, f32[1022,1024]{0,1:T(8,128)}) fusion(f32[1024,1024]{0,1:T(8,128)S(1)} %multiply_multiply_fusion, f32[1022]{0:T(1024)S(1)} %copy-done.29, f32[1022]{0:T(1024)S(1)} %bitcast.95), kind=kLoop, calls=%fused_computation.21 | loop fusion | flops 2093056 | bytes 16752624 | tf_op jit(solution)/shard_map/mul | solution.py:141
  136.6 4.9 %slice_multiply_fusion.4 = (f32[1023,1024]{0,1:T(8,128)}, f32[1023,1024]{0,1:T(8,128)}) fusion(f32[1024,1024]{0,1:T(8,128)S(1)} %multiply_multiply_fusion, f32[1023]{0:T(1024)S(1)} %copy-done.28, f32[1023]{0:T(1024)S(1)} %bitcast.96), kind=kLoop, calls=%fused_computation.20 | loop fusion | flops 2095104 | bytes 16769016 | tf_op jit(solution)/shard_map/mul | solution.py:141
  141.5 14.0 %multiply_convert_fusion.2 = (bf16[1024,1024]{0,1:T(8,128)(2,1)}, f32[1024,1024]{0,1:T(8,128)S(1)}) fusion(f32[1024,2048]{0,1:T(8,128)S(1)} %bitcast.73, f32[1020,1024]{0,1:T(8,128)} %get-tuple-element.46, f32[1024]{0:T(1024)} %bitcast.112, f32[1021,1024]{0,1:T(8,128)} %get-tuple-element.48, f32[1024]{0:T(1024)} %bitcast.114, ...), kind=kLoop, calls=%fused_computation.40 | loop fusion | flops 23068672 | bytes 48189440 | tf_op jit(solution)/shard_map/convert.3
  155.6 1.7 multiply_convert_fusion.1
  157.8 6.2 %convolution_convert_fusion = bf16[1024,2048]{1,0:T(8,128)(2,1)S(1)} fusion(bf16[1024,1024]{0,1:T(8,128)(2,1)S(1)} %copy-done.12, f32[1024]{0:T(1024)S(1)} %copy-done.33, f32[1024]{0:T(1024)S(1)} %copy-done.27, f32[1024]{0:T(1024)S(1)} %broadcast_multiply_fusion.2, bf16[1024,1024]{0,1:T(8,128)(2,1)S(1)} %multiply_convert_fusion.1, ...), kind=kOutput, calls=%fused_computation.46 | convolution fusion | flops 4310695936 | bytes 10498048 | tf_op jit(solution)/shard_map/dot_general | solution.py:26
  164.1 2.5 pad_maximum_fusion.1
  166.6 3.3 %pad_maximum_fusion = bf16[1024,3072]{1,0:T(8,128)(2,1)} fusion(bf16[1024,1024]{1,0:T(8,128)(2,1)S(1)} %copy-done.16, bf16[1024,2048]{1,0:T(8,128)(2,1)S(1)} %convolution_convert_fusion), kind=kLoop, calls=%fused_computation | loop fusion | flops 12582912 | bytes 12582912 | tf_op jit(solution)/shard_map/concatenate | solution.py:146
  170.0 11.3 %fusion.11 = (f32[1024]{0:T(1024)S(1)}, f32[1024]{0:T(1024)S(1)}, f32[1024]{0:T(1024)S(1)}, f32[1024,1024]{0,1:T(8,128)}) fusion(bf16[1024,1024]{0,1:T(8,128)(2,1)} %copy-done.11, f32[1024]{0:T(1024)S(1)} %copy-done.27, f32[1024]{0:T(1024)S(1)} %broadcast_multiply_fusion.2, f32[1024]{0:T(1024)S(1)} %copy-done.33, ...), kind=kOutput, calls=%fused_computation.14 | convolution fusion | flops 4304401408 | bytes 14704640 | tf_op jit(solution)/shard_map/dot_general | solution.py:159
  181.3 2.0 copy-done.9
  183.3 1.4 copy-done.10
  184.6 12.2 %multiply_reduce_fusion = (f32[1024]{0:T(1024)S(1)}, f32[1024]{0:T(1024)S(1)}, f32[1024]{0:T(1024)S(1)}, f32[1024]{0:T(1024)S(1)}, f32[1024]{0:T(1024)S(1)}, /*i...) fusion(f32[1024,1024]{0,1:T(8,128)S(1)} %copy-done.1, f32[1020,1024]{0,1:T(8,128)S(1)} %copy-done.6, ...), kind=kLoop, calls=%fused_computation.29 | loop fusion | flops 33545216 | bytes 46125056 | tf_op jit(solution)/shard_map/reduce_sum | solution.py:157
  197.2 1.1 collective-permute-done.2
  198.3 2.3 collective-permute-start.5
  202.5 4.3 %fusion.10 = bf16[1024,1024]{0,1:T(8,128)(2,1)S(1)} fusion(bf16[1024,1024]{0,1:T(8,128)(2,1)} %copy-done.11, f32[1024,1024]{0,1:T(8,128)} %get-tuple-element.86, f32[1024]{0:T(1024)S(1)} %get-tuple-element.87, f32[1024]{0:T(1024)S(1)} %get-tuple-element.88, f32[1024]{0:T(1024)S(1)} %copy-done.33, f32[1024]{0:T(1024)S(1)} %copy-done.27, ...), kind=kLoop, calls=%fused_computation.13 | loop fusion | flops 9437184 | bytes 8409088 | tf_op jit(solution)/shard_map/convert_element_type | solution.py:171
  206.7 2.6 copy.44
  209.4 2.4 collective-permute-start.8
  212.6 0.9 collective-permute-start.6
  213.5 41.9 %reduce-scatter.2.cloned.1.call-done = bf16[32,3072]{1,0:T(8,128)(2,1)} async-done(((bf16[1024,3072]{1,0:T(8,128)(2,1)}), bf16[32,3072]{1,0:T(8,128)(2,1)}) %reduce-scatter.2.cloned.1.call-update) | async-done | bytes 196624 | tf_op jit(solution)/shard_map/reduce_scatter | solution.py:152
  255.5 1.0 convert_element_type.104
  256.4 1.6 collective-permute-start
  258.2 2.2 collective-permute-start.11
  261.2 1.1 collective-permute-start.9
  262.4 4.7 %collective-permute-done = f32[32,3072]{1,0:T(8,128)S(1)} collective-permute-done((f32[32,3072]{1,0:T(8,128)S(1)}, f32[32,3072]{1,0:T(8,128)S(1)}, u32[]{:S(2)}, u32[]{:S(2)}) %collective-permute-start) | collective-permute-done | bytes 393248 | tf_op jit(solution)/shard_map/ppermute | solution.py:37
  267.1 1.0 convert_add_fusion
  268.0 3.3 %collective-permute-start.1 = (f32[32,3072]{1,0:T(8,128)S(1)}, f32[32,3072]{1,0:T(8,128)S(1)}, u32[]{:S(2)}, u32[]{:S(2)}) collective-permute-start(f32[32,3072]{1,0:T(8,128)S(1)} %convert_add_fusion), channel_id=1, source_target_pairs={{0,64},{32,96},{64,0},{96,32},{1,65},{33,97},{65,1},{97,33},{2,66}... | collective-permute-start | bytes 1179656 | tf_op jit(solution)/shard_map/ppermute | solution.py:37
  273.5 5.8 %collective-permute-done.1 = f32[32,3072]{1,0:T(8,128)S(1)} collective-permute-done((f32[32,3072]{1,0:T(8,128)S(1)}, f32[32,3072]{1,0:T(8,128)S(1)}, u32[]{:S(2)}, u32[]{:S(2)}) %collective-permute-start.1) | collective-permute-done | bytes 393248 | tf_op jit(solution)/shard_map/ppermute | solution.py:37
  (134 shorter events, 15.3 us)
Async XLA Ops:
  7.2 3.9 %copy-start.35 = (s32[1,128]{1,0:T(1,128)S(1)}, s32[1,128]{1,0:T(1,128)}, u32[]{:S(2)}) copy-start(s32[1,128]{1,0:T(1,128)} %param.11) | copy-start | bytes 1540
  7.2 64.6 %all-gather.5.cloned.1.call-start = ((), (), s32[]{:S(2)}) async-start(), calls=%async_computation.3 | async-start | bytes 4325376 | tf_op jit(solution)/shard_map/all_gather | solution.py:109
  15.1 15.6 %copy-start.34 = (s32[1024]{0:T(1024)S(1)}, s32[1024]{0:T(1024)}, u32[]{:S(2)}) copy-start(s32[1024]{0:T(1024)} %param.13) | copy-start | bytes 12292
  15.1 15.7 %copy-start.36 = (s32[1,4]{1,0:T(1,128)S(1)}, s32[1,4]{1,0:T(1,128)}, u32[]{:S(2)}) copy-start(s32[1,4]{1,0:T(1,128)} %param.12) | copy-start | bytes 52
  15.1 48.5 %all-to-all-start = ((bf16[128,80,128]{2,1,0:T(8,128)(2,1)}), bf16[128,80,128]{2,1,0:T(8,128)(2,1)}, u32[]{:S(2)}, u32[]{:S(2)}) async-start(bf16[128,80,128]{2,1,0:T(8,128)(2,1)} %copy.38), calls=%async_computation | async-start | bytes 5242880 | tf_op jit(solution)/shard_map/all_to_all | solution.py:86
  26.8 90.3 %all-gather.3.cloned.1.call-start = ((), (), s32[]{:S(2)}) async-start(), calls=%async_computation.2 | async-start | bytes 2162688 | tf_op jit(solution)/shard_map/all_gather | solution.py:110
  27.5 7.6 %copy-start.25 = (f32[9,1024]{1,0:T(8,128)S(1)}, f32[9,1024]{1,0:T(8,128)}, u32[]{:S(2)}) copy-start(f32[9,1024]{1,0:T(8,128)} %param.16) | copy-start | bytes 110596
  27.5 227.9 %reduce-scatter.2.cloned.1.call-start = ((), (), s32[]{:S(2)}) async-start(), calls=%async_computation.4 | async-start | bytes 6488064 | tf_op jit(solution)/shard_map/reduce_scatter | solution.py:152
  30.8 41.0 %copy-start.11 = (bf16[1024,1024]{0,1:T(8,128)(2,1)}, bf16[1024,1024]{0,1:T(8,128)(2,1)S(1)}, u32[]{:S(2)}) copy-start(bf16[1024,1024]{0,1:T(8,128)(2,1)S(1)} %copy.36) | copy-start | bytes 6291460
  35.1 36.7 %copy-start.26 = (f32[1024]{0:T(1024)}, f32[1024]{0:T(1024)S(1)}, u32[]{:S(2)}) copy-start(f32[1024]{0:T(1024)S(1)} %add_rsqrt_fusion) | copy-start | bytes 12292
  35.1 62.3 %copy-start.17 = (f32[1,1024]{1,0:T(1,128)}, f32[1,1024]{1,0:T(1,128)S(1)}, u32[]{:S(2)}) copy-start(f32[1,1024]{1,0:T(1,128)S(1)} %get-tuple-element.62) | copy-start | bytes 12292
  35.2 62.3 %copy-start.18 = (f32[1,1024]{1,0:T(1,128)}, f32[1,1024]{1,0:T(1,128)S(1)}, u32[]{:S(2)}) copy-start(f32[1,1024]{1,0:T(1,128)S(1)} %get-tuple-element.63) | copy-start | bytes 12292
  35.2 62.3 %copy-start.19 = (f32[1,1024]{1,0:T(1,128)}, f32[1,1024]{1,0:T(1,128)S(1)}, u32[]{:S(2)}) copy-start(f32[1,1024]{1,0:T(1,128)S(1)} %get-tuple-element.64) | copy-start | bytes 12292
  35.2 62.3 %copy-start.20 = (f32[1,1024]{1,0:T(1,128)}, f32[1,1024]{1,0:T(1,128)S(1)}, u32[]{:S(2)}) copy-start(f32[1,1024]{1,0:T(1,128)S(1)} %get-tuple-element.65) | copy-start | bytes 12292
  35.2 62.3 %copy-start.21 = (f32[1,1024]{1,0:T(1,128)}, f32[1,1024]{1,0:T(1,128)S(1)}, u32[]{:S(2)}) copy-start(f32[1,1024]{1,0:T(1,128)S(1)} %get-tuple-element.66) | copy-start | bytes 12292
  35.2 62.3 %copy-start.22 = (f32[1,1024]{1,0:T(1,128)}, f32[1,1024]{1,0:T(1,128)S(1)}, u32[]{:S(2)}) copy-start(f32[1,1024]{1,0:T(1,128)S(1)} %get-tuple-element.67) | copy-start | bytes 12292
  35.2 62.3 %copy-start.23 = (f32[1,1024]{1,0:T(1,128)}, f32[1,1024]{1,0:T(1,128)S(1)}, u32[]{:S(2)}) copy-start(f32[1,1024]{1,0:T(1,128)S(1)} %get-tuple-element.68) | copy-start | bytes 12292
  35.2 62.3 %copy-start.24 = (f32[1,1024]{1,0:T(1,128)}, f32[1,1024]{1,0:T(1,128)S(1)}, u32[]{:S(2)}) copy-start(f32[1,1024]{1,0:T(1,128)S(1)} %get-tuple-element.69) | copy-start | bytes 12292
  67.4 4.4 %copy-start.32 = (f32[1024]{0:T(1024)S(1)}, f32[1024]{0:T(1024)}, u32[]{:S(2)}) copy-start(f32[1024]{0:T(1024)} %param.14) | copy-start | bytes 12292
  79.3 18.2 %copy-start.2 = (f32[1024,2048]{0,1:T(8,128)}, f32[1024,2048]{0,1:T(8,128)S(1)}, u32[]{:S(2)}) copy-start(f32[1024,2048]{0,1:T(8,128)S(1)} %fusion.38) | copy-start | bytes 25165828
  82.5 15.0 %copy-start.3 = (f32[1020,1024]{0,1:T(8,128)}, f32[1020,1024]{0,1:T(8,128)S(1)}, u32[]{:S(2)}) copy-start(f32[1020,1024]{0,1:T(8,128)S(1)} %get-tuple-element.53) | copy-start | bytes 12533764
  82.5 15.0 %copy-start.5 = (f32[1020,1024]{0,1:T(8,128)}, f32[1020,1024]{0,1:T(8,128)S(1)}, u32[]{:S(2)}) copy-start(f32[1020,1024]{0,1:T(8,128)S(1)} %get-tuple-element.54) | copy-start | bytes 12533764
  97.5 14.7 %copy-start.15 = (bf16[128,8,8,128]{3,1,2,0:T(8,128)(2,1)S(1)}, bf16[128,8,8,128]{3,1,2,0:T(8,128)(2,1)}, u32[]{:S(2)}) copy-start(bf16[128,8,8,128]{3,1,2,0:T(8,128)(2,1)} %copy.62) | copy-start | bytes 6291460
  117.1 6.2 %copy-start.31 = (f32[1020]{0:T(1024)S(1)}, f32[1020]{0:T(1024)}, u32[]{:S(2)}) copy-start(f32[1020]{0:T(1024)} %slice.199) | copy-start | bytes 12244
  123.3 18.2 %copy-start = (f32[1024,1024]{0,1:T(8,128)}, f32[1024,1024]{0,1:T(8,128)S(1)}, u32[]{:S(2)}) copy-start(f32[1024,1024]{0,1:T(8,128)S(1)} %multiply_multiply_fusion) | copy-start | bytes 12582916
  126.9 4.9 %copy-start.29 = (f32[1022]{0:T(1024)S(1)}, f32[1022]{0:T(1024)}, u32[]{:S(2)}) copy-start(f32[1022]{0:T(1024)} %slice.203) | copy-start | bytes 12268
  131.8 4.8 %copy-start.28 = (f32[1023]{0:T(1024)S(1)}, f32[1023]{0:T(1024)}, u32[]{:S(2)}) copy-start(f32[1023]{0:T(1024)} %slice.205) | copy-start | bytes 12280
  131.8 9.8 %slice-start = ((s8[8388608]{0:T(1024)(128)(4,1)}), s8[4194304]{0:T(1024)(128)(4,1)S(1)}, s32[]{:S(2)}) async-start(s8[8388608]{0:T(1024)(128)(4,1)} %bitcast.72), calls=%async_computation.5 | async-start | bytes 8388608
  136.6 4.9 %slice-start.1 = ((s8[8388608]{0:T(1024)(128)(4,1)}), s8[4194304]{0:T(1024)(128)(4,1)S(1)}, s32[]{:S(2)}) async-start(s8[8388608]{0:T(1024)(128)(4,1)} %bitcast.72), calls=%async_computation.6 | async-start | bytes 8388608
  169.9 11.3 %copy-start.1 = (f32[1024,1024]{0,1:T(8,128)S(1)}, f32[1024,1024]{0,1:T(8,128)}, u32[]{:S(2)}) copy-start(f32[1024,1024]{0,1:T(8,128)} %copy-done) | copy-start | bytes 12582916
  169.9 11.3 %copy-start.4 = (f32[1020,1024]{0,1:T(8,128)S(1)}, f32[1020,1024]{0,1:T(8,128)}, u32[]{:S(2)}) copy-start(f32[1020,1024]{0,1:T(8,128)} %copy-done.3) | copy-start | bytes 12533764
  169.9 11.3 %copy-start.6 = (f32[1020,1024]{0,1:T(8,128)S(1)}, f32[1020,1024]{0,1:T(8,128)}, u32[]{:S(2)}) copy-start(f32[1020,1024]{0,1:T(8,128)} %copy-done.5) | copy-start | bytes 12533764
  170.0 11.3 %copy-start.7 = (f32[1021,1024]{0,1:T(8,128)S(1)}, f32[1021,1024]{0,1:T(8,128)}, u32[]{:S(2)}) copy-start(f32[1021,1024]{0,1:T(8,128)} %get-tuple-element.55) | copy-start | bytes 12546052
  170.0 11.3 %copy-start.8 = (f32[1021,1024]{0,1:T(8,128)S(1)}, f32[1021,1024]{0,1:T(8,128)}, u32[]{:S(2)}) copy-start(f32[1021,1024]{0,1:T(8,128)} %get-tuple-element.56) | copy-start | bytes 12546052
  170.0 13.3 %copy-start.9 = (f32[1022,1024]{0,1:T(8,128)S(1)}, f32[1022,1024]{0,1:T(8,128)}, u32[]{:S(2)}) copy-start(f32[1022,1024]{0,1:T(8,128)} %get-tuple-element.57) | copy-start | bytes 12558340
  170.0 14.6 %copy-start.10 = (f32[1022,1024]{0,1:T(8,128)S(1)}, f32[1022,1024]{0,1:T(8,128)}, u32[]{:S(2)}) copy-start(f32[1022,1024]{0,1:T(8,128)} %get-tuple-element.58) | copy-start | bytes 12558340
  196.9 1.4 collective-permute-start.2
  198.3 11.0 %collective-permute-start.5 = (f32[10,1024]{1,0:T(8,128)S(1)}, f32[10,1024]{1,0:T(8,128)S(1)}, u32[]{:S(2)}, u32[]{:S(2)}) collective-permute-start(f32[10,1024]{1,0:T(8,128)S(1)} %bitcast.80), channel_id=1, source_target_pairs={{0,6},{1,7},{2,4},{3,5},{4,2},{5,3},{6,0},{7,1},{8,14},{9,15},{10,... | collective-permute-start | bytes 122888 | tf_op jit(solution)/shard_map/ppermute | solution.py:53
  200.6 8.7 %collective-permute-start.4 = (f32[10,1024]{1,0:T(8,128)S(1)}, f32[10,1024]{1,0:T(8,128)S(1)}, u32[]{:S(2)}, u32[]{:S(2)}) collective-permute-start(f32[10,1024]{1,0:T(8,128)S(1)} %bitcast.81), channel_id=1, source_target_pairs={{0,4},{1,5},{2,6},{3,7},{4,0},{5,1},{6,2},{7,3},{8,12},{9,13},{10,... | collective-permute-start | bytes 122888 | tf_op jit(solution)/shard_map/ppermute | solution.py:53
  201.5 7.8 %collective-permute-start.3 = (f32[10,1024]{1,0:T(8,128)S(1)}, f32[10,1024]{1,0:T(8,128)S(1)}, u32[]{:S(2)}, u32[]{:S(2)}) collective-permute-start(f32[10,1024]{1,0:T(8,128)S(1)} %bitcast.82), channel_id=1, source_target_pairs={{0,2},{1,3},{2,0},{3,1},{4,6},{5,7},{6,4},{7,5},{8,10},{9,11},{10,... | collective-permute-start | bytes 122888 | tf_op jit(solution)/shard_map/ppermute | solution.py:53
  209.4 48.7 %collective-permute-start.8 = (f32[10,1024]{1,0:T(8,128)S(1)}, f32[10,1024]{1,0:T(8,128)S(1)}, u32[]{:S(2)}, u32[]{:S(2)}) collective-permute-start(f32[10,1024]{1,0:T(8,128)S(1)} %fusion.76), channel_id=1, source_target_pairs={{0,24},{1,25},{2,26},{3,27},{4,28},{5,29},{6,30},{7,31},{8,16},{9,... | collective-permute-start | bytes 122888 | tf_op jit(solution)/shard_map/ppermute | solution.py:53
  211.7 46.3 %collective-permute-start.7 = (f32[10,1024]{1,0:T(8,128)S(1)}, f32[10,1024]{1,0:T(8,128)S(1)}, u32[]{:S(2)}, u32[]{:S(2)}) collective-permute-start(f32[10,1024]{1,0:T(8,128)S(1)} %fusion.76), channel_id=1, source_target_pairs={{0,16},{1,17},{2,18},{3,19},{4,20},{5,21},{6,22},{7,23},{8,24},{9,... | collective-permute-start | bytes 122888 | tf_op jit(solution)/shard_map/ppermute | solution.py:53
  212.6 45.5 %collective-permute-start.6 = (f32[10,1024]{1,0:T(8,128)S(1)}, f32[10,1024]{1,0:T(8,128)S(1)}, u32[]{:S(2)}, u32[]{:S(2)}) collective-permute-start(f32[10,1024]{1,0:T(8,128)S(1)} %fusion.76), channel_id=1, source_target_pairs={{0,8},{1,9},{2,10},{3,11},{4,12},{5,13},{6,14},{7,15},{8,0},{9,1},... | collective-permute-start | bytes 122888 | tf_op jit(solution)/shard_map/ppermute | solution.py:53
  256.4 10.7 %collective-permute-start = (f32[32,3072]{1,0:T(8,128)S(1)}, f32[32,3072]{1,0:T(8,128)S(1)}, u32[]{:S(2)}, u32[]{:S(2)}) collective-permute-start(f32[32,3072]{1,0:T(8,128)S(1)} %convert_element_type.104), channel_id=1, source_target_pairs={{0,32},{32,0},{64,96},{96,64},{1,33},{33,1},{65,97},{97,65},{2,34}... | collective-permute-start | bytes 1179656 | tf_op jit(solution)/shard_map/ppermute | solution.py:37
  258.2 13.2 %collective-permute-start.11 = (f32[10,1024]{1,0:T(8,128)S(1)}, f32[10,1024]{1,0:T(8,128)S(1)}, u32[]{:S(2)}, u32[]{:S(2)}) collective-permute-start(f32[10,1024]{1,0:T(8,128)S(1)} %fusion.75), channel_id=1, source_target_pairs={{0,96},{32,64},{64,32},{96,0},{1,97},{33,65},{65,33},{97,1},{2,98}... | collective-permute-start | bytes 122888 | tf_op jit(solution)/shard_map/ppermute | solution.py:53
  260.4 11.8 %collective-permute-start.10 = (f32[10,1024]{1,0:T(8,128)S(1)}, f32[10,1024]{1,0:T(8,128)S(1)}, u32[]{:S(2)}, u32[]{:S(2)}) collective-permute-start(f32[10,1024]{1,0:T(8,128)S(1)} %fusion.75), channel_id=1, source_target_pairs={{0,64},{32,96},{64,0},{96,32},{1,65},{33,97},{65,1},{97,33},{2,66}... | collective-permute-start | bytes 122888 | tf_op jit(solution)/shard_map/ppermute | solution.py:53
  261.2 11.0 %collective-permute-start.9 = (f32[10,1024]{1,0:T(8,128)S(1)}, f32[10,1024]{1,0:T(8,128)S(1)}, u32[]{:S(2)}, u32[]{:S(2)}) collective-permute-start(f32[10,1024]{1,0:T(8,128)S(1)} %fusion.75), channel_id=1, source_target_pairs={{0,32},{32,0},{64,96},{96,64},{1,33},{33,1},{65,97},{97,65},{2,34}... | collective-permute-start | bytes 122888 | tf_op jit(solution)/shard_map/ppermute | solution.py:53
  268.0 11.2 %collective-permute-start.1 = (f32[32,3072]{1,0:T(8,128)S(1)}, f32[32,3072]{1,0:T(8,128)S(1)}, u32[]{:S(2)}, u32[]{:S(2)}) collective-permute-start(f32[32,3072]{1,0:T(8,128)S(1)} %convert_add_fusion), channel_id=1, source_target_pairs={{0,64},{32,96},{64,0},{96,32},{1,65},{33,97},{65,1},{97,33},{2,66}... | collective-permute-start | bytes 1179656 | tf_op jit(solution)/shard_map/ppermute | solution.py:37
  (7 other events, 16.5 us)
Sparse Core Ops, SparseCore 0:
  10.2 61.5 all-gather.4
  74.1 43.0 all-gather.2
  170.0 85.4 reduce-scatter.1

commit v5 on v4

--- a/solution.py
+++ b/solution.py
@@ -138,8 +138,9 @@
     glu_grad = jnp.zeros((rows, width), jnp.float32)
     for k in range(taps):
         offset = k - middle
-        masked = conv_grad * sames[k]
-        glu_grad = glu_grad + kernel[k][None, :] * shift_rows(masked, -offset, 0.0)
+        glu_grad = glu_grad + kernel[k][None, :] * (
+            shift_rows(conv_grad, -offset, 0.0) * sames[taps - 1 - k]
+        )
     value_grad = glu_grad * sig_b
     gate_grad = glu_grad * value * sig_b * (1.0 - sig_b)
     up_out_grad = jnp.concatenate([value_grad, gate_grad], axis=1).astype(jnp.bfloat16)

time: 292 us -> 289 us (0.990)
  other arithmetic: 75.9 us -> 56.9 us
  local copies, waits for them, and re-layouts: 44.3 us -> 57.2 us
    mul x4 -> x0, other arithmetic: 18.2 us -> none  [on_device(): masked = conv_grad * sames[k]]
    slice x4, local copies, waits for them, and re-layouts: 2.65 us -> 15.7 us  [shift_rows(): return jnp.concatenate([values[offset:], pad], axis=0)]
    unnamed x80 -> x50, local copies, waits for them, and re-layouts: 11.3 us -> 11.3 us
where the time goes in v5:
time: 289 us; the launch traced here: 284 us
  waiting for transfers between devices  88.1 us (30%)
  local copies, waits for them, and re-layouts  57.2 us (20%)
  other arithmetic  56.9 us (20%)
  matrix products  37.4 us (13%)
  starting transfers between devices  29.9 us (10%)
  between operations  14.5 us (5%)
    reduce_scatter x1, waiting for transfers between devices, on_device(): lax.psum_scatter(weight_terms, 'fsdp', scatter_dimension=0, tiled=True)  41.9 us
    all_to_all x1, waiting for transfers between devices, route(): lax.all_to_all(outbox, ('dp', 'fsdp'), split_axis=0, concat_axis=0, tiled...  31.2 us
    slice x8, local copies, waits for them, and re-layouts, shift_rows(): return jnp.concatenate([pad, values[:rows + offset]], axis=0)  16.8 us
    slice x4, local copies, waits for them, and re-layouts, shift_rows(): return jnp.concatenate([values[offset:], pad], axis=0)  15.7 us
    another operation x3, other arithmetic  15 us
    ppermute x10, starting transfers between devices, group_sum(): lax.ppermute(x, axis, [(i, i ^ d << shift) for i in range(size)])  12.8 us
    mul x1, other arithmetic, on_device(): conv = conv * keep  12.7 us
    reduce_sum x1, other arithmetic, on_device(): kernel_rows.append(jnp.sum(masked * shift_rows(glu_f, offset, 0.0), axis=0))  12.2 us
  transfers between devices with their start and end apart: 16, of which 7 were waited for; matrix products, arithmetic and copies ran while one was open for 34% of the time, Pallas kernels for 0%

profile of v5, /device:TPU:0, one launch (start us, length us, event | category | flops | bytes accessed | tf_op | source)
XLA Modules:
  0.0 284.0 jit_solution(5866154751341233861)
XLA Ops:
  7.9 2.9 %copy.37 = bf16[128,8,8,128]{3,0,1,2:T(8,128)(2,1)S(1)} copy(bf16[128,8,8,128]{3,1,2,0:T(8,128)(2,1)} %bitcast.72) | data formatting | bytes 4194304 | tf_op jit(solution)/shard_map/reshape | solution.py:74
  11.9 3.2 %copy.38 = bf16[128,80,128]{2,1,0:T(8,128)(2,1)} copy(bf16[128,80,128]{2,0,1:T(8,128)(2,1)S(1)} %fusion.26) | data formatting | bytes 5242880 | tf_op jit(solution)/shard_map/convert_element_type | solution.py:85
  15.1 11.6 %all-to-all-start = ((bf16[128,80,128]{2,1,0:T(8,128)(2,1)}), bf16[128,80,128]{2,1,0:T(8,128)(2,1)}, u32[]{:S(2)}, u32[]{:S(2)}) async-start(bf16[128,80,128]{2,1,0:T(8,128)(2,1)} %copy.38), calls=%async_computation | async-start | bytes 5242880 | tf_op jit(solution)/shard_map/all_to_all | solution.py:86
  27.9 2.9 %copy.36 = bf16[1024,1024]{0,1:T(8,128)(2,1)S(1)} copy(bf16[1024,1024]{1,0:T(8,128)(2,1)} %param.9) | data formatting | bytes 4194304 | tf_op args[0]
  32.4 31.2 %all-to-all-done = bf16[128,80,128]{2,1,0:T(8,128)(2,1)} async-done(((bf16[128,80,128]{2,1,0:T(8,128)(2,1)}), bf16[128,80,128]{2,1,0:T(8,128)(2,1)}, u32[]{:S(2)}, u32[]{:S(2)}) %all-to-all-start) | async-done | bytes 2621472 | tf_op jit(solution)/shard_map/all_to_all | solution.py:86
  63.6 1.8 slice.187
  65.4 2.0 fusion.43
  67.4 1.7 fusion.29
  69.2 2.7 copy.62
  71.9 7.5 %fusion.38 = f32[1024,2048]{0,1:T(8,128)S(1)} fusion(bf16[1024,2048]{1,0:T(8,128)(2,1)} %all-gather.5.cloned.1.call-done, bf16[1024,1024]{0,1:T(8,128)(2,1)S(1)} %copy.36, f32[1024]{0:T(1024)S(1)} %copy-done.18, f32[1024]{0:T(1024)S(1)} %add_rsqrt_fusion, f32[1024]{0:T(1024)S(1)} %broadcast_multiply_fusion.2), kind=kOutput, calls=%fused_computation.56 | convolution fusion | flops 4300210176 | bytes 14692352 | tf_op jit(solution)/shard_map/dot_general | solution.py:120
  79.3 1.5 fusion.20
  80.9 1.7 fusion.66
  82.6 5.2 %fusion.67 = (f32[1021,1024]{0,1:T(8,128)}, f32[1021,1024]{0,1:T(8,128)}) fusion(f32[1024,1024]{0,1:T(8,128)S(1)} %fusion.20), kind=kLoop, calls=%fused_computation.112 | loop fusion | bytes 16728064 | tf_op jit(solution)/shard_map/slice | solution.py:16
  87.8 4.7 %fusion.68 = (f32[1022,1024]{0,1:T(8,128)}, f32[1022,1024]{0,1:T(8,128)}) fusion(f32[1024,1024]{0,1:T(8,128)S(1)} %fusion.20), kind=kLoop, calls=%fused_computation.113 | loop fusion | bytes 16744448 | tf_op jit(solution)/shard_map/slice | solution.py:16
  92.6 4.8 %fusion.69 = (f32[1023,1024]{0,1:T(8,128)}, f32[1023,1024]{0,1:T(8,128)}) fusion(f32[1024,1024]{0,1:T(8,128)S(1)} %fusion.20), kind=kLoop, calls=%fused_computation.114 | loop fusion | bytes 16760832 | tf_op jit(solution)/shard_map/slice | solution.py:16
  97.4 12.7 %add_multiply_fusion = f32[1024,1024]{0,1:T(8,128)S(1)} fusion(f32[1020,1024]{0,1:T(8,128)S(1)} %get-tuple-element.54, f32[1021,1024]{0,1:T(8,128)} %get-tuple-element.56, f32[1022,1024]{0,1:T(8,128)} %get-tuple-element.58, f32[1023,1024]{0,1:T(8,128)} %get-tuple-element.60, f32[1023,1024]{0,1:T(8,128)} %get-tuple-element.59, ...), kind=kLoop, calls=%fused_computation.36 | loop fusion | flops 33554432 | bytes 46129152 | tf_op jit(solution)/shard_map/mul | solution.py:133
  110.1 2.0 copy-done.14
  112.1 3.7 %fusion.32 = bf16[1024,1024]{1,0:T(8,128)(2,1)} fusion(f32[1024,1024]{0,1:T(8,128)S(1)} %add_multiply_fusion, bf16[128,8,8,128]{3,2,1,0:T(8,128)(2,1)S(1)} %bitcast.73), kind=kOutput, calls=%fused_computation.53 | convolution fusion | flops 2153775104 | bytes 8388608 | tf_op jit(solution)/shard_map/dot_general | solution.py:26
  115.8 1.3 all-gather.3.cloned.1.call-done
  117.1 6.2 %multiply_multiply_fusion = f32[1024,1024]{0,1:T(8,128)S(1)} fusion(f32[1024,1024]{0,1:T(8,128)} %copy-done.14, bf16[1024,1024]{1,0:T(8,128)(2,1)} %all-gather.3.cloned.1.call-done, f32[1024]{0:T(1024)S(1)} %convert_element_type.101, bf16[128,8,8,128]{3,2,1,0:T(8,128)(2,1)S(1)} %bitcast.74), kind=kOutput, calls=%fused_computation.34 | convolution fusion | flops 2156920832 | bytes 12587008 | tf_op jit(solution)/shard_map/dot_general | solution.py:136
  123.2 1.7 fusion.62
  124.9 4.7 %fusion.63 = (f32[1021,1024]{0,1:T(8,128)}, f32[1021,1024]{0,1:T(8,128)}) fusion(f32[1024,1024]{0,1:T(8,128)S(1)} %multiply_multiply_fusion), kind=kLoop, calls=%fused_computation.108 | loop fusion | bytes 16728064 | tf_op jit(solution)/shard_map/slice | solution.py:15
  129.6 4.6 %fusion.64 = (f32[1022,1024]{0,1:T(8,128)}, f32[1022,1024]{0,1:T(8,128)}) fusion(f32[1024,1024]{0,1:T(8,128)S(1)} %multiply_multiply_fusion), kind=kLoop, calls=%fused_computation.109 | loop fusion | bytes 16744448 | tf_op jit(solution)/shard_map/slice | solution.py:15
  134.2 4.7 %fusion.65 = (f32[1023,1024]{0,1:T(8,128)}, f32[1023,1024]{0,1:T(8,128)}) fusion(f32[1024,1024]{0,1:T(8,128)S(1)} %multiply_multiply_fusion), kind=kLoop, calls=%fused_computation.110 | loop fusion | bytes 16760832 | tf_op jit(solution)/shard_map/slice | solution.py:15
  139.0 13.2 %multiply_convert_fusion.2 = (bf16[1024,1024]{0,1:T(8,128)(2,1)}, f32[1024,1024]{0,1:T(8,128)S(1)}) fusion(f32[1024,2048]{0,1:T(8,128)S(1)} %bitcast.69, f32[1024]{0:T(1024)S(1)} %get-tuple-element.70, f32[1020,1024]{0,1:T(8,128)S(1)} %get-tuple-element.46, f32[1024]{0:T(1024)S(1)} %bitcast.104, f32[1024]{0:T(1024)S(1)} %get-tuple-element.77, ...), kind=kLoop, calls=%fused_computation.32 | loop fusion | flops 31457280 | bytes 48222208 | tf_op jit(solution)/shard_map/convert.3
  152.1 1.7 multiply_convert_fusion.1
  154.3 6.2 %convolution_convert_fusion = bf16[1024,2048]{1,0:T(8,128)(2,1)S(1)} fusion(bf16[1024,1024]{0,1:T(8,128)(2,1)S(1)} %copy-done.12, f32[1024]{0:T(1024)S(1)} %copy-done.18, f32[1024]{0:T(1024)S(1)} %add_rsqrt_fusion, f32[1024]{0:T(1024)S(1)} %broadcast_multiply_fusion.2, bf16[1024,1024]{0,1:T(8,128)(2,1)S(1)} %multiply_convert_fusion.1, ...), kind=kOutput, calls=%fused_computation.38 | convolution fusion | flops 4310695936 | bytes 10498048 | tf_op jit(solution)/shard_map/dot_general | solution.py:26
  160.6 2.5 pad_maximum_fusion.1
  163.1 3.2 %pad_maximum_fusion = bf16[1024,3072]{1,0:T(8,128)(2,1)} fusion(bf16[1024,1024]{1,0:T(8,128)(2,1)S(1)} %copy-done.16, bf16[1024,2048]{1,0:T(8,128)(2,1)S(1)} %convolution_convert_fusion), kind=kLoop, calls=%fused_computation | loop fusion | flops 12582912 | bytes 12582912 | tf_op jit(solution)/shard_map/concatenate | solution.py:147
  166.5 11.3 %fusion.11 = (f32[1024]{0:T(1024)S(1)}, f32[1024]{0:T(1024)S(1)}, f32[1024]{0:T(1024)S(1)}, f32[1024,1024]{0,1:T(8,128)}) fusion(bf16[1024,1024]{0,1:T(8,128)(2,1)} %copy-done.11, f32[1024]{0:T(1024)S(1)} %add_rsqrt_fusion, f32[1024]{0:T(1024)S(1)} %broadcast_multiply_fusion.2, f32[1024]{0:T(1024)S(1)} %copy-done.18, ...), kind=kOutput, calls=%fused_computation.14 | convolution fusion | flops 4304401408 | bytes 14704640 | tf_op jit(solution)/shard_map/dot_general | solution.py:160
  177.8 2.0 copy-done.9
  179.8 1.4 copy-done.10
  181.1 12.2 %multiply_reduce_fusion = (f32[1024]{0:T(1024)S(1)}, f32[1024]{0:T(1024)S(1)}, f32[1024]{0:T(1024)S(1)}, f32[1024]{0:T(1024)S(1)}, f32[1024]{0:T(1024)S(1)}, /*i...) fusion(f32[1024,1024]{0,1:T(8,128)S(1)} %copy-done.1, f32[1020,1024]{0,1:T(8,128)S(1)} %copy-done.6, ...), kind=kLoop, calls=%fused_computation.21 | loop fusion | flops 33545216 | bytes 46125056 | tf_op jit(solution)/shard_map/reduce_sum | solution.py:158
  193.7 1.1 collective-permute-done.2
  194.8 2.3 collective-permute-start.5
  198.0 1.0 collective-permute-start.3
  199.0 4.3 %fusion.10 = bf16[1024,1024]{0,1:T(8,128)(2,1)S(1)} fusion(bf16[1024,1024]{0,1:T(8,128)(2,1)} %copy-done.11, f32[1024,1024]{0,1:T(8,128)} %get-tuple-element.86, f32[1024]{0:T(1024)S(1)} %get-tuple-element.87, f32[1024]{0:T(1024)S(1)} %get-tuple-element.88, f32[1024]{0:T(1024)S(1)} %copy-done.18, f32[1024]{0:T(1024)S(1)} %add_rsqrt_fusion, ...), kind=kLoop, calls=%fused_computation.13 | loop fusion | flops 9437184 | bytes 8409088 | tf_op jit(solution)/shard_map/convert_element_type | solution.py:172
  203.2 2.6 copy.44
  205.9 2.4 collective-permute-start.8
  210.1 41.9 %reduce-scatter.2.cloned.1.call-done = bf16[32,3072]{1,0:T(8,128)(2,1)} async-done(((bf16[1024,3072]{1,0:T(8,128)(2,1)}), bf16[32,3072]{1,0:T(8,128)(2,1)}) %reduce-scatter.2.cloned.1.call-update) | async-done | bytes 196624 | tf_op jit(solution)/shard_map/reduce_scatter | solution.py:153
  252.0 1.0 convert_element_type.104
  253.0 1.6 collective-permute-start
  254.7 2.2 collective-permute-start.11
  257.7 1.1 collective-permute-start.9
  258.9 4.7 %collective-permute-done = f32[32,3072]{1,0:T(8,128)S(1)} collective-permute-done((f32[32,3072]{1,0:T(8,128)S(1)}, f32[32,3072]{1,0:T(8,128)S(1)}, u32[]{:S(2)}, u32[]{:S(2)}) %collective-permute-start) | collective-permute-done | bytes 393248 | tf_op jit(solution)/shard_map/ppermute | solution.py:37
  263.6 1.0 convert_add_fusion
  264.6 3.4 %collective-permute-start.1 = (f32[32,3072]{1,0:T(8,128)S(1)}, f32[32,3072]{1,0:T(8,128)S(1)}, u32[]{:S(2)}, u32[]{:S(2)}) collective-permute-start(f32[32,3072]{1,0:T(8,128)S(1)} %convert_add_fusion), channel_id=1, source_target_pairs={{0,64},{32,96},{64,0},{96,32},{1,65},{33,97},{65,1},{97,33},{2,66}... | collective-permute-start | bytes 1179656 | tf_op jit(solution)/shard_map/ppermute | solution.py:37
  270.0 5.8 %collective-permute-done.1 = f32[32,3072]{1,0:T(8,128)S(1)} collective-permute-done((f32[32,3072]{1,0:T(8,128)S(1)}, f32[32,3072]{1,0:T(8,128)S(1)}, u32[]{:S(2)}, u32[]{:S(2)}) %collective-permute-start.1) | collective-permute-done | bytes 393248 | tf_op jit(solution)/shard_map/ppermute | solution.py:37
  (100 shorter events, 12.6 us)
Async XLA Ops:
  7.2 3.9 %copy-start.20 = (s32[1,128]{1,0:T(1,128)S(1)}, s32[1,128]{1,0:T(1,128)}, u32[]{:S(2)}) copy-start(s32[1,128]{1,0:T(1,128)} %param.11) | copy-start | bytes 1540
  7.2 64.7 %all-gather.5.cloned.1.call-start = ((), (), s32[]{:S(2)}) async-start(), calls=%async_computation.3 | async-start | bytes 4325376 | tf_op jit(solution)/shard_map/all_gather | solution.py:109
  15.1 15.6 %copy-start.19 = (s32[1024]{0:T(1024)S(1)}, s32[1024]{0:T(1024)}, u32[]{:S(2)}) copy-start(s32[1024]{0:T(1024)} %param.13) | copy-start | bytes 12292
  15.1 15.7 %copy-start.21 = (s32[1,4]{1,0:T(1,128)S(1)}, s32[1,4]{1,0:T(1,128)}, u32[]{:S(2)}) copy-start(s32[1,4]{1,0:T(1,128)} %param.12) | copy-start | bytes 52
  15.1 48.5 %all-to-all-start = ((bf16[128,80,128]{2,1,0:T(8,128)(2,1)}), bf16[128,80,128]{2,1,0:T(8,128)(2,1)}, u32[]{:S(2)}, u32[]{:S(2)}) async-start(bf16[128,80,128]{2,1,0:T(8,128)(2,1)} %copy.38), calls=%async_computation | async-start | bytes 5242880 | tf_op jit(solution)/shard_map/all_to_all | solution.py:86
  26.7 90.3 %all-gather.3.cloned.1.call-start = ((), (), s32[]{:S(2)}) async-start(), calls=%async_computation.2 | async-start | bytes 2162688 | tf_op jit(solution)/shard_map/all_gather | solution.py:110
  27.5 4.9 %copy-start.17 = (f32[9,1024]{1,0:T(8,128)S(1)}, f32[9,1024]{1,0:T(8,128)}, u32[]{:S(2)}) copy-start(f32[9,1024]{1,0:T(8,128)} %param.16) | copy-start | bytes 110596
  27.5 224.5 %reduce-scatter.2.cloned.1.call-start = ((), (), s32[]{:S(2)}) async-start(), calls=%async_computation.4 | async-start | bytes 6488064 | tf_op jit(solution)/shard_map/reduce_scatter | solution.py:153
  30.7 41.1 %copy-start.11 = (bf16[1024,1024]{0,1:T(8,128)(2,1)}, bf16[1024,1024]{0,1:T(8,128)(2,1)S(1)}, u32[]{:S(2)}) copy-start(bf16[1024,1024]{0,1:T(8,128)(2,1)S(1)} %copy.36) | copy-start | bytes 6291460
  67.4 4.5 %copy-start.18 = (f32[1024]{0:T(1024)S(1)}, f32[1024]{0:T(1024)}, u32[]{:S(2)}) copy-start(f32[1024]{0:T(1024)} %param.14) | copy-start | bytes 12292
  79.3 18.1 %copy-start.2 = (f32[1024,2048]{0,1:T(8,128)}, f32[1024,2048]{0,1:T(8,128)S(1)}, u32[]{:S(2)}) copy-start(f32[1024,2048]{0,1:T(8,128)S(1)} %fusion.38) | copy-start | bytes 25165828
  82.6 14.8 %copy-start.3 = (f32[1020,1024]{0,1:T(8,128)}, f32[1020,1024]{0,1:T(8,128)S(1)}, u32[]{:S(2)}) copy-start(f32[1020,1024]{0,1:T(8,128)S(1)} %get-tuple-element.53) | copy-start | bytes 12533764
  82.6 14.8 %copy-start.5 = (f32[1020,1024]{0,1:T(8,128)}, f32[1020,1024]{0,1:T(8,128)S(1)}, u32[]{:S(2)}) copy-start(f32[1020,1024]{0,1:T(8,128)S(1)} %get-tuple-element.54) | copy-start | bytes 12533764
  97.4 14.7 %copy-start.15 = (bf16[128,8,8,128]{3,1,2,0:T(8,128)(2,1)S(1)}, bf16[128,8,8,128]{3,1,2,0:T(8,128)(2,1)}, u32[]{:S(2)}) copy-start(bf16[128,8,8,128]{3,1,2,0:T(8,128)(2,1)} %copy.62) | copy-start | bytes 6291460
  110.1 2.0 copy-start.14
  123.2 15.7 %copy-start = (f32[1024,1024]{0,1:T(8,128)}, f32[1024,1024]{0,1:T(8,128)S(1)}, u32[]{:S(2)}) copy-start(f32[1024,1024]{0,1:T(8,128)S(1)} %multiply_multiply_fusion) | copy-start | bytes 12582916
  129.6 9.4 %slice-start = ((s8[8388608]{0:T(1024)(128)(4,1)}), s8[4194304]{0:T(1024)(128)(4,1)S(1)}, s32[]{:S(2)}) async-start(s8[8388608]{0:T(1024)(128)(4,1)} %bitcast.68), calls=%async_computation.5 | async-start | bytes 8388608
  134.2 4.7 %slice-start.1 = ((s8[8388608]{0:T(1024)(128)(4,1)}), s8[4194304]{0:T(1024)(128)(4,1)S(1)}, s32[]{:S(2)}) async-start(s8[8388608]{0:T(1024)(128)(4,1)} %bitcast.68), calls=%async_computation.6 | async-start | bytes 8388608
  152.1 1.7 copy-start.12
  152.1 2.2 copy-start.13
  160.6 2.5 copy-start.16
  166.4 11.3 %copy-start.1 = (f32[1024,1024]{0,1:T(8,128)S(1)}, f32[1024,1024]{0,1:T(8,128)}, u32[]{:S(2)}) copy-start(f32[1024,1024]{0,1:T(8,128)} %copy-done) | copy-start | bytes 12582916
  166.5 11.3 %copy-start.4 = (f32[1020,1024]{0,1:T(8,128)S(1)}, f32[1020,1024]{0,1:T(8,128)}, u32[]{:S(2)}) copy-start(f32[1020,1024]{0,1:T(8,128)} %copy-done.3) | copy-start | bytes 12533764
  166.5 11.3 %copy-start.6 = (f32[1020,1024]{0,1:T(8,128)S(1)}, f32[1020,1024]{0,1:T(8,128)}, u32[]{:S(2)}) copy-start(f32[1020,1024]{0,1:T(8,128)} %copy-done.5) | copy-start | bytes 12533764
  166.5 11.3 %copy-start.7 = (f32[1021,1024]{0,1:T(8,128)S(1)}, f32[1021,1024]{0,1:T(8,128)}, u32[]{:S(2)}) copy-start(f32[1021,1024]{0,1:T(8,128)} %get-tuple-element.55) | copy-start | bytes 12546052
  166.5 11.3 %copy-start.8 = (f32[1021,1024]{0,1:T(8,128)S(1)}, f32[1021,1024]{0,1:T(8,128)}, u32[]{:S(2)}) copy-start(f32[1021,1024]{0,1:T(8,128)} %get-tuple-element.56) | copy-start | bytes 12546052
  166.5 13.3 %copy-start.9 = (f32[1022,1024]{0,1:T(8,128)S(1)}, f32[1022,1024]{0,1:T(8,128)}, u32[]{:S(2)}) copy-start(f32[1022,1024]{0,1:T(8,128)} %get-tuple-element.57) | copy-start | bytes 12558340
  166.5 14.6 %copy-start.10 = (f32[1022,1024]{0,1:T(8,128)S(1)}, f32[1022,1024]{0,1:T(8,128)}, u32[]{:S(2)}) copy-start(f32[1022,1024]{0,1:T(8,128)} %get-tuple-element.58) | copy-start | bytes 12558340
  193.4 1.4 collective-permute-start.2
  194.8 11.0 %collective-permute-start.5 = (f32[10,1024]{1,0:T(8,128)S(1)}, f32[10,1024]{1,0:T(8,128)S(1)}, u32[]{:S(2)}, u32[]{:S(2)}) collective-permute-start(f32[10,1024]{1,0:T(8,128)S(1)} %bitcast.76), channel_id=1, source_target_pairs={{0,6},{1,7},{2,4},{3,5},{4,2},{5,3},{6,0},{7,1},{8,14},{9,15},{10,... | collective-permute-start | bytes 122888 | tf_op jit(solution)/shard_map/ppermute | solution.py:53
  197.1 8.7 %collective-permute-start.4 = (f32[10,1024]{1,0:T(8,128)S(1)}, f32[10,1024]{1,0:T(8,128)S(1)}, u32[]{:S(2)}, u32[]{:S(2)}) collective-permute-start(f32[10,1024]{1,0:T(8,128)S(1)} %bitcast.77), channel_id=1, source_target_pairs={{0,4},{1,5},{2,6},{3,7},{4,0},{5,1},{6,2},{7,3},{8,12},{9,13},{10,... | collective-permute-start | bytes 122888 | tf_op jit(solution)/shard_map/ppermute | solution.py:53
  198.0 7.8 %collective-permute-start.3 = (f32[10,1024]{1,0:T(8,128)S(1)}, f32[10,1024]{1,0:T(8,128)S(1)}, u32[]{:S(2)}, u32[]{:S(2)}) collective-permute-start(f32[10,1024]{1,0:T(8,128)S(1)} %bitcast.78), channel_id=1, source_target_pairs={{0,2},{1,3},{2,0},{3,1},{4,6},{5,7},{6,4},{7,5},{8,10},{9,11},{10,... | collective-permute-start | bytes 122888 | tf_op jit(solution)/shard_map/ppermute | solution.py:53
  205.9 48.7 %collective-permute-start.8 = (f32[10,1024]{1,0:T(8,128)S(1)}, f32[10,1024]{1,0:T(8,128)S(1)}, u32[]{:S(2)}, u32[]{:S(2)}) collective-permute-start(f32[10,1024]{1,0:T(8,128)S(1)} %fusion.80), channel_id=1, source_target_pairs={{0,24},{1,25},{2,26},{3,27},{4,28},{5,29},{6,30},{7,31},{8,16},{9,... | collective-permute-start | bytes 122888 | tf_op jit(solution)/shard_map/ppermute | solution.py:53
  208.3 46.4 %collective-permute-start.7 = (f32[10,1024]{1,0:T(8,128)S(1)}, f32[10,1024]{1,0:T(8,128)S(1)}, u32[]{:S(2)}, u32[]{:S(2)}) collective-permute-start(f32[10,1024]{1,0:T(8,128)S(1)} %fusion.80), channel_id=1, source_target_pairs={{0,16},{1,17},{2,18},{3,19},{4,20},{5,21},{6,22},{7,23},{8,24},{9,... | collective-permute-start | bytes 122888 | tf_op jit(solution)/shard_map/ppermute | solution.py:53
  209.1 45.5 %collective-permute-start.6 = (f32[10,1024]{1,0:T(8,128)S(1)}, f32[10,1024]{1,0:T(8,128)S(1)}, u32[]{:S(2)}, u32[]{:S(2)}) collective-permute-start(f32[10,1024]{1,0:T(8,128)S(1)} %fusion.80), channel_id=1, source_target_pairs={{0,8},{1,9},{2,10},{3,11},{4,12},{5,13},{6,14},{7,15},{8,0},{9,1},... | collective-permute-start | bytes 122888 | tf_op jit(solution)/shard_map/ppermute | solution.py:53
  253.0 10.6 %collective-permute-start = (f32[32,3072]{1,0:T(8,128)S(1)}, f32[32,3072]{1,0:T(8,128)S(1)}, u32[]{:S(2)}, u32[]{:S(2)}) collective-permute-start(f32[32,3072]{1,0:T(8,128)S(1)} %convert_element_type.104), channel_id=1, source_target_pairs={{0,32},{32,0},{64,96},{96,64},{1,33},{33,1},{65,97},{97,65},{2,34}... | collective-permute-start | bytes 1179656 | tf_op jit(solution)/shard_map/ppermute | solution.py:37
  254.7 13.2 %collective-permute-start.11 = (f32[10,1024]{1,0:T(8,128)S(1)}, f32[10,1024]{1,0:T(8,128)S(1)}, u32[]{:S(2)}, u32[]{:S(2)}) collective-permute-start(f32[10,1024]{1,0:T(8,128)S(1)} %fusion.79), channel_id=1, source_target_pairs={{0,96},{32,64},{64,32},{96,0},{1,97},{33,65},{65,33},{97,1},{2,98}... | collective-permute-start | bytes 122888 | tf_op jit(solution)/shard_map/ppermute | solution.py:53
  256.9 11.8 %collective-permute-start.10 = (f32[10,1024]{1,0:T(8,128)S(1)}, f32[10,1024]{1,0:T(8,128)S(1)}, u32[]{:S(2)}, u32[]{:S(2)}) collective-permute-start(f32[10,1024]{1,0:T(8,128)S(1)} %fusion.79), channel_id=1, source_target_pairs={{0,64},{32,96},{64,0},{96,32},{1,65},{33,97},{65,1},{97,33},{2,66}... | collective-permute-start | bytes 122888 | tf_op jit(solution)/shard_map/ppermute | solution.py:53
  257.7 11.0 %collective-permute-start.9 = (f32[10,1024]{1,0:T(8,128)S(1)}, f32[10,1024]{1,0:T(8,128)S(1)}, u32[]{:S(2)}, u32[]{:S(2)}) collective-permute-start(f32[10,1024]{1,0:T(8,128)S(1)} %fusion.79), channel_id=1, source_target_pairs={{0,32},{32,0},{64,96},{96,64},{1,33},{33,1},{65,97},{97,65},{2,34}... | collective-permute-start | bytes 122888 | tf_op jit(solution)/shard_map/ppermute | solution.py:53
  264.6 11.2 %collective-permute-start.1 = (f32[32,3072]{1,0:T(8,128)S(1)}, f32[32,3072]{1,0:T(8,128)S(1)}, u32[]{:S(2)}, u32[]{:S(2)}) collective-permute-start(f32[32,3072]{1,0:T(8,128)S(1)} %convert_add_fusion), channel_id=1, source_target_pairs={{0,64},{32,96},{64,0},{96,32},{1,65},{33,97},{65,1},{97,33},{2,66}... | collective-permute-start | bytes 1179656 | tf_op jit(solution)/shard_map/ppermute | solution.py:37
Sparse Core Ops, SparseCore 0:
  10.2 61.5 all-gather.4
  74.1 42.9 all-gather.2
  166.5 85.4 reduce-scatter.1

commit v6 on v5

--- a/solution.py
+++ b/solution.py
@@ -133,16 +133,17 @@
     conv = conv * keep
     sig_c = jax.nn.sigmoid(conv)
     act = (conv * sig_c).astype(jnp.bfloat16)
+    conv_kept, sig_c_kept, value_kept, sig_b_kept = lax.optimization_barrier((conv, sig_c, value, sig_b))
     act_grad = jnp.dot(out_grad, down_full.T, preferred_element_type=jnp.float32)
-    conv_grad = act_grad * sig_c * (1.0 + conv * (1.0 - sig_c)) * keep
+    conv_grad = act_grad * sig_c_kept * (1.0 + conv_kept * (1.0 - sig_c_kept)) * keep
     glu_grad = jnp.zeros((rows, width), jnp.float32)
     for k in range(taps):
         offset = k - middle
         glu_grad = glu_grad + kernel[k][None, :] * (
             shift_rows(conv_grad, -offset, 0.0) * sames[taps - 1 - k]
         )
-    value_grad = glu_grad * sig_b
-    gate_grad = glu_grad * value * sig_b * (1.0 - sig_b)
+    value_grad = glu_grad * sig_b_kept
+    gate_grad = glu_grad * value_kept * sig_b_kept * (1.0 - sig_b_kept)
     up_out_grad = jnp.concatenate([value_grad, gate_grad], axis=1).astype(jnp.bfloat16)
     weight_terms = jnp.concatenate(
         [contract_rows(hidden, up_out_grad), contract_rows(act, out_grad)], axis=1

time: 289 us -> 303 us (1.048)
  other arithmetic: 56.9 us -> 75.1 us
  waiting for transfers between devices: 88.1 us -> 84.5 us
  local copies, waits for them, and re-layouts: 57.2 us -> 53.8 us
  matrix products: 37.4 us -> 40.6 us
    div x0 -> x2, other arithmetic: none -> 24.1 us  [on_device(): sig_b = jax.nn.sigmoid(up[:, width:])]
    mul x1 -> x0, other arithmetic: 12.7 us -> none  [on_device(): conv = conv * keep]
    reduce_sum x1, other arithmetic: 12.2 us -> 18.2 us  [on_device(): kernel_rows.append(jnp.sum(masked * shift_rows(glu_f, offset, 0.0), axis=0))]
    unnamed x50 -> x64, local copies, waits for them, and re-layouts: 11.3 us -> 7.38 us
  transfers between devices with their start and end apart: 16 -> 16, of which waited for: 7 -> 6; matrix products, arithmetic and copies ran while one was open for 34% -> 38% of each run, Pallas kernels for 0% -> 0%
where the time goes in v6:
time: 303 us; the launch traced here: 298 us
  waiting for transfers between devices  84.5 us (28%)
  other arithmetic  75.1 us (25%)
  local copies, waits for them, and re-layouts  53.8 us (18%)
  matrix products  40.6 us (13%)
  starting transfers between devices  29.8 us (10%)
  between operations  14.6 us (5%)
    reduce_scatter x1, waiting for transfers between devices, on_device(): lax.psum_scatter(weight_terms, 'fsdp', scatter_dimension=0, tiled=True)  39.5 us
    all_to_all x1, waiting for transfers between devices, route(): lax.all_to_all(outbox, ('dp', 'fsdp'), split_axis=0, concat_axis=0, tiled...  31.1 us
    div x2, other arithmetic, on_device(): sig_b = jax.nn.sigmoid(up[:, width:])  24.1 us
    reduce_sum x1, other arithmetic, on_device(): kernel_rows.append(jnp.sum(masked * shift_rows(glu_f, offset, 0.0), axis=0))  18.2 us
    slice x4, local copies, waits for them, and re-layouts, shift_rows(): return jnp.concatenate([values[offset:], pad], axis=0)  17.5 us
    another operation x3, other arithmetic  16.9 us
    slice x8, local copies, waits for them, and re-layouts, shift_rows(): return jnp.concatenate([pad, values[:rows + offset]], axis=0)  15.4 us
    ppermute x10, starting transfers between devices, group_sum(): lax.ppermute(x, axis, [(i, i ^ d << shift) for i in range(size)])  12.7 us
  transfers between devices with their start and end apart: 16, of which 6 were waited for; matrix products, arithmetic and copies ran while one was open for 38% of the time, Pallas kernels for 0%

profile of v6, /device:TPU:0, one launch (start us, length us, event | category | flops | bytes accessed | tf_op | source)
XLA Modules:
  0.0 298.4 jit_solution(1077070184224487655)
XLA Ops:
  7.9 2.9 copy.37
  11.1 0.8 fusion.26
  11.9 3.2 %copy.38 = bf16[128,80,128]{2,1,0:T(8,128)(2,1)} copy(bf16[128,80,128]{2,0,1:T(8,128)(2,1)S(1)} %fusion.26) | data formatting | bytes 5242880 | tf_op jit(solution)/shard_map/convert_element_type | solution.py:85
  15.1 11.6 %all-to-all-start = ((bf16[128,80,128]{2,1,0:T(8,128)(2,1)}), bf16[128,80,128]{2,1,0:T(8,128)(2,1)}, u32[]{:S(2)}, u32[]{:S(2)}) async-start(bf16[128,80,128]{2,1,0:T(8,128)(2,1)} %copy.38), calls=%async_computation | async-start | bytes 5242880 | tf_op jit(solution)/shard_map/all_to_all | solution.py:86
  27.9 2.9 copy.36
  32.5 31.1 %all-to-all-done = bf16[128,80,128]{2,1,0:T(8,128)(2,1)} async-done(((bf16[128,80,128]{2,1,0:T(8,128)(2,1)}), bf16[128,80,128]{2,1,0:T(8,128)(2,1)}, u32[]{:S(2)}, u32[]{:S(2)}) %all-to-all-start) | async-done | bytes 2621472 | tf_op jit(solution)/shard_map/all_to_all | solution.py:86
  63.6 1.8 slice.187
  65.4 2.0 fusion.43
  67.4 1.7 fusion.29
  69.2 2.7 copy.62
  71.8 9.8 %fusion.38 = f32[1024,2048]{0,1:T(8,128)} fusion(bf16[1024,2048]{1,0:T(8,128)(2,1)} %all-gather.5.cloned.1.call-done, bf16[1024,1024]{0,1:T(8,128)(2,1)S(1)} %copy.36, f32[1024]{0:T(1024)S(1)} %copy-done.26, f32[1024]{0:T(1024)S(1)} %add_rsqrt_fusion, f32[1024]{0:T(1024)S(1)} %broadcast_multiply_fusion.2), kind=kOutput, calls=%fused_computation.56 | convolution fusion | flops 4300210176 | bytes 14692352 | tf_op jit(solution)/shard_map/dot_general | solution.py:120
  81.7 9.0 %fusion.15 = (f32[1024,1024]{0,1:T(8,128)}, f32[1024,1024]{0,1:T(8,128)S(1)}, f32[1024,1024]{0,1:T(8,128)}) fusion(f32[1024,2048]{0,1:T(8,128)} %fusion.38), kind=kLoop, calls=%fused_computation.19 | loop fusion | flops 6291456 | bytes 20971520 | tf_op jit(solution)/shard_map/div | solution.py:122
  90.7 1.6 fusion.65
  92.3 4.2 %fusion.66 = (f32[1021,1024]{0,1:T(8,128)S(1)}, f32[1021,1024]{0,1:T(8,128)}) fusion(f32[1024,1024]{0,1:T(8,128)S(1)} %get-tuple-element.56), kind=kLoop, calls=%fused_computation.111 | loop fusion | bytes 16728064 | tf_op jit(solution)/shard_map/slice | solution.py:16
  96.4 4.6 %fusion.67 = (f32[1022,1024]{0,1:T(8,128)}, f32[1022,1024]{0,1:T(8,128)}) fusion(f32[1024,1024]{0,1:T(8,128)S(1)} %get-tuple-element.56), kind=kLoop, calls=%fused_computation.112 | loop fusion | bytes 16744448 | tf_op jit(solution)/shard_map/slice | solution.py:16
  101.1 4.8 %fusion.68 = (f32[1023,1024]{0,1:T(8,128)}, f32[1023,1024]{0,1:T(8,128)}) fusion(f32[1024,1024]{0,1:T(8,128)S(1)} %get-tuple-element.56), kind=kLoop, calls=%fused_computation.113 | loop fusion | bytes 16760832 | tf_op jit(solution)/shard_map/slice | solution.py:16
  105.9 15.1 %add_divide_fusion = (f32[1024,1024]{0,1:T(8,128)}, f32[1024,1024]{0,1:T(8,128)}) fusion(f32[1024]{0:T(1024)S(1)} %convert_element_type.101, f32[1024]{0:T(1024)S(1)} %get-tuple-element.84, f32[1020,1024]{0,1:T(8,128)S(1)} %get-tuple-element.67, f32[1024]{0:T(1024)S(1)} %bitcast.101, f32[1024]{0:T(1024)S(1)} %get-tuple-element.85, ...), kind=kLoop, calls=%fused_computation.35 | loop fusion | flops 30408704 | bytes 46129152 | tf_op jit(solution)/shard_map/div | solution.py:122
  121.1 6.1 %fusion.32 = bf16[1024,1024]{1,0:T(8,128)(2,1)} fusion(f32[1024,1024]{0,1:T(8,128)} %get-tuple-element.13, bf16[128,8,8,128]{3,2,1,0:T(8,128)(2,1)S(1)} %bitcast.71), kind=kOutput, calls=%fused_computation.53 | convolution fusion | flops 2153775104 | bytes 8388608 | tf_op jit(solution)/shard_map/dot_general | solution.py:26
  127.1 6.7 %multiply_multiply_fusion = f32[1024,1024]{0,1:T(8,128)S(1)} fusion(f32[1024,1024]{0,1:T(8,128)} %get-tuple-element.13, f32[1024,1024]{0,1:T(8,128)} %get-tuple-element.12, bf16[1024,1024]{1,0:T(8,128)(2,1)} %all-gather.3.cloned.1.call-done, f32[1024]{0:T(1024)S(1)} %convert_element_type.101, bf16[128,8,8,128]{3,2,1,0:T(8,128)(2,1)S(1)} %bitcast.72), kind=kOutput, calls=%fused_computation.34 | convolution fusion | flops 2153775104 | bytes 16781312 | tf_op jit(solution)/shard_map/dot_general | solution.py:137
  133.8 3.4 %fusion.61 = (f32[1020,1024]{0,1:T(8,128)S(1)}, f32[1020,1024]{0,1:T(8,128)}) fusion(f32[1024,1024]{0,1:T(8,128)S(1)} %multiply_multiply_fusion), kind=kLoop, calls=%fused_computation.106 | loop fusion | bytes 16711680 | tf_op jit(solution)/shard_map/slice | solution.py:15
  137.2 4.7 %fusion.62 = (f32[1021,1024]{0,1:T(8,128)}, f32[1021,1024]{0,1:T(8,128)}) fusion(f32[1024,1024]{0,1:T(8,128)S(1)} %multiply_multiply_fusion), kind=kLoop, calls=%fused_computation.107 | loop fusion | bytes 16728064 | tf_op jit(solution)/shard_map/slice | solution.py:15
  141.9 4.6 %fusion.63 = (f32[1022,1024]{0,1:T(8,128)}, f32[1022,1024]{0,1:T(8,128)}) fusion(f32[1024,1024]{0,1:T(8,128)S(1)} %multiply_multiply_fusion), kind=kLoop, calls=%fused_computation.108 | loop fusion | bytes 16744448 | tf_op jit(solution)/shard_map/slice | solution.py:15
  146.5 4.7 %fusion.64 = (f32[1023,1024]{0,1:T(8,128)}, f32[1023,1024]{0,1:T(8,128)}) fusion(f32[1024,1024]{0,1:T(8,128)S(1)} %multiply_multiply_fusion), kind=kLoop, calls=%fused_computation.109 | loop fusion | bytes 16760832 | tf_op jit(solution)/shard_map/slice | solution.py:15
  151.3 15.0 %multiply_convert_fusion.2 = (bf16[1024,1024]{0,1:T(8,128)(2,1)}, f32[1024,1024]{0,1:T(8,128)S(1)}) fusion(f32[1024,1024]{0,1:T(8,128)S(1)} %copy-done.2, f32[1024]{0:T(1024)S(1)} %get-tuple-element.83, f32[1020,1024]{0,1:T(8,128)} %get-tuple-element.59, f32[1024]{0:T(1024)} %bitcast.102, f32[1024]{0:T(1024)S(1)} %get-tuple-element.90, ...), kind=kLoop, calls=%fused_computation.32 | loop fusion | flops 28311552 | bytes 48222208 | tf_op jit(solution)/shard_map/convert.3
  166.4 1.7 multiply_convert_fusion.1
  168.5 6.3 %convolution_convert_fusion = bf16[1024,2048]{1,0:T(8,128)(2,1)S(1)} fusion(bf16[1024,1024]{0,1:T(8,128)(2,1)S(1)} %copy-done.7, f32[1024]{0:T(1024)S(1)} %copy-done.27, f32[1024]{0:T(1024)S(1)} %copy-done.25, f32[1024]{0:T(1024)S(1)} %copy-done.22, bf16[1024,1024]{0,1:T(8,128)(2,1)S(1)} %multiply_convert_fusion.1, bf16[1024,1024]{0,1:T(8,128)(2,1)S(1)} %copy-done.9), kind=kOutput, calls=%fused_computation.38 | convolution fusion | flops 4310695936 | bytes 10498048 | tf_op jit(solution)/shard_map/dot_general | solution.py:26
  174.8 2.5 pad_maximum_fusion.1
  177.3 3.2 %pad_maximum_fusion = bf16[1024,3072]{1,0:T(8,128)(2,1)} fusion(bf16[1024,1024]{1,0:T(8,128)(2,1)S(1)} %copy-done.13, bf16[1024,2048]{1,0:T(8,128)(2,1)S(1)} %convolution_convert_fusion), kind=kLoop, calls=%fused_computation | loop fusion | flops 12582912 | bytes 12582912 | tf_op jit(solution)/shard_map/concatenate | solution.py:148
  180.7 18.2 %multiply_reduce_fusion = (f32[1024]{0:T(1024)S(1)}, f32[1024]{0:T(1024)S(1)}, f32[1024]{0:T(1024)S(1)}, f32[1024]{0:T(1024)S(1)}, f32[1024]{0:T(1024)S(1)}, /*i...) fusion(f32[1024,1024]{0,1:T(8,128)} %copy-done.1, f32[1020,1024]{0,1:T(8,128)} %copy-done.4, ...), kind=kLoop, calls=%fused_computation.21 | loop fusion | flops 27253760 | bytes 41930752 | tf_op jit(solution)/shard_map/reduce_sum | solution.py:159
  198.9 9.2 %fusion.11 = (f32[1024]{0:T(1024)S(1)}, f32[1024]{0:T(1024)S(1)}, f32[1024]{0:T(1024)S(1)}, f32[1024,1024]{0,1:T(8,128)}) fusion(bf16[1024,1024]{0,1:T(8,128)(2,1)S(1)} %copy-done.7, f32[1024]{0:T(1024)S(1)} %copy-done.25, f32[1024]{0:T(1024)S(1)} %copy-done.22, f32[1024]{0:T(1024)S(1)} %copy-done.27, bf16[1024,2048]{1,0:T(8,128)(2,1)} %all-gather.5.cloned.1.call-done, ...), kind=kOutput, calls=%fused_computation.14 | convolution fusion | flops 4304401408 | bytes 14704640 | tf_op jit(solution)/shard_map/dot_general | solution.py:161
  208.4 1.2 collective-permute-done.2
  209.6 2.1 collective-permute-start.5
  211.7 0.9 collective-permute-start.4
  212.6 1.2 collective-permute-start.3
  213.8 4.9 %fusion.10 = bf16[1024,1024]{0,1:T(8,128)(2,1)} fusion(bf16[1024,1024]{0,1:T(8,128)(2,1)S(1)} %copy-done.7, f32[1024,1024]{0,1:T(8,128)} %get-tuple-element.99, f32[1024]{0:T(1024)S(1)} %get-tuple-element.100, f32[1024]{0:T(1024)S(1)} %get-tuple-element.101, f32[1024]{0:T(1024)S(1)} %copy-done.27, f32[1024]{0:T(1024)S(1)} %copy-done.25, f32[1024]{0:T(1024)S(1)} %copy-done.22), kind=kLoop, calls=%fused_computation.13 | loop fusion | flops 9437184 | bytes 8409088 | tf_op jit(solution)/shard_map/convert_element_type | solution.py:173
  218.7 3.9 %copy.44 = bf16[1024,1024]{1,0:T(8,128)(2,1)} copy(bf16[1024,1024]{0,1:T(8,128)(2,1)} %fusion.10) | data formatting | bytes 4194304
  222.7 2.1 collective-permute-start.8
  224.8 0.9 collective-permute-start.7
  225.7 1.2 collective-permute-start.6
  226.8 39.5 %reduce-scatter.2.cloned.1.call-done = bf16[32,3072]{1,0:T(8,128)(2,1)} async-done(((bf16[1024,3072]{1,0:T(8,128)(2,1)}), bf16[32,3072]{1,0:T(8,128)(2,1)}) %reduce-scatter.2.cloned.1.call-update) | async-done | bytes 196624 | tf_op jit(solution)/shard_map/reduce_scatter | solution.py:154
  266.4 1.0 convert_element_type.104
  267.3 1.7 collective-permute-start
  269.1 2.2 collective-permute-start.11
  272.1 1.1 collective-permute-start.9
  273.3 4.7 %collective-permute-done = f32[32,3072]{1,0:T(8,128)S(1)} collective-permute-done((f32[32,3072]{1,0:T(8,128)S(1)}, f32[32,3072]{1,0:T(8,128)S(1)}, u32[]{:S(2)}, u32[]{:S(2)}) %collective-permute-start) | collective-permute-done | bytes 393248 | tf_op jit(solution)/shard_map/ppermute | solution.py:37
  278.0 1.0 convert_add_fusion
  278.9 3.3 %collective-permute-start.1 = (f32[32,3072]{1,0:T(8,128)S(1)}, f32[32,3072]{1,0:T(8,128)S(1)}, u32[]{:S(2)}, u32[]{:S(2)}) collective-permute-start(f32[32,3072]{1,0:T(8,128)S(1)} %convert_add_fusion), channel_id=1, source_target_pairs={{0,64},{32,96},{64,0},{96,32},{1,65},{33,97},{65,1},{97,33},{2,66}... | collective-permute-start | bytes 1179656 | tf_op jit(solution)/shard_map/ppermute | solution.py:37
  284.4 5.8 %collective-permute-done.1 = f32[32,3072]{1,0:T(8,128)S(1)} collective-permute-done((f32[32,3072]{1,0:T(8,128)S(1)}, f32[32,3072]{1,0:T(8,128)S(1)}, u32[]{:S(2)}, u32[]{:S(2)}) %collective-permute-start.1) | collective-permute-done | bytes 393248 | tf_op jit(solution)/shard_map/ppermute | solution.py:37
  (113 shorter events, 9.0 us)
Async XLA Ops:
  7.2 3.9 %copy-start.29 = (s32[1,128]{1,0:T(1,128)S(1)}, s32[1,128]{1,0:T(1,128)}, u32[]{:S(2)}) copy-start(s32[1,128]{1,0:T(1,128)} %param.11) | copy-start | bytes 1540
  7.2 64.7 %all-gather.5.cloned.1.call-start = ((), (), s32[]{:S(2)}) async-start(), calls=%async_computation.3 | async-start | bytes 4325376 | tf_op jit(solution)/shard_map/all_gather | solution.py:109
  15.1 15.6 %copy-start.28 = (s32[1024]{0:T(1024)S(1)}, s32[1024]{0:T(1024)}, u32[]{:S(2)}) copy-start(s32[1024]{0:T(1024)} %param.13) | copy-start | bytes 12292
  15.1 15.7 %copy-start.30 = (s32[1,4]{1,0:T(1,128)S(1)}, s32[1,4]{1,0:T(1,128)}, u32[]{:S(2)}) copy-start(s32[1,4]{1,0:T(1,128)} %param.12) | copy-start | bytes 52
  15.1 48.5 %all-to-all-start = ((bf16[128,80,128]{2,1,0:T(8,128)(2,1)}), bf16[128,80,128]{2,1,0:T(8,128)(2,1)}, u32[]{:S(2)}, u32[]{:S(2)}) async-start(bf16[128,80,128]{2,1,0:T(8,128)(2,1)} %copy.38), calls=%async_computation | async-start | bytes 5242880 | tf_op jit(solution)/shard_map/all_to_all | solution.py:86
  26.8 100.4 %all-gather.3.cloned.1.call-start = ((), (), s32[]{:S(2)}) async-start(), calls=%async_computation.2 | async-start | bytes 2162688 | tf_op jit(solution)/shard_map/all_gather | solution.py:110
  27.5 4.9 %copy-start.23 = (f32[9,1024]{1,0:T(8,128)S(1)}, f32[9,1024]{1,0:T(8,128)}, u32[]{:S(2)}) copy-start(f32[9,1024]{1,0:T(8,128)} %param.16) | copy-start | bytes 110596
  27.5 238.8 %reduce-scatter.2.cloned.1.call-start = ((), (), s32[]{:S(2)}) async-start(), calls=%async_computation.4 | async-start | bytes 6488064 | tf_op jit(solution)/shard_map/reduce_scatter | solution.py:154
  30.8 41.1 %copy-start.6 = (bf16[1024,1024]{0,1:T(8,128)(2,1)}, bf16[1024,1024]{0,1:T(8,128)(2,1)S(1)}, u32[]{:S(2)}) copy-start(bf16[1024,1024]{0,1:T(8,128)(2,1)S(1)} %copy.36) | copy-start | bytes 6291460
  31.4 40.4 %copy-start.21 = (f32[1024]{0:T(1024)}, f32[1024]{0:T(1024)S(1)}, u32[]{:S(2)}) copy-start(f32[1024]{0:T(1024)S(1)} %broadcast_multiply_fusion.2) | copy-start | bytes 12292
  32.1 39.8 %copy-start.24 = (f32[1024]{0:T(1024)}, f32[1024]{0:T(1024)S(1)}, u32[]{:S(2)}) copy-start(f32[1024]{0:T(1024)S(1)} %add_rsqrt_fusion) | copy-start | bytes 12292
  32.5 73.4 %copy-start.14 = (f32[1,1024]{1,0:T(1,128)}, f32[1,1024]{1,0:T(1,128)S(1)}, u32[]{:S(2)}) copy-start(f32[1,1024]{1,0:T(1,128)S(1)} %get-tuple-element.76) | copy-start | bytes 12292
  32.5 73.4 %copy-start.15 = (f32[1,1024]{1,0:T(1,128)}, f32[1,1024]{1,0:T(1,128)S(1)}, u32[]{:S(2)}) copy-start(f32[1,1024]{1,0:T(1,128)S(1)} %get-tuple-element.77) | copy-start | bytes 12292
  32.5 73.3 %copy-start.16 = (f32[1,1024]{1,0:T(1,128)}, f32[1,1024]{1,0:T(1,128)S(1)}, u32[]{:S(2)}) copy-start(f32[1,1024]{1,0:T(1,128)S(1)} %get-tuple-element.78) | copy-start | bytes 12292
  32.5 73.3 %copy-start.17 = (f32[1,1024]{1,0:T(1,128)}, f32[1,1024]{1,0:T(1,128)S(1)}, u32[]{:S(2)}) copy-start(f32[1,1024]{1,0:T(1,128)S(1)} %get-tuple-element.79) | copy-start | bytes 12292
  32.5 73.3 %copy-start.18 = (f32[1,1024]{1,0:T(1,128)}, f32[1,1024]{1,0:T(1,128)S(1)}, u32[]{:S(2)}) copy-start(f32[1,1024]{1,0:T(1,128)S(1)} %get-tuple-element.80) | copy-start | bytes 12292
  32.5 73.3 %copy-start.19 = (f32[1,1024]{1,0:T(1,128)}, f32[1,1024]{1,0:T(1,128)S(1)}, u32[]{:S(2)}) copy-start(f32[1,1024]{1,0:T(1,128)S(1)} %get-tuple-element.81) | copy-start | bytes 12292
  32.5 73.3 %copy-start.20 = (f32[1,1024]{1,0:T(1,128)}, f32[1,1024]{1,0:T(1,128)S(1)}, u32[]{:S(2)}) copy-start(f32[1,1024]{1,0:T(1,128)S(1)} %get-tuple-element.82) | copy-start | bytes 12292
  67.4 4.4 %copy-start.26 = (f32[1024]{0:T(1024)S(1)}, f32[1024]{0:T(1024)}, u32[]{:S(2)}) copy-start(f32[1024]{0:T(1024)} %param.14) | copy-start | bytes 12292
  90.6 15.2 %copy-start = (f32[1024,1024]{0,1:T(8,128)}, f32[1024,1024]{0,1:T(8,128)S(1)}, u32[]{:S(2)}) copy-start(f32[1024,1024]{0,1:T(8,128)S(1)} %get-tuple-element.56) | copy-start | bytes 12582916
  92.2 13.7 %copy-start.3 = (f32[1020,1024]{0,1:T(8,128)}, f32[1020,1024]{0,1:T(8,128)S(1)}, u32[]{:S(2)}) copy-start(f32[1020,1024]{0,1:T(8,128)S(1)} %get-tuple-element.66) | copy-start | bytes 12533764
  92.2 13.7 %copy-start.4 = (f32[1020,1024]{0,1:T(8,128)}, f32[1020,1024]{0,1:T(8,128)S(1)}, u32[]{:S(2)}) copy-start(f32[1020,1024]{0,1:T(8,128)S(1)} %get-tuple-element.67) | copy-start | bytes 12533764
  96.4 9.5 %copy-start.5 = (f32[1021,1024]{0,1:T(8,128)}, f32[1021,1024]{0,1:T(8,128)S(1)}, u32[]{:S(2)}) copy-start(f32[1021,1024]{0,1:T(8,128)S(1)} %get-tuple-element.68) | copy-start | bytes 12546052
  105.9 15.1 %copy-start.11 = (bf16[128,8,8,128]{3,1,2,0:T(8,128)(2,1)S(1)}, bf16[128,8,8,128]{3,1,2,0:T(8,128)(2,1)}, u32[]{:S(2)}) copy-start(bf16[128,8,8,128]{3,1,2,0:T(8,128)(2,1)} %copy.62) | copy-start | bytes 6291460
  121.0 6.1 %copy-start.12 = (bf16[128,8,8,128]{3,1,2,0:T(8,128)(2,1)S(1)}, bf16[128,8,8,128]{3,1,2,0:T(8,128)(2,1)}, u32[]{:S(2)}) copy-start(bf16[128,8,8,128]{3,1,2,0:T(8,128)(2,1)} %copy.62) | copy-start | bytes 6291460
  133.8 17.5 %copy-start.1 = (f32[1024,1024]{0,1:T(8,128)}, f32[1024,1024]{0,1:T(8,128)S(1)}, u32[]{:S(2)}) copy-start(f32[1024,1024]{0,1:T(8,128)S(1)} %multiply_multiply_fusion) | copy-start | bytes 12582916
  146.5 4.7 %copy-start.2 = (f32[1024,1024]{0,1:T(8,128)S(1)}, f32[1024,1024]{0,1:T(8,128)}, u32[]{:S(2)}) copy-start(f32[1024,1024]{0,1:T(8,128)} %get-tuple-element.14) | copy-start | bytes 12582916
  151.3 15.0 %copy-start.8 = (f32[1024,1024]{0,1:T(8,128)S(1)}, f32[1024,1024]{0,1:T(8,128)}, u32[]{:S(2)}) copy-start(f32[1024,1024]{0,1:T(8,128)} %get-tuple-element.15) | copy-start | bytes 12582916
  166.3 1.8 copy-start.7
  166.3 2.2 copy-start.9
  166.3 2.2 copy-start.22
  166.3 2.2 copy-start.25
  166.3 2.2 copy-start.27
  174.8 2.5 copy-start.13
  180.7 18.2 %copy-start.10 = (bf16[1024,2048]{0,1:T(8,128)(2,1)S(1)}, bf16[1024,2048]{0,1:T(8,128)(2,1)}, u32[]{:S(2)}) copy-start(bf16[1024,2048]{0,1:T(8,128)(2,1)} %pad_maximum_fusion.1) | copy-start | bytes 12582916
  208.2 1.4 collective-permute-start.2
  209.6 13.0 %collective-permute-start.5 = (f32[10,1024]{1,0:T(8,128)S(1)}, f32[10,1024]{1,0:T(8,128)S(1)}, u32[]{:S(2)}, u32[]{:S(2)}) collective-permute-start(f32[10,1024]{1,0:T(8,128)S(1)} %bitcast.74), channel_id=1, source_target_pairs={{0,6},{1,7},{2,4},{3,5},{4,2},{5,3},{6,0},{7,1},{8,14},{9,15},{10,... | collective-permute-start | bytes 122888 | tf_op jit(solution)/shard_map/ppermute | solution.py:53
  211.7 10.9 %collective-permute-start.4 = (f32[10,1024]{1,0:T(8,128)S(1)}, f32[10,1024]{1,0:T(8,128)S(1)}, u32[]{:S(2)}, u32[]{:S(2)}) collective-permute-start(f32[10,1024]{1,0:T(8,128)S(1)} %bitcast.75), channel_id=1, source_target_pairs={{0,4},{1,5},{2,6},{3,7},{4,0},{5,1},{6,2},{7,3},{8,12},{9,13},{10,... | collective-permute-start | bytes 122888 | tf_op jit(solution)/shard_map/ppermute | solution.py:53
  212.6 10.0 %collective-permute-start.3 = (f32[10,1024]{1,0:T(8,128)S(1)}, f32[10,1024]{1,0:T(8,128)S(1)}, u32[]{:S(2)}, u32[]{:S(2)}) collective-permute-start(f32[10,1024]{1,0:T(8,128)S(1)} %bitcast.76), channel_id=1, source_target_pairs={{0,2},{1,3},{2,0},{3,1},{4,6},{5,7},{6,4},{7,5},{8,10},{9,11},{10,... | collective-permute-start | bytes 122888 | tf_op jit(solution)/shard_map/ppermute | solution.py:53
  222.7 46.3 %collective-permute-start.8 = (f32[10,1024]{1,0:T(8,128)S(1)}, f32[10,1024]{1,0:T(8,128)S(1)}, u32[]{:S(2)}, u32[]{:S(2)}) collective-permute-start(f32[10,1024]{1,0:T(8,128)S(1)} %fusion.79), channel_id=1, source_target_pairs={{0,24},{1,25},{2,26},{3,27},{4,28},{5,29},{6,30},{7,31},{8,16},{9,... | collective-permute-start | bytes 122888 | tf_op jit(solution)/shard_map/ppermute | solution.py:53
  224.8 44.2 %collective-permute-start.7 = (f32[10,1024]{1,0:T(8,128)S(1)}, f32[10,1024]{1,0:T(8,128)S(1)}, u32[]{:S(2)}, u32[]{:S(2)}) collective-permute-start(f32[10,1024]{1,0:T(8,128)S(1)} %fusion.79), channel_id=1, source_target_pairs={{0,16},{1,17},{2,18},{3,19},{4,20},{5,21},{6,22},{7,23},{8,24},{9,... | collective-permute-start | bytes 122888 | tf_op jit(solution)/shard_map/ppermute | solution.py:53
  225.7 43.3 %collective-permute-start.6 = (f32[10,1024]{1,0:T(8,128)S(1)}, f32[10,1024]{1,0:T(8,128)S(1)}, u32[]{:S(2)}, u32[]{:S(2)}) collective-permute-start(f32[10,1024]{1,0:T(8,128)S(1)} %fusion.79), channel_id=1, source_target_pairs={{0,8},{1,9},{2,10},{3,11},{4,12},{5,13},{6,14},{7,15},{8,0},{9,1},... | collective-permute-start | bytes 122888 | tf_op jit(solution)/shard_map/ppermute | solution.py:53
  267.3 10.7 %collective-permute-start = (f32[32,3072]{1,0:T(8,128)S(1)}, f32[32,3072]{1,0:T(8,128)S(1)}, u32[]{:S(2)}, u32[]{:S(2)}) collective-permute-start(f32[32,3072]{1,0:T(8,128)S(1)} %convert_element_type.104), channel_id=1, source_target_pairs={{0,32},{32,0},{64,96},{96,64},{1,33},{33,1},{65,97},{97,65},{2,34}... | collective-permute-start | bytes 1179656 | tf_op jit(solution)/shard_map/ppermute | solution.py:37
  269.1 13.2 %collective-permute-start.11 = (f32[10,1024]{1,0:T(8,128)S(1)}, f32[10,1024]{1,0:T(8,128)S(1)}, u32[]{:S(2)}, u32[]{:S(2)}) collective-permute-start(f32[10,1024]{1,0:T(8,128)S(1)} %fusion.78), channel_id=1, source_target_pairs={{0,96},{32,64},{64,32},{96,0},{1,97},{33,65},{65,33},{97,1},{2,98}... | collective-permute-start | bytes 122888 | tf_op jit(solution)/shard_map/ppermute | solution.py:53
  271.3 11.8 %collective-permute-start.10 = (f32[10,1024]{1,0:T(8,128)S(1)}, f32[10,1024]{1,0:T(8,128)S(1)}, u32[]{:S(2)}, u32[]{:S(2)}) collective-permute-start(f32[10,1024]{1,0:T(8,128)S(1)} %fusion.78), channel_id=1, source_target_pairs={{0,64},{32,96},{64,0},{96,32},{1,65},{33,97},{65,1},{97,33},{2,66}... | collective-permute-start | bytes 122888 | tf_op jit(solution)/shard_map/ppermute | solution.py:53
  272.1 11.0 %collective-permute-start.9 = (f32[10,1024]{1,0:T(8,128)S(1)}, f32[10,1024]{1,0:T(8,128)S(1)}, u32[]{:S(2)}, u32[]{:S(2)}) collective-permute-start(f32[10,1024]{1,0:T(8,128)S(1)} %fusion.78), channel_id=1, source_target_pairs={{0,32},{32,0},{64,96},{96,64},{1,33},{33,1},{65,97},{97,65},{2,34}... | collective-permute-start | bytes 122888 | tf_op jit(solution)/shard_map/ppermute | solution.py:53
  278.9 11.2 %collective-permute-start.1 = (f32[32,3072]{1,0:T(8,128)S(1)}, f32[32,3072]{1,0:T(8,128)S(1)}, u32[]{:S(2)}, u32[]{:S(2)}) collective-permute-start(f32[32,3072]{1,0:T(8,128)S(1)} %convert_add_fusion), channel_id=1, source_target_pairs={{0,64},{32,96},{64,0},{96,32},{1,65},{33,97},{65,1},{97,33},{2,66}... | collective-permute-start | bytes 1179656 | tf_op jit(solution)/shard_map/ppermute | solution.py:37
Sparse Core Ops, SparseCore 0:
  10.2 61.4 all-gather.4
  74.0 43.0 all-gather.2
  180.7 85.5 reduce-scatter.1

commit v7 on v5

--- a/solution.py
+++ b/solution.py
@@ -167,7 +167,18 @@
     )
     small = jnp.concatenate([kernel_term, gain_term[None, :]], axis=0)
     small = group_sum(group_sum(small, "fsdp"), "dp")
-    shard_sum = butterfly(shard_sum.astype(jnp.float32), "dp")
+    n_dp = lax.axis_size("dp")
+    if n_dp > 1 and not n_dp & (n_dp - 1):
+        swap = [(i, i ^ 1) for i in range(n_dp)]
+        shard_sum = shard_sum.astype(jnp.float32) + lax.ppermute(shard_sum, "dp", swap).astype(
+            jnp.float32
+        )
+        m = 2
+        while m < n_dp:
+            shard_sum = shard_sum + lax.ppermute(shard_sum, "dp", [(i, i ^ m) for i in range(n_dp)])
+            m *= 2
+    else:
+        shard_sum = butterfly(shard_sum.astype(jnp.float32), "dp")
     return (
         input_grad.astype(jnp.bfloat16),
         shard_sum[:, : 2 * width],

time: 289 us -> 285 us (0.986)
  waiting for transfers between devices: 88.1 us -> 84.5 us
    reduce_scatter x1, waiting for transfers between devices: 41.9 us -> 37.9 us  [on_device(): lax.psum_scatter(weight_terms, 'fsdp', scatter_dimension=0, tiled=True)]
    ppermute x10, waiting for transfers between devices: 1.9 us -> 5.05 us  [group_sum(): lax.ppermute(x, axis, [(i, i ^ d << shift) for i in range(size)])]
  transfers between devices with their start and end apart: 16 -> 16, of which waited for: 7 -> 8; matrix products, arithmetic and copies ran while one was open for 34% -> 34% of each run, Pallas kernels for 0% -> 0%
where the time goes in v7:
time: 285 us; the launch traced here: 280 us
  waiting for transfers between devices  84.5 us (30%)
  local copies, waits for them, and re-layouts  57.2 us (20%)
  other arithmetic  56.9 us (20%)
  matrix products  37.4 us (13%)
  starting transfers between devices  29.5 us (10%)
  between operations  14.5 us (5%)
    reduce_scatter x1, waiting for transfers between devices, on_device(): lax.psum_scatter(weight_terms, 'fsdp', scatter_dimension=0, tiled=True)  37.9 us
    all_to_all x1, waiting for transfers between devices, route(): lax.all_to_all(outbox, ('dp', 'fsdp'), split_axis=0, concat_axis=0, tiled...  31.2 us
    slice x8, local copies, waits for them, and re-layouts, shift_rows(): return jnp.concatenate([pad, values[:rows + offset]], axis=0)  16.8 us
    slice x4, local copies, waits for them, and re-layouts, shift_rows(): return jnp.concatenate([values[offset:], pad], axis=0)  15.7 us
    another operation x3, other arithmetic  15 us
    ppermute x10, starting transfers between devices, group_sum(): lax.ppermute(x, axis, [(i, i ^ d << shift) for i in range(size)])  12.8 us
    mul x1, other arithmetic, on_device(): conv = conv * keep  12.7 us
    reduce_sum x1, other arithmetic, on_device(): kernel_rows.append(jnp.sum(masked * shift_rows(glu_f, offset, 0.0), axis=0))  12.2 us
  transfers between devices with their start and end apart: 16, of which 8 were waited for; matrix products, arithmetic and copies ran while one was open for 34% of the time, Pallas kernels for 0%

profile of v7, /device:TPU:0, one launch (start us, length us, event | category | flops | bytes accessed | tf_op | source)
XLA Modules:
  0.0 280.0 jit_solution(15497369010790990374)
XLA Ops:
  7.9 2.9 %copy.37 = bf16[128,8,8,128]{3,0,1,2:T(8,128)(2,1)S(1)} copy(bf16[128,8,8,128]{3,1,2,0:T(8,128)(2,1)} %bitcast.72) | data formatting | bytes 4194304 | tf_op jit(solution)/shard_map/reshape | solution.py:74
  11.9 3.2 %copy.38 = bf16[128,80,128]{2,1,0:T(8,128)(2,1)} copy(bf16[128,80,128]{2,0,1:T(8,128)(2,1)S(1)} %fusion.26) | data formatting | bytes 5242880 | tf_op jit(solution)/shard_map/convert_element_type | solution.py:85
  15.1 11.6 %all-to-all-start = ((bf16[128,80,128]{2,1,0:T(8,128)(2,1)}), bf16[128,80,128]{2,1,0:T(8,128)(2,1)}, u32[]{:S(2)}, u32[]{:S(2)}) async-start(bf16[128,80,128]{2,1,0:T(8,128)(2,1)} %copy.38), calls=%async_computation | async-start | bytes 5242880 | tf_op jit(solution)/shard_map/all_to_all | solution.py:86
  27.9 2.9 %copy.36 = bf16[1024,1024]{0,1:T(8,128)(2,1)S(1)} copy(bf16[1024,1024]{1,0:T(8,128)(2,1)} %param.9) | data formatting | bytes 4194304 | tf_op args[0]
  32.4 31.2 %all-to-all-done = bf16[128,80,128]{2,1,0:T(8,128)(2,1)} async-done(((bf16[128,80,128]{2,1,0:T(8,128)(2,1)}), bf16[128,80,128]{2,1,0:T(8,128)(2,1)}, u32[]{:S(2)}, u32[]{:S(2)}) %all-to-all-start) | async-done | bytes 2621472 | tf_op jit(solution)/shard_map/all_to_all | solution.py:86
  63.6 1.8 slice.187
  65.4 2.0 fusion.43
  67.4 1.7 fusion.29
  69.2 2.7 copy.62
  71.9 7.5 %fusion.38 = f32[1024,2048]{0,1:T(8,128)S(1)} fusion(bf16[1024,2048]{1,0:T(8,128)(2,1)} %all-gather.5.cloned.1.call-done, bf16[1024,1024]{0,1:T(8,128)(2,1)S(1)} %copy.36, f32[1024]{0:T(1024)S(1)} %copy-done.18, f32[1024]{0:T(1024)S(1)} %add_rsqrt_fusion, f32[1024]{0:T(1024)S(1)} %broadcast_multiply_fusion.2), kind=kOutput, calls=%fused_computation.57 | convolution fusion | flops 4300210176 | bytes 14692352 | tf_op jit(solution)/shard_map/dot_general | solution.py:120
  79.3 1.5 fusion.20
  80.9 1.7 fusion.67
  82.6 5.2 %fusion.68 = (f32[1021,1024]{0,1:T(8,128)}, f32[1021,1024]{0,1:T(8,128)}) fusion(f32[1024,1024]{0,1:T(8,128)S(1)} %fusion.20), kind=kLoop, calls=%fused_computation.113 | loop fusion | bytes 16728064 | tf_op jit(solution)/shard_map/slice | solution.py:16
  87.8 4.7 %fusion.69 = (f32[1022,1024]{0,1:T(8,128)}, f32[1022,1024]{0,1:T(8,128)}) fusion(f32[1024,1024]{0,1:T(8,128)S(1)} %fusion.20), kind=kLoop, calls=%fused_computation.114 | loop fusion | bytes 16744448 | tf_op jit(solution)/shard_map/slice | solution.py:16
  92.6 4.8 %fusion.70 = (f32[1023,1024]{0,1:T(8,128)}, f32[1023,1024]{0,1:T(8,128)}) fusion(f32[1024,1024]{0,1:T(8,128)S(1)} %fusion.20), kind=kLoop, calls=%fused_computation.115 | loop fusion | bytes 16760832 | tf_op jit(solution)/shard_map/slice | solution.py:16
  97.4 12.7 %add_multiply_fusion = f32[1024,1024]{0,1:T(8,128)S(1)} fusion(f32[1020,1024]{0,1:T(8,128)S(1)} %get-tuple-element.54, f32[1021,1024]{0,1:T(8,128)} %get-tuple-element.56, f32[1022,1024]{0,1:T(8,128)} %get-tuple-element.58, f32[1023,1024]{0,1:T(8,128)} %get-tuple-element.60, f32[1023,1024]{0,1:T(8,128)} %get-tuple-element.59, ...), kind=kLoop, calls=%fused_computation.36 | loop fusion | flops 33554432 | bytes 46129152 | tf_op jit(solution)/shard_map/mul | solution.py:133
  110.1 2.0 copy-done.14
  112.1 3.7 %fusion.32 = bf16[1024,1024]{1,0:T(8,128)(2,1)} fusion(f32[1024,1024]{0,1:T(8,128)S(1)} %add_multiply_fusion, bf16[128,8,8,128]{3,2,1,0:T(8,128)(2,1)S(1)} %bitcast.73), kind=kOutput, calls=%fused_computation.53 | convolution fusion | flops 2153775104 | bytes 8388608 | tf_op jit(solution)/shard_map/dot_general | solution.py:26
  115.8 1.3 all-gather.3.cloned.1.call-done
  117.1 6.2 %multiply_multiply_fusion = f32[1024,1024]{0,1:T(8,128)S(1)} fusion(f32[1024,1024]{0,1:T(8,128)} %copy-done.14, bf16[1024,1024]{1,0:T(8,128)(2,1)} %all-gather.3.cloned.1.call-done, f32[1024]{0:T(1024)S(1)} %convert_element_type.104, bf16[128,8,8,128]{3,2,1,0:T(8,128)(2,1)S(1)} %bitcast.74), kind=kOutput, calls=%fused_computation.34 | convolution fusion | flops 2156920832 | bytes 12587008 | tf_op jit(solution)/shard_map/dot_general | solution.py:136
  123.2 1.7 fusion.63
  124.9 4.7 %fusion.64 = (f32[1021,1024]{0,1:T(8,128)}, f32[1021,1024]{0,1:T(8,128)}) fusion(f32[1024,1024]{0,1:T(8,128)S(1)} %multiply_multiply_fusion), kind=kLoop, calls=%fused_computation.109 | loop fusion | bytes 16728064 | tf_op jit(solution)/shard_map/slice | solution.py:15
  129.6 4.6 %fusion.65 = (f32[1022,1024]{0,1:T(8,128)}, f32[1022,1024]{0,1:T(8,128)}) fusion(f32[1024,1024]{0,1:T(8,128)S(1)} %multiply_multiply_fusion), kind=kLoop, calls=%fused_computation.110 | loop fusion | bytes 16744448 | tf_op jit(solution)/shard_map/slice | solution.py:15
  134.2 4.7 %fusion.66 = (f32[1023,1024]{0,1:T(8,128)}, f32[1023,1024]{0,1:T(8,128)}) fusion(f32[1024,1024]{0,1:T(8,128)S(1)} %multiply_multiply_fusion), kind=kLoop, calls=%fused_computation.111 | loop fusion | bytes 16760832 | tf_op jit(solution)/shard_map/slice | solution.py:15
  139.0 13.2 %multiply_convert_fusion.2 = (bf16[1024,1024]{0,1:T(8,128)(2,1)}, f32[1024,1024]{0,1:T(8,128)S(1)}) fusion(f32[1024,2048]{0,1:T(8,128)S(1)} %bitcast.69, f32[1024]{0:T(1024)S(1)} %get-tuple-element.70, f32[1020,1024]{0,1:T(8,128)S(1)} %get-tuple-element.46, f32[1024]{0:T(1024)S(1)} %bitcast.104, f32[1024]{0:T(1024)S(1)} %get-tuple-element.77, ...), kind=kLoop, calls=%fused_computation.32 | loop fusion | flops 31457280 | bytes 48222208 | tf_op jit(solution)/shard_map/convert.3
  152.1 1.7 multiply_convert_fusion.1
  154.3 6.2 %convolution_convert_fusion = bf16[1024,2048]{1,0:T(8,128)(2,1)S(1)} fusion(bf16[1024,1024]{0,1:T(8,128)(2,1)S(1)} %copy-done.12, f32[1024]{0:T(1024)S(1)} %copy-done.18, f32[1024]{0:T(1024)S(1)} %add_rsqrt_fusion, f32[1024]{0:T(1024)S(1)} %broadcast_multiply_fusion.2, bf16[1024,1024]{0,1:T(8,128)(2,1)S(1)} %multiply_convert_fusion.1, ...), kind=kOutput, calls=%fused_computation.38 | convolution fusion | flops 4310695936 | bytes 10498048 | tf_op jit(solution)/shard_map/dot_general | solution.py:26
  160.6 2.5 pad_maximum_fusion.1
  163.1 3.2 %pad_maximum_fusion = bf16[1024,3072]{1,0:T(8,128)(2,1)} fusion(bf16[1024,1024]{1,0:T(8,128)(2,1)S(1)} %copy-done.16, bf16[1024,2048]{1,0:T(8,128)(2,1)S(1)} %convolution_convert_fusion), kind=kLoop, calls=%fused_computation | loop fusion | flops 12582912 | bytes 12582912 | tf_op jit(solution)/shard_map/concatenate | solution.py:147
  166.5 11.3 %fusion.11 = (f32[1024]{0:T(1024)S(1)}, f32[1024]{0:T(1024)S(1)}, f32[1024]{0:T(1024)S(1)}, f32[1024,1024]{0,1:T(8,128)}) fusion(bf16[1024,1024]{0,1:T(8,128)(2,1)} %copy-done.11, f32[1024]{0:T(1024)S(1)} %add_rsqrt_fusion, f32[1024]{0:T(1024)S(1)} %broadcast_multiply_fusion.2, f32[1024]{0:T(1024)S(1)} %copy-done.18, ...), kind=kOutput, calls=%fused_computation.14 | convolution fusion | flops 4304401408 | bytes 14704640 | tf_op jit(solution)/shard_map/dot_general | solution.py:160
  177.8 2.0 copy-done.9
  179.8 1.4 copy-done.10
  181.1 12.2 %multiply_reduce_fusion = (f32[1024]{0:T(1024)S(1)}, f32[1024]{0:T(1024)S(1)}, f32[1024]{0:T(1024)S(1)}, f32[1024]{0:T(1024)S(1)}, f32[1024]{0:T(1024)S(1)}, /*i...) fusion(f32[1024,1024]{0,1:T(8,128)S(1)} %copy-done.1, f32[1020,1024]{0,1:T(8,128)S(1)} %copy-done.6, ...), kind=kLoop, calls=%fused_computation.21 | loop fusion | flops 33545216 | bytes 46125056 | tf_op jit(solution)/shard_map/reduce_sum | solution.py:158
  193.7 1.1 collective-permute-done.2
  194.8 2.3 collective-permute-start.5
  199.0 4.3 %fusion.10 = bf16[1024,1024]{0,1:T(8,128)(2,1)S(1)} fusion(bf16[1024,1024]{0,1:T(8,128)(2,1)} %copy-done.11, f32[1024,1024]{0,1:T(8,128)} %get-tuple-element.86, f32[1024]{0:T(1024)S(1)} %get-tuple-element.87, f32[1024]{0:T(1024)S(1)} %get-tuple-element.88, f32[1024]{0:T(1024)S(1)} %copy-done.18, f32[1024]{0:T(1024)S(1)} %add_rsqrt_fusion, ...), kind=kLoop, calls=%fused_computation.13 | loop fusion | flops 9437184 | bytes 8409088 | tf_op jit(solution)/shard_map/convert_element_type | solution.py:183
  203.2 2.6 copy.44
  205.9 2.4 collective-permute-start.8
  210.1 1.4 collective-permute-done.8
  211.4 2.6 collective-permute-done.7
  214.1 37.9 %reduce-scatter.2.cloned.1.call-done = bf16[32,3072]{1,0:T(8,128)(2,1)} async-done(((bf16[1024,3072]{1,0:T(8,128)(2,1)}), bf16[32,3072]{1,0:T(8,128)(2,1)}) %reduce-scatter.2.cloned.1.call-update) | async-done | bytes 196624 | tf_op jit(solution)/shard_map/reduce_scatter | solution.py:153
  252.0 1.6 collective-permute-start
  253.6 2.2 collective-permute-start.11
  256.6 1.1 collective-permute-start.9
  257.8 1.5 collective-permute-done
  260.3 3.1 %collective-permute-start.1 = (f32[32,3072]{1,0:T(8,128)S(1)}, f32[32,3072]{1,0:T(8,128)S(1)}, u32[]{:S(2)}, u32[]{:S(2)}) collective-permute-start(f32[32,3072]{1,0:T(8,128)S(1)} %convert_add_fusion), channel_id=1, source_target_pairs={{0,64},{32,96},{64,0},{96,32},{1,65},{33,97},{65,1},{97,33},{2,66}... | collective-permute-start | bytes 1179656 | tf_op jit(solution)/shard_map/ppermute | solution.py:178
  264.7 6.1 %collective-permute-done.1 = f32[32,3072]{1,0:T(8,128)S(1)} collective-permute-done((f32[32,3072]{1,0:T(8,128)S(1)}, f32[32,3072]{1,0:T(8,128)S(1)}, u32[]{:S(2)}, u32[]{:S(2)}) %collective-permute-start.1) | collective-permute-done | bytes 393248 | tf_op jit(solution)/shard_map/ppermute | solution.py:178
  270.8 1.0 fusion.62
  (99 shorter events, 13.7 us)
Async XLA Ops:
  7.2 3.9 %copy-start.20 = (s32[1,128]{1,0:T(1,128)S(1)}, s32[1,128]{1,0:T(1,128)}, u32[]{:S(2)}) copy-start(s32[1,128]{1,0:T(1,128)} %param.11) | copy-start | bytes 1540
  7.2 64.7 %all-gather.5.cloned.1.call-start = ((), (), s32[]{:S(2)}) async-start(), calls=%async_computation.3 | async-start | bytes 4325376 | tf_op jit(solution)/shard_map/all_gather | solution.py:109
  15.1 15.6 %copy-start.19 = (s32[1024]{0:T(1024)S(1)}, s32[1024]{0:T(1024)}, u32[]{:S(2)}) copy-start(s32[1024]{0:T(1024)} %param.13) | copy-start | bytes 12292
  15.1 15.7 %copy-start.21 = (s32[1,4]{1,0:T(1,128)S(1)}, s32[1,4]{1,0:T(1,128)}, u32[]{:S(2)}) copy-start(s32[1,4]{1,0:T(1,128)} %param.12) | copy-start | bytes 52
  15.1 48.5 %all-to-all-start = ((bf16[128,80,128]{2,1,0:T(8,128)(2,1)}), bf16[128,80,128]{2,1,0:T(8,128)(2,1)}, u32[]{:S(2)}, u32[]{:S(2)}) async-start(bf16[128,80,128]{2,1,0:T(8,128)(2,1)} %copy.38), calls=%async_computation | async-start | bytes 5242880 | tf_op jit(solution)/shard_map/all_to_all | solution.py:86
  26.7 90.3 %all-gather.3.cloned.1.call-start = ((), (), s32[]{:S(2)}) async-start(), calls=%async_computation.2 | async-start | bytes 2162688 | tf_op jit(solution)/shard_map/all_gather | solution.py:110
  27.5 4.9 %copy-start.17 = (f32[9,1024]{1,0:T(8,128)S(1)}, f32[9,1024]{1,0:T(8,128)}, u32[]{:S(2)}) copy-start(f32[9,1024]{1,0:T(8,128)} %param.16) | copy-start | bytes 110596
  27.5 224.5 %reduce-scatter.2.cloned.1.call-start = ((), (), s32[]{:S(2)}) async-start(), calls=%async_computation.4 | async-start | bytes 6488064 | tf_op jit(solution)/shard_map/reduce_scatter | solution.py:153
  30.7 41.1 %copy-start.11 = (bf16[1024,1024]{0,1:T(8,128)(2,1)}, bf16[1024,1024]{0,1:T(8,128)(2,1)S(1)}, u32[]{:S(2)}) copy-start(bf16[1024,1024]{0,1:T(8,128)(2,1)S(1)} %copy.36) | copy-start | bytes 6291460
  67.4 4.5 %copy-start.18 = (f32[1024]{0:T(1024)S(1)}, f32[1024]{0:T(1024)}, u32[]{:S(2)}) copy-start(f32[1024]{0:T(1024)} %param.14) | copy-start | bytes 12292
  79.3 18.1 %copy-start.2 = (f32[1024,2048]{0,1:T(8,128)}, f32[1024,2048]{0,1:T(8,128)S(1)}, u32[]{:S(2)}) copy-start(f32[1024,2048]{0,1:T(8,128)S(1)} %fusion.38) | copy-start | bytes 25165828
  82.6 14.8 %copy-start.3 = (f32[1020,1024]{0,1:T(8,128)}, f32[1020,1024]{0,1:T(8,128)S(1)}, u32[]{:S(2)}) copy-start(f32[1020,1024]{0,1:T(8,128)S(1)} %get-tuple-element.53) | copy-start | bytes 12533764
  82.6 14.8 %copy-start.5 = (f32[1020,1024]{0,1:T(8,128)}, f32[1020,1024]{0,1:T(8,128)S(1)}, u32[]{:S(2)}) copy-start(f32[1020,1024]{0,1:T(8,128)S(1)} %get-tuple-element.54) | copy-start | bytes 12533764
  97.4 14.7 %copy-start.15 = (bf16[128,8,8,128]{3,1,2,0:T(8,128)(2,1)S(1)}, bf16[128,8,8,128]{3,1,2,0:T(8,128)(2,1)}, u32[]{:S(2)}) copy-start(bf16[128,8,8,128]{3,1,2,0:T(8,128)(2,1)} %copy.62) | copy-start | bytes 6291460
  110.1 2.0 copy-start.14
  123.2 15.7 %copy-start = (f32[1024,1024]{0,1:T(8,128)}, f32[1024,1024]{0,1:T(8,128)S(1)}, u32[]{:S(2)}) copy-start(f32[1024,1024]{0,1:T(8,128)S(1)} %multiply_multiply_fusion) | copy-start | bytes 12582916
  129.6 9.4 %slice-start = ((s8[8388608]{0:T(1024)(128)(4,1)}), s8[4194304]{0:T(1024)(128)(4,1)S(1)}, s32[]{:S(2)}) async-start(s8[8388608]{0:T(1024)(128)(4,1)} %bitcast.68), calls=%async_computation.5 | async-start | bytes 8388608
  134.2 4.7 %slice-start.1 = ((s8[8388608]{0:T(1024)(128)(4,1)}), s8[4194304]{0:T(1024)(128)(4,1)S(1)}, s32[]{:S(2)}) async-start(s8[8388608]{0:T(1024)(128)(4,1)} %bitcast.68), calls=%async_computation.6 | async-start | bytes 8388608
  152.1 1.7 copy-start.12
  152.1 2.2 copy-start.13
  160.6 2.5 copy-start.16
  166.4 11.3 %copy-start.1 = (f32[1024,1024]{0,1:T(8,128)S(1)}, f32[1024,1024]{0,1:T(8,128)}, u32[]{:S(2)}) copy-start(f32[1024,1024]{0,1:T(8,128)} %copy-done) | copy-start | bytes 12582916
  166.5 11.3 %copy-start.4 = (f32[1020,1024]{0,1:T(8,128)S(1)}, f32[1020,1024]{0,1:T(8,128)}, u32[]{:S(2)}) copy-start(f32[1020,1024]{0,1:T(8,128)} %copy-done.3) | copy-start | bytes 12533764
  166.5 11.3 %copy-start.6 = (f32[1020,1024]{0,1:T(8,128)S(1)}, f32[1020,1024]{0,1:T(8,128)}, u32[]{:S(2)}) copy-start(f32[1020,1024]{0,1:T(8,128)} %copy-done.5) | copy-start | bytes 12533764
  166.5 11.3 %copy-start.7 = (f32[1021,1024]{0,1:T(8,128)S(1)}, f32[1021,1024]{0,1:T(8,128)}, u32[]{:S(2)}) copy-start(f32[1021,1024]{0,1:T(8,128)} %get-tuple-element.55) | copy-start | bytes 12546052
  166.5 11.3 %copy-start.8 = (f32[1021,1024]{0,1:T(8,128)S(1)}, f32[1021,1024]{0,1:T(8,128)}, u32[]{:S(2)}) copy-start(f32[1021,1024]{0,1:T(8,128)} %get-tuple-element.56) | copy-start | bytes 12546052
  166.5 13.3 %copy-start.9 = (f32[1022,1024]{0,1:T(8,128)S(1)}, f32[1022,1024]{0,1:T(8,128)}, u32[]{:S(2)}) copy-start(f32[1022,1024]{0,1:T(8,128)} %get-tuple-element.57) | copy-start | bytes 12558340
  166.5 14.6 %copy-start.10 = (f32[1022,1024]{0,1:T(8,128)S(1)}, f32[1022,1024]{0,1:T(8,128)}, u32[]{:S(2)}) copy-start(f32[1022,1024]{0,1:T(8,128)} %get-tuple-element.58) | copy-start | bytes 12558340
  193.4 1.4 collective-permute-start.2
  194.8 11.0 %collective-permute-start.5 = (f32[10,1024]{1,0:T(8,128)S(1)}, f32[10,1024]{1,0:T(8,128)S(1)}, u32[]{:S(2)}, u32[]{:S(2)}) collective-permute-start(f32[10,1024]{1,0:T(8,128)S(1)} %bitcast.76), channel_id=1, source_target_pairs={{0,6},{1,7},{2,4},{3,5},{4,2},{5,3},{6,0},{7,1},{8,14},{9,15},{10,... | collective-permute-start | bytes 122888 | tf_op jit(solution)/shard_map/ppermute | solution.py:53
  197.1 8.7 %collective-permute-start.4 = (f32[10,1024]{1,0:T(8,128)S(1)}, f32[10,1024]{1,0:T(8,128)S(1)}, u32[]{:S(2)}, u32[]{:S(2)}) collective-permute-start(f32[10,1024]{1,0:T(8,128)S(1)} %bitcast.77), channel_id=1, source_target_pairs={{0,4},{1,5},{2,6},{3,7},{4,0},{5,1},{6,2},{7,3},{8,12},{9,13},{10,... | collective-permute-start | bytes 122888 | tf_op jit(solution)/shard_map/ppermute | solution.py:53
  198.0 7.8 %collective-permute-start.3 = (f32[10,1024]{1,0:T(8,128)S(1)}, f32[10,1024]{1,0:T(8,128)S(1)}, u32[]{:S(2)}, u32[]{:S(2)}) collective-permute-start(f32[10,1024]{1,0:T(8,128)S(1)} %bitcast.78), channel_id=1, source_target_pairs={{0,2},{1,3},{2,0},{3,1},{4,6},{5,7},{6,4},{7,5},{8,10},{9,11},{10,... | collective-permute-start | bytes 122888 | tf_op jit(solution)/shard_map/ppermute | solution.py:53
  205.9 5.6 %collective-permute-start.8 = (f32[10,1024]{1,0:T(8,128)S(1)}, f32[10,1024]{1,0:T(8,128)S(1)}, u32[]{:S(2)}, u32[]{:S(2)}) collective-permute-start(f32[10,1024]{1,0:T(8,128)S(1)} %fusion.81), channel_id=1, source_target_pairs={{0,24},{1,25},{2,26},{3,27},{4,28},{5,29},{6,30},{7,31},{8,16},{9,... | collective-permute-start | bytes 122888 | tf_op jit(solution)/shard_map/ppermute | solution.py:53
  208.3 5.8 %collective-permute-start.7 = (f32[10,1024]{1,0:T(8,128)S(1)}, f32[10,1024]{1,0:T(8,128)S(1)}, u32[]{:S(2)}, u32[]{:S(2)}) collective-permute-start(f32[10,1024]{1,0:T(8,128)S(1)} %fusion.81), channel_id=1, source_target_pairs={{0,16},{1,17},{2,18},{3,19},{4,20},{5,21},{6,22},{7,23},{8,24},{9,... | collective-permute-start | bytes 122888 | tf_op jit(solution)/shard_map/ppermute | solution.py:53
  209.1 4.9 %collective-permute-start.6 = (f32[10,1024]{1,0:T(8,128)S(1)}, f32[10,1024]{1,0:T(8,128)S(1)}, u32[]{:S(2)}, u32[]{:S(2)}) collective-permute-start(f32[10,1024]{1,0:T(8,128)S(1)} %fusion.81), channel_id=1, source_target_pairs={{0,8},{1,9},{2,10},{3,11},{4,12},{5,13},{6,14},{7,15},{8,0},{9,1},... | collective-permute-start | bytes 122888 | tf_op jit(solution)/shard_map/ppermute | solution.py:53
  252.0 7.3 %collective-permute-start = (bf16[32,3072]{1,0:T(8,128)(2,1)}, bf16[32,3072]{1,0:T(8,128)(2,1)S(1)}, u32[]{:S(2)}, u32[]{:S(2)}) collective-permute-start(bf16[32,3072]{1,0:T(8,128)(2,1)} %reduce-scatter.2.cloned.1.call-done), channel_id=1, source_target_pairs={{0,32},{32,0},{64,96},{96,64},{1,33},{33,1},{65,97},{97,65},{2,34}... | collective-permute-start | bytes 589832 | tf_op jit(solution)/shard_map/ppermute | solution.py:173
  253.6 9.8 %collective-permute-start.11 = (f32[10,1024]{1,0:T(8,128)S(1)}, f32[10,1024]{1,0:T(8,128)S(1)}, u32[]{:S(2)}, u32[]{:S(2)}) collective-permute-start(f32[10,1024]{1,0:T(8,128)S(1)} %fusion.80), channel_id=1, source_target_pairs={{0,96},{32,64},{64,32},{96,0},{1,97},{33,65},{65,33},{97,1},{2,98}... | collective-permute-start | bytes 122888 | tf_op jit(solution)/shard_map/ppermute | solution.py:53
  255.8 7.6 %collective-permute-start.10 = (f32[10,1024]{1,0:T(8,128)S(1)}, f32[10,1024]{1,0:T(8,128)S(1)}, u32[]{:S(2)}, u32[]{:S(2)}) collective-permute-start(f32[10,1024]{1,0:T(8,128)S(1)} %fusion.80), channel_id=1, source_target_pairs={{0,64},{32,96},{64,0},{96,32},{1,65},{33,97},{65,1},{97,33},{2,66}... | collective-permute-start | bytes 122888 | tf_op jit(solution)/shard_map/ppermute | solution.py:53
  256.6 6.8 %collective-permute-start.9 = (f32[10,1024]{1,0:T(8,128)S(1)}, f32[10,1024]{1,0:T(8,128)S(1)}, u32[]{:S(2)}, u32[]{:S(2)}) collective-permute-start(f32[10,1024]{1,0:T(8,128)S(1)} %fusion.80), channel_id=1, source_target_pairs={{0,32},{32,0},{64,96},{96,64},{1,33},{33,1},{65,97},{97,65},{2,34}... | collective-permute-start | bytes 122888 | tf_op jit(solution)/shard_map/ppermute | solution.py:53
  260.3 10.6 %collective-permute-start.1 = (f32[32,3072]{1,0:T(8,128)S(1)}, f32[32,3072]{1,0:T(8,128)S(1)}, u32[]{:S(2)}, u32[]{:S(2)}) collective-permute-start(f32[32,3072]{1,0:T(8,128)S(1)} %convert_add_fusion), channel_id=1, source_target_pairs={{0,64},{32,96},{64,0},{96,32},{1,65},{33,97},{65,1},{97,33},{2,66}... | collective-permute-start | bytes 1179656 | tf_op jit(solution)/shard_map/ppermute | solution.py:178
Sparse Core Ops, SparseCore 0:
  10.2 61.5 all-gather.4
  74.1 42.9 all-gather.2
  166.5 85.4 reduce-scatter.1

commit v8 on v7

--- a/solution.py
+++ b/solution.py
@@ -175,7 +175,10 @@
         )
         m = 2
         while m < n_dp:
-            shard_sum = shard_sum + lax.ppermute(shard_sum, "dp", [(i, i ^ m) for i in range(n_dp)])
+            half = shard_sum.astype(jnp.bfloat16)
+            shard_sum = half.astype(jnp.float32) + lax.ppermute(
+                half, "dp", [(i, i ^ m) for i in range(n_dp)]
+            ).astype(jnp.float32)
             m *= 2
     else:
         shard_sum = butterfly(shard_sum.astype(jnp.float32), "dp")

time: 285 us -> 279 us (0.979)
  waiting for transfers between devices: 84.5 us -> 79.7 us
    reduce_scatter x1, waiting for transfers between devices: 37.9 us -> 33.7 us  [on_device(): lax.psum_scatter(weight_terms, 'fsdp', scatter_dimension=0, tiled=True)]
where the time goes in v8:
time: 279 us; the launch traced here: 274 us
  waiting for transfers between devices  79.7 us (29%)
  local copies, waits for them, and re-layouts  57.2 us (21%)
  other arithmetic  55.9 us (20%)
  matrix products  37.4 us (13%)
  starting transfers between devices  29.6 us (11%)
  between operations  14.5 us (5%)
    reduce_scatter x1, waiting for transfers between devices, on_device(): lax.psum_scatter(weight_terms, 'fsdp', scatter_dimension=0, tiled=True)  33.7 us
    all_to_all x1, waiting for transfers between devices, route(): lax.all_to_all(outbox, ('dp', 'fsdp'), split_axis=0, concat_axis=0, tiled...  31.2 us
    slice x8, local copies, waits for them, and re-layouts, shift_rows(): return jnp.concatenate([pad, values[:rows + offset]], axis=0)  16.8 us
    slice x4, local copies, waits for them, and re-layouts, shift_rows(): return jnp.concatenate([values[offset:], pad], axis=0)  15.7 us
    another operation x3, other arithmetic  15 us
    ppermute x10, starting transfers between devices, group_sum(): lax.ppermute(x, axis, [(i, i ^ d << shift) for i in range(size)])  12.8 us
    mul x1, other arithmetic, on_device(): conv = conv * keep  12.7 us
    reduce_sum x1, other arithmetic, on_device(): kernel_rows.append(jnp.sum(masked * shift_rows(glu_f, offset, 0.0), axis=0))  12.2 us
  transfers between devices with their start and end apart: 16, of which 8 were waited for; matrix products, arithmetic and copies ran while one was open for 34% of the time, Pallas kernels for 0%

profile of v8, /device:TPU:0, one launch (start us, length us, event | category | flops | bytes accessed | tf_op | source)
XLA Modules:
  0.0 274.3 jit_solution(12374964340783732288)
XLA Ops:
  7.9 2.9 %copy.37 = bf16[128,8,8,128]{3,0,1,2:T(8,128)(2,1)S(1)} copy(bf16[128,8,8,128]{3,1,2,0:T(8,128)(2,1)} %bitcast.72) | data formatting | bytes 4194304 | tf_op jit(solution)/shard_map/reshape | solution.py:74
  11.9 3.2 %copy.38 = bf16[128,80,128]{2,1,0:T(8,128)(2,1)} copy(bf16[128,80,128]{2,0,1:T(8,128)(2,1)S(1)} %fusion.26) | data formatting | bytes 5242880 | tf_op jit(solution)/shard_map/convert_element_type | solution.py:85
  15.1 11.6 %all-to-all-start = ((bf16[128,80,128]{2,1,0:T(8,128)(2,1)}), bf16[128,80,128]{2,1,0:T(8,128)(2,1)}, u32[]{:S(2)}, u32[]{:S(2)}) async-start(bf16[128,80,128]{2,1,0:T(8,128)(2,1)} %copy.38), calls=%async_computation | async-start | bytes 5242880 | tf_op jit(solution)/shard_map/all_to_all | solution.py:86
  27.9 2.9 %copy.36 = bf16[1024,1024]{0,1:T(8,128)(2,1)S(1)} copy(bf16[1024,1024]{1,0:T(8,128)(2,1)} %param.9) | data formatting | bytes 4194304 | tf_op args[0]
  32.4 31.2 %all-to-all-done = bf16[128,80,128]{2,1,0:T(8,128)(2,1)} async-done(((bf16[128,80,128]{2,1,0:T(8,128)(2,1)}), bf16[128,80,128]{2,1,0:T(8,128)(2,1)}, u32[]{:S(2)}, u32[]{:S(2)}) %all-to-all-start) | async-done | bytes 2621472 | tf_op jit(solution)/shard_map/all_to_all | solution.py:86
  63.6 1.8 slice.187
  65.4 2.0 fusion.43
  67.4 1.7 fusion.29
  69.2 2.7 copy.62
  71.9 7.5 %fusion.38 = f32[1024,2048]{0,1:T(8,128)S(1)} fusion(bf16[1024,2048]{1,0:T(8,128)(2,1)} %all-gather.5.cloned.1.call-done, bf16[1024,1024]{0,1:T(8,128)(2,1)S(1)} %copy.36, f32[1024]{0:T(1024)S(1)} %copy-done.18, f32[1024]{0:T(1024)S(1)} %add_rsqrt_fusion, f32[1024]{0:T(1024)S(1)} %broadcast_multiply_fusion.2), kind=kOutput, calls=%fused_computation.58 | convolution fusion | flops 4300210176 | bytes 14692352 | tf_op jit(solution)/shard_map/dot_general | solution.py:120
  79.3 1.5 fusion.20
  80.9 1.7 fusion.66
  82.6 5.2 %fusion.67 = (f32[1021,1024]{0,1:T(8,128)}, f32[1021,1024]{0,1:T(8,128)}) fusion(f32[1024,1024]{0,1:T(8,128)S(1)} %fusion.20), kind=kLoop, calls=%fused_computation.113 | loop fusion | bytes 16728064 | tf_op jit(solution)/shard_map/slice | solution.py:16
  87.8 4.7 %fusion.68 = (f32[1022,1024]{0,1:T(8,128)}, f32[1022,1024]{0,1:T(8,128)}) fusion(f32[1024,1024]{0,1:T(8,128)S(1)} %fusion.20), kind=kLoop, calls=%fused_computation.114 | loop fusion | bytes 16744448 | tf_op jit(solution)/shard_map/slice | solution.py:16
  92.6 4.8 %fusion.69 = (f32[1023,1024]{0,1:T(8,128)}, f32[1023,1024]{0,1:T(8,128)}) fusion(f32[1024,1024]{0,1:T(8,128)S(1)} %fusion.20), kind=kLoop, calls=%fused_computation.115 | loop fusion | bytes 16760832 | tf_op jit(solution)/shard_map/slice | solution.py:16
  97.4 12.7 %add_multiply_fusion = f32[1024,1024]{0,1:T(8,128)S(1)} fusion(f32[1020,1024]{0,1:T(8,128)S(1)} %get-tuple-element.54, f32[1021,1024]{0,1:T(8,128)} %get-tuple-element.56, f32[1022,1024]{0,1:T(8,128)} %get-tuple-element.58, f32[1023,1024]{0,1:T(8,128)} %get-tuple-element.60, f32[1023,1024]{0,1:T(8,128)} %get-tuple-element.59, ...), kind=kLoop, calls=%fused_computation.36 | loop fusion | flops 33554432 | bytes 46129152 | tf_op jit(solution)/shard_map/mul | solution.py:133
  110.1 2.0 copy-done.14
  112.1 3.7 %fusion.32 = bf16[1024,1024]{1,0:T(8,128)(2,1)} fusion(f32[1024,1024]{0,1:T(8,128)S(1)} %add_multiply_fusion, bf16[128,8,8,128]{3,2,1,0:T(8,128)(2,1)S(1)} %bitcast.73), kind=kOutput, calls=%fused_computation.53 | convolution fusion | flops 2153775104 | bytes 8388608 | tf_op jit(solution)/shard_map/dot_general | solution.py:26
  115.8 1.3 all-gather.3.cloned.1.call-done
  117.1 6.2 %multiply_multiply_fusion = f32[1024,1024]{0,1:T(8,128)S(1)} fusion(f32[1024,1024]{0,1:T(8,128)} %copy-done.14, bf16[1024,1024]{1,0:T(8,128)(2,1)} %all-gather.3.cloned.1.call-done, f32[1024]{0:T(1024)S(1)} %convert_element_type.113, bf16[128,8,8,128]{3,2,1,0:T(8,128)(2,1)S(1)} %bitcast.74), kind=kOutput, calls=%fused_computation.34 | convolution fusion | flops 2156920832 | bytes 12587008 | tf_op jit(solution)/shard_map/dot_general | solution.py:136
  123.2 1.7 fusion.62
  124.9 4.7 %fusion.63 = (f32[1021,1024]{0,1:T(8,128)}, f32[1021,1024]{0,1:T(8,128)}) fusion(f32[1024,1024]{0,1:T(8,128)S(1)} %multiply_multiply_fusion), kind=kLoop, calls=%fused_computation.109 | loop fusion | bytes 16728064 | tf_op jit(solution)/shard_map/slice | solution.py:15
  129.6 4.6 %fusion.64 = (f32[1022,1024]{0,1:T(8,128)}, f32[1022,1024]{0,1:T(8,128)}) fusion(f32[1024,1024]{0,1:T(8,128)S(1)} %multiply_multiply_fusion), kind=kLoop, calls=%fused_computation.110 | loop fusion | bytes 16744448 | tf_op jit(solution)/shard_map/slice | solution.py:15
  134.2 4.7 %fusion.65 = (f32[1023,1024]{0,1:T(8,128)}, f32[1023,1024]{0,1:T(8,128)}) fusion(f32[1024,1024]{0,1:T(8,128)S(1)} %multiply_multiply_fusion), kind=kLoop, calls=%fused_computation.111 | loop fusion | bytes 16760832 | tf_op jit(solution)/shard_map/slice | solution.py:15
  139.0 13.2 %multiply_convert_fusion.2 = (bf16[1024,1024]{0,1:T(8,128)(2,1)}, f32[1024,1024]{0,1:T(8,128)S(1)}) fusion(f32[1024,2048]{0,1:T(8,128)S(1)} %bitcast.69, f32[1024]{0:T(1024)S(1)} %get-tuple-element.70, f32[1020,1024]{0,1:T(8,128)S(1)} %get-tuple-element.46, f32[1024]{0:T(1024)S(1)} %bitcast.104, f32[1024]{0:T(1024)S(1)} %get-tuple-element.77, ...), kind=kLoop, calls=%fused_computation.32 | loop fusion | flops 31457280 | bytes 48222208 | tf_op jit(solution)/shard_map/convert.3
  152.1 1.7 multiply_convert_fusion.1
  154.3 6.2 %convolution_convert_fusion = bf16[1024,2048]{1,0:T(8,128)(2,1)S(1)} fusion(bf16[1024,1024]{0,1:T(8,128)(2,1)S(1)} %copy-done.12, f32[1024]{0:T(1024)S(1)} %copy-done.18, f32[1024]{0:T(1024)S(1)} %add_rsqrt_fusion, f32[1024]{0:T(1024)S(1)} %broadcast_multiply_fusion.2, bf16[1024,1024]{0,1:T(8,128)(2,1)S(1)} %multiply_convert_fusion.1, ...), kind=kOutput, calls=%fused_computation.38 | convolution fusion | flops 4310695936 | bytes 10498048 | tf_op jit(solution)/shard_map/dot_general | solution.py:26
  160.6 2.5 pad_maximum_fusion.1
  163.1 3.2 %pad_maximum_fusion = bf16[1024,3072]{1,0:T(8,128)(2,1)} fusion(bf16[1024,1024]{1,0:T(8,128)(2,1)S(1)} %copy-done.16, bf16[1024,2048]{1,0:T(8,128)(2,1)S(1)} %convolution_convert_fusion), kind=kLoop, calls=%fused_computation | loop fusion | flops 12582912 | bytes 12582912 | tf_op jit(solution)/shard_map/concatenate | solution.py:147
  166.5 11.3 %fusion.11 = (f32[1024]{0:T(1024)S(1)}, f32[1024]{0:T(1024)S(1)}, f32[1024]{0:T(1024)S(1)}, f32[1024,1024]{0,1:T(8,128)}) fusion(bf16[1024,1024]{0,1:T(8,128)(2,1)} %copy-done.11, f32[1024]{0:T(1024)S(1)} %add_rsqrt_fusion, f32[1024]{0:T(1024)S(1)} %broadcast_multiply_fusion.2, f32[1024]{0:T(1024)S(1)} %copy-done.18, ...), kind=kOutput, calls=%fused_computation.14 | convolution fusion | flops 4304401408 | bytes 14704640 | tf_op jit(solution)/shard_map/dot_general | solution.py:160
  177.8 2.0 copy-done.9
  179.8 1.4 copy-done.10
  181.1 12.2 %multiply_reduce_fusion = (f32[1024]{0:T(1024)S(1)}, f32[1024]{0:T(1024)S(1)}, f32[1024]{0:T(1024)S(1)}, f32[1024]{0:T(1024)S(1)}, f32[1024]{0:T(1024)S(1)}, /*i...) fusion(f32[1024,1024]{0,1:T(8,128)S(1)} %copy-done.1, f32[1020,1024]{0,1:T(8,128)S(1)} %copy-done.6, ...), kind=kLoop, calls=%fused_computation.21 | loop fusion | flops 33545216 | bytes 46125056 | tf_op jit(solution)/shard_map/reduce_sum | solution.py:158
  193.7 1.1 collective-permute-done.2
  194.8 2.3 collective-permute-start.5
  198.0 1.0 collective-permute-start.3
  199.0 4.3 %fusion.10 = bf16[1024,1024]{0,1:T(8,128)(2,1)S(1)} fusion(bf16[1024,1024]{0,1:T(8,128)(2,1)} %copy-done.11, f32[1024,1024]{0,1:T(8,128)} %get-tuple-element.86, f32[1024]{0:T(1024)S(1)} %get-tuple-element.87, f32[1024]{0:T(1024)S(1)} %get-tuple-element.88, f32[1024]{0:T(1024)S(1)} %copy-done.18, f32[1024]{0:T(1024)S(1)} %add_rsqrt_fusion, ...), kind=kLoop, calls=%fused_computation.13 | loop fusion | flops 9437184 | bytes 8409088 | tf_op jit(solution)/shard_map/convert_element_type | solution.py:186
  203.2 2.6 copy.44
  205.9 2.4 collective-permute-start.8
  210.1 1.4 collective-permute-done.8
  211.4 2.6 collective-permute-done.7
  214.1 3.0 %collective-permute-start.11 = (f32[10,1024]{1,0:T(8,128)S(1)}, f32[10,1024]{1,0:T(8,128)S(1)}, u32[]{:S(2)}, u32[]{:S(2)}) collective-permute-start(f32[10,1024]{1,0:T(8,128)S(1)} %fusion.79), channel_id=1, source_target_pairs={{0,96},{32,64},{64,32},{96,0},{1,97},{33,65},{65,33},{97,1},{2,98}... | collective-permute-start | bytes 122888 | tf_op jit(solution)/shard_map/ppermute | solution.py:53
  218.3 33.7 %reduce-scatter.2.cloned.1.call-done = bf16[32,3072]{1,0:T(8,128)(2,1)} async-done(((bf16[1024,3072]{1,0:T(8,128)(2,1)}), bf16[32,3072]{1,0:T(8,128)(2,1)}) %reduce-scatter.2.cloned.1.call-update) | async-done | bytes 196624 | tf_op jit(solution)/shard_map/reduce_scatter | solution.py:153
  252.0 1.6 collective-permute-start
  254.2 3.6 %collective-permute-done = bf16[32,3072]{1,0:T(8,128)(2,1)S(1)} collective-permute-done((bf16[32,3072]{1,0:T(8,128)(2,1)}, bf16[32,3072]{1,0:T(8,128)(2,1)S(1)}, u32[]{:S(2)}, u32[]{:S(2)}) %collective-permute-start) | collective-permute-done | bytes 196640 | tf_op jit(solution)/shard_map/ppermute | solution.py:173
  257.9 1.0 add_convert_fusion
  258.9 3.2 %collective-permute-start.1 = (bf16[32,3072]{1,0:T(8,128)(2,1)S(1)}, bf16[32,3072]{1,0:T(8,128)(2,1)S(1)}, u32[]{:S(2)}, u32[]{:S(2)}) collective-permute-start(bf16[32,3072]{1,0:T(8,128)(2,1)S(1)} %add_convert_fusion), channel_id=1, source_target_pairs={{0,64},{32,96},{64,0},{96,32},{1,65},{33,97},{65,1},{97,33},{2,66}... | collective-permute-start | bytes 589832 | tf_op jit(solution)/shard_map/ppermute | solution.py:179
  262.7 3.4 %collective-permute-done.1 = bf16[32,3072]{1,0:T(8,128)(2,1)S(1)} collective-permute-done((bf16[32,3072]{1,0:T(8,128)(2,1)S(1)}, bf16[32,3072]{1,0:T(8,128)(2,1)S(1)}, u32[]{:S(2)}, u32[]{:S(2)}) %collective-permute-start.1) | collective-permute-done | bytes 196640 | tf_op jit(solution)/shard_map/ppermute | solution.py:179
  (99 shorter events, 12.2 us)
Async XLA Ops:
  7.2 3.9 %copy-start.20 = (s32[1,128]{1,0:T(1,128)S(1)}, s32[1,128]{1,0:T(1,128)}, u32[]{:S(2)}) copy-start(s32[1,128]{1,0:T(1,128)} %param.11) | copy-start | bytes 1540
  7.2 64.7 %all-gather.5.cloned.1.call-start = ((), (), s32[]{:S(2)}) async-start(), calls=%async_computation.3 | async-start | bytes 4325376 | tf_op jit(solution)/shard_map/all_gather | solution.py:109
  15.1 15.6 %copy-start.19 = (s32[1024]{0:T(1024)S(1)}, s32[1024]{0:T(1024)}, u32[]{:S(2)}) copy-start(s32[1024]{0:T(1024)} %param.13) | copy-start | bytes 12292
  15.1 15.7 %copy-start.21 = (s32[1,4]{1,0:T(1,128)S(1)}, s32[1,4]{1,0:T(1,128)}, u32[]{:S(2)}) copy-start(s32[1,4]{1,0:T(1,128)} %param.12) | copy-start | bytes 52
  15.1 48.5 %all-to-all-start = ((bf16[128,80,128]{2,1,0:T(8,128)(2,1)}), bf16[128,80,128]{2,1,0:T(8,128)(2,1)}, u32[]{:S(2)}, u32[]{:S(2)}) async-start(bf16[128,80,128]{2,1,0:T(8,128)(2,1)} %copy.38), calls=%async_computation | async-start | bytes 5242880 | tf_op jit(solution)/shard_map/all_to_all | solution.py:86
  26.7 90.3 %all-gather.3.cloned.1.call-start = ((), (), s32[]{:S(2)}) async-start(), calls=%async_computation.2 | async-start | bytes 2162688 | tf_op jit(solution)/shard_map/all_gather | solution.py:110
  27.5 4.9 %copy-start.17 = (f32[9,1024]{1,0:T(8,128)S(1)}, f32[9,1024]{1,0:T(8,128)}, u32[]{:S(2)}) copy-start(f32[9,1024]{1,0:T(8,128)} %param.16) | copy-start | bytes 110596
  27.5 224.5 %reduce-scatter.2.cloned.1.call-start = ((), (), s32[]{:S(2)}) async-start(), calls=%async_computation.4 | async-start | bytes 6488064 | tf_op jit(solution)/shard_map/reduce_scatter | solution.py:153
  30.7 41.1 %copy-start.11 = (bf16[1024,1024]{0,1:T(8,128)(2,1)}, bf16[1024,1024]{0,1:T(8,128)(2,1)S(1)}, u32[]{:S(2)}) copy-start(bf16[1024,1024]{0,1:T(8,128)(2,1)S(1)} %copy.36) | copy-start | bytes 6291460
  67.4 4.5 %copy-start.18 = (f32[1024]{0:T(1024)S(1)}, f32[1024]{0:T(1024)}, u32[]{:S(2)}) copy-start(f32[1024]{0:T(1024)} %param.14) | copy-start | bytes 12292
  79.3 18.1 %copy-start.2 = (f32[1024,2048]{0,1:T(8,128)}, f32[1024,2048]{0,1:T(8,128)S(1)}, u32[]{:S(2)}) copy-start(f32[1024,2048]{0,1:T(8,128)S(1)} %fusion.38) | copy-start | bytes 25165828
  82.6 14.8 %copy-start.3 = (f32[1020,1024]{0,1:T(8,128)}, f32[1020,1024]{0,1:T(8,128)S(1)}, u32[]{:S(2)}) copy-start(f32[1020,1024]{0,1:T(8,128)S(1)} %get-tuple-element.53) | copy-start | bytes 12533764
  82.6 14.8 %copy-start.5 = (f32[1020,1024]{0,1:T(8,128)}, f32[1020,1024]{0,1:T(8,128)S(1)}, u32[]{:S(2)}) copy-start(f32[1020,1024]{0,1:T(8,128)S(1)} %get-tuple-element.54) | copy-start | bytes 12533764
  97.4 14.7 %copy-start.15 = (bf16[128,8,8,128]{3,1,2,0:T(8,128)(2,1)S(1)}, bf16[128,8,8,128]{3,1,2,0:T(8,128)(2,1)}, u32[]{:S(2)}) copy-start(bf16[128,8,8,128]{3,1,2,0:T(8,128)(2,1)} %copy.62) | copy-start | bytes 6291460
  110.1 2.0 copy-start.14
  123.2 15.7 %copy-start = (f32[1024,1024]{0,1:T(8,128)}, f32[1024,1024]{0,1:T(8,128)S(1)}, u32[]{:S(2)}) copy-start(f32[1024,1024]{0,1:T(8,128)S(1)} %multiply_multiply_fusion) | copy-start | bytes 12582916
  129.6 9.4 %slice-start = ((s8[8388608]{0:T(1024)(128)(4,1)}), s8[4194304]{0:T(1024)(128)(4,1)S(1)}, s32[]{:S(2)}) async-start(s8[8388608]{0:T(1024)(128)(4,1)} %bitcast.68), calls=%async_computation.5 | async-start | bytes 8388608
  134.2 4.7 %slice-start.1 = ((s8[8388608]{0:T(1024)(128)(4,1)}), s8[4194304]{0:T(1024)(128)(4,1)S(1)}, s32[]{:S(2)}) async-start(s8[8388608]{0:T(1024)(128)(4,1)} %bitcast.68), calls=%async_computation.6 | async-start | bytes 8388608
  152.1 1.7 copy-start.12
  152.1 2.2 copy-start.13
  160.6 2.5 copy-start.16
  166.4 11.3 %copy-start.1 = (f32[1024,1024]{0,1:T(8,128)S(1)}, f32[1024,1024]{0,1:T(8,128)}, u32[]{:S(2)}) copy-start(f32[1024,1024]{0,1:T(8,128)} %copy-done) | copy-start | bytes 12582916
  166.5 11.3 %copy-start.4 = (f32[1020,1024]{0,1:T(8,128)S(1)}, f32[1020,1024]{0,1:T(8,128)}, u32[]{:S(2)}) copy-start(f32[1020,1024]{0,1:T(8,128)} %copy-done.3) | copy-start | bytes 12533764
  166.5 11.3 %copy-start.6 = (f32[1020,1024]{0,1:T(8,128)S(1)}, f32[1020,1024]{0,1:T(8,128)}, u32[]{:S(2)}) copy-start(f32[1020,1024]{0,1:T(8,128)} %copy-done.5) | copy-start | bytes 12533764
  166.5 11.3 %copy-start.7 = (f32[1021,1024]{0,1:T(8,128)S(1)}, f32[1021,1024]{0,1:T(8,128)}, u32[]{:S(2)}) copy-start(f32[1021,1024]{0,1:T(8,128)} %get-tuple-element.55) | copy-start | bytes 12546052
  166.5 11.3 %copy-start.8 = (f32[1021,1024]{0,1:T(8,128)S(1)}, f32[1021,1024]{0,1:T(8,128)}, u32[]{:S(2)}) copy-start(f32[1021,1024]{0,1:T(8,128)} %get-tuple-element.56) | copy-start | bytes 12546052
  166.5 13.3 %copy-start.9 = (f32[1022,1024]{0,1:T(8,128)S(1)}, f32[1022,1024]{0,1:T(8,128)}, u32[]{:S(2)}) copy-start(f32[1022,1024]{0,1:T(8,128)} %get-tuple-element.57) | copy-start | bytes 12558340
  166.5 14.6 %copy-start.10 = (f32[1022,1024]{0,1:T(8,128)S(1)}, f32[1022,1024]{0,1:T(8,128)}, u32[]{:S(2)}) copy-start(f32[1022,1024]{0,1:T(8,128)} %get-tuple-element.58) | copy-start | bytes 12558340
  193.4 1.4 collective-permute-start.2
  194.8 11.0 %collective-permute-start.5 = (f32[10,1024]{1,0:T(8,128)S(1)}, f32[10,1024]{1,0:T(8,128)S(1)}, u32[]{:S(2)}, u32[]{:S(2)}) collective-permute-start(f32[10,1024]{1,0:T(8,128)S(1)} %bitcast.76), channel_id=1, source_target_pairs={{0,6},{1,7},{2,4},{3,5},{4,2},{5,3},{6,0},{7,1},{8,14},{9,15},{10,... | collective-permute-start | bytes 122888 | tf_op jit(solution)/shard_map/ppermute | solution.py:53
  197.1 8.7 %collective-permute-start.4 = (f32[10,1024]{1,0:T(8,128)S(1)}, f32[10,1024]{1,0:T(8,128)S(1)}, u32[]{:S(2)}, u32[]{:S(2)}) collective-permute-start(f32[10,1024]{1,0:T(8,128)S(1)} %bitcast.77), channel_id=1, source_target_pairs={{0,4},{1,5},{2,6},{3,7},{4,0},{5,1},{6,2},{7,3},{8,12},{9,13},{10,... | collective-permute-start | bytes 122888 | tf_op jit(solution)/shard_map/ppermute | solution.py:53
  198.0 7.8 %collective-permute-start.3 = (f32[10,1024]{1,0:T(8,128)S(1)}, f32[10,1024]{1,0:T(8,128)S(1)}, u32[]{:S(2)}, u32[]{:S(2)}) collective-permute-start(f32[10,1024]{1,0:T(8,128)S(1)} %bitcast.78), channel_id=1, source_target_pairs={{0,2},{1,3},{2,0},{3,1},{4,6},{5,7},{6,4},{7,5},{8,10},{9,11},{10,... | collective-permute-start | bytes 122888 | tf_op jit(solution)/shard_map/ppermute | solution.py:53
  205.9 5.6 %collective-permute-start.8 = (f32[10,1024]{1,0:T(8,128)S(1)}, f32[10,1024]{1,0:T(8,128)S(1)}, u32[]{:S(2)}, u32[]{:S(2)}) collective-permute-start(f32[10,1024]{1,0:T(8,128)S(1)} %fusion.80), channel_id=1, source_target_pairs={{0,24},{1,25},{2,26},{3,27},{4,28},{5,29},{6,30},{7,31},{8,16},{9,... | collective-permute-start | bytes 122888 | tf_op jit(solution)/shard_map/ppermute | solution.py:53
  208.3 5.8 %collective-permute-start.7 = (f32[10,1024]{1,0:T(8,128)S(1)}, f32[10,1024]{1,0:T(8,128)S(1)}, u32[]{:S(2)}, u32[]{:S(2)}) collective-permute-start(f32[10,1024]{1,0:T(8,128)S(1)} %fusion.80), channel_id=1, source_target_pairs={{0,16},{1,17},{2,18},{3,19},{4,20},{5,21},{6,22},{7,23},{8,24},{9,... | collective-permute-start | bytes 122888 | tf_op jit(solution)/shard_map/ppermute | solution.py:53
  209.1 4.9 %collective-permute-start.6 = (f32[10,1024]{1,0:T(8,128)S(1)}, f32[10,1024]{1,0:T(8,128)S(1)}, u32[]{:S(2)}, u32[]{:S(2)}) collective-permute-start(f32[10,1024]{1,0:T(8,128)S(1)} %fusion.80), channel_id=1, source_target_pairs={{0,8},{1,9},{2,10},{3,11},{4,12},{5,13},{6,14},{7,15},{8,0},{9,1},... | collective-permute-start | bytes 122888 | tf_op jit(solution)/shard_map/ppermute | solution.py:53
  214.1 39.5 %collective-permute-start.11 = (f32[10,1024]{1,0:T(8,128)S(1)}, f32[10,1024]{1,0:T(8,128)S(1)}, u32[]{:S(2)}, u32[]{:S(2)}) collective-permute-start(f32[10,1024]{1,0:T(8,128)S(1)} %fusion.79), channel_id=1, source_target_pairs={{0,96},{32,64},{64,32},{96,0},{1,97},{33,65},{65,33},{97,1},{2,98}... | collective-permute-start | bytes 122888 | tf_op jit(solution)/shard_map/ppermute | solution.py:53
  217.1 36.5 %collective-permute-start.10 = (f32[10,1024]{1,0:T(8,128)S(1)}, f32[10,1024]{1,0:T(8,128)S(1)}, u32[]{:S(2)}, u32[]{:S(2)}) collective-permute-start(f32[10,1024]{1,0:T(8,128)S(1)} %fusion.79), channel_id=1, source_target_pairs={{0,64},{32,96},{64,0},{96,32},{1,65},{33,97},{65,1},{97,33},{2,66}... | collective-permute-start | bytes 122888 | tf_op jit(solution)/shard_map/ppermute | solution.py:53
  217.8 35.8 %collective-permute-start.9 = (f32[10,1024]{1,0:T(8,128)S(1)}, f32[10,1024]{1,0:T(8,128)S(1)}, u32[]{:S(2)}, u32[]{:S(2)}) collective-permute-start(f32[10,1024]{1,0:T(8,128)S(1)} %fusion.79), channel_id=1, source_target_pairs={{0,32},{32,0},{64,96},{96,64},{1,33},{33,1},{65,97},{97,65},{2,34}... | collective-permute-start | bytes 122888 | tf_op jit(solution)/shard_map/ppermute | solution.py:53
  252.0 5.9 %collective-permute-start = (bf16[32,3072]{1,0:T(8,128)(2,1)}, bf16[32,3072]{1,0:T(8,128)(2,1)S(1)}, u32[]{:S(2)}, u32[]{:S(2)}) collective-permute-start(bf16[32,3072]{1,0:T(8,128)(2,1)} %reduce-scatter.2.cloned.1.call-done), channel_id=1, source_target_pairs={{0,32},{32,0},{64,96},{96,64},{1,33},{33,1},{65,97},{97,65},{2,34}... | collective-permute-start | bytes 589832 | tf_op jit(solution)/shard_map/ppermute | solution.py:173
  258.9 7.3 %collective-permute-start.1 = (bf16[32,3072]{1,0:T(8,128)(2,1)S(1)}, bf16[32,3072]{1,0:T(8,128)(2,1)S(1)}, u32[]{:S(2)}, u32[]{:S(2)}) collective-permute-start(bf16[32,3072]{1,0:T(8,128)(2,1)S(1)} %add_convert_fusion), channel_id=1, source_target_pairs={{0,64},{32,96},{64,0},{96,32},{1,65},{33,97},{65,1},{97,33},{2,66}... | collective-permute-start | bytes 589832 | tf_op jit(solution)/shard_map/ppermute | solution.py:179
Sparse Core Ops, SparseCore 0:
  10.2 61.5 all-gather.4
  74.1 42.9 all-gather.2
  166.5 85.4 reduce-scatter.1

commit v9 on v8

--- a/solution.py
+++ b/solution.py
@@ -133,6 +133,7 @@
     conv = conv * keep
     sig_c = jax.nn.sigmoid(conv)
     act = (conv * sig_c).astype(jnp.bfloat16)
+    sig_b_kept = lax.optimization_barrier(sig_b)
     act_grad = jnp.dot(out_grad, down_full.T, preferred_element_type=jnp.float32)
     conv_grad = act_grad * sig_c * (1.0 + conv * (1.0 - sig_c)) * keep
     glu_grad = jnp.zeros((rows, width), jnp.float32)
@@ -141,8 +142,8 @@
         glu_grad = glu_grad + kernel[k][None, :] * (
             shift_rows(conv_grad, -offset, 0.0) * sames[taps - 1 - k]
         )
-    value_grad = glu_grad * sig_b
-    gate_grad = glu_grad * value * sig_b * (1.0 - sig_b)
+    value_grad = glu_grad * sig_b_kept
+    gate_grad = glu_grad * value * sig_b_kept * (1.0 - sig_b_kept)
     up_out_grad = jnp.concatenate([value_grad, gate_grad], axis=1).astype(jnp.bfloat16)
     weight_terms = jnp.concatenate(
         [contract_rows(hidden, up_out_grad), contract_rows(act, out_grad)], axis=1

time: 279 us -> 287 us (1.029)
  other arithmetic: 55.9 us -> 70.4 us
  local copies, waits for them, and re-layouts: 57.2 us -> 52.5 us
  waiting for transfers between devices: 79.7 us -> 76.8 us
    reduce_sum x1, other arithmetic: 12.2 us -> 18.2 us  [on_device(): kernel_rows.append(jnp.sum(masked * shift_rows(glu_f, offset, 0.0), axis=0))]
    another operation x3, other arithmetic: 15 us -> 20.7 us
    div x0 -> x1, other arithmetic: none -> 3.99 us  [on_device(): sig_b = jax.nn.sigmoid(up[:, width:])]
    unnamed x50 -> x70, local copies, waits for them, and re-layouts: 11.3 us -> 7.47 us
    slice x8, local copies, waits for them, and re-layouts: 16.8 us -> 13.5 us  [shift_rows(): return jnp.concatenate([pad, values[:rows + offset]], axis=0)]
    reduce_scatter x1, waiting for transfers between devices: 33.7 us -> 30.5 us  [on_device(): lax.psum_scatter(weight_terms, 'fsdp', scatter_dimension=0, tiled=True)]
  transfers between devices with their start and end apart: 16 -> 16, of which waited for: 8 -> 9; matrix products, arithmetic and copies ran while one was open for 34% -> 36% of each run, Pallas kernels for 0% -> 0%
where the time goes in v9:
time: 287 us; the launch traced here: 282 us
  waiting for transfers between devices  76.8 us (27%)
  other arithmetic  70.4 us (25%)
  local copies, waits for them, and re-layouts  52.5 us (18%)
  matrix products  37.8 us (13%)
  starting transfers between devices  29.7 us (10%)
  between operations  14.9 us (5%)
    all_to_all x1, waiting for transfers between devices, route(): lax.all_to_all(outbox, ('dp', 'fsdp'), split_axis=0, concat_axis=0, tiled...  31.1 us
    reduce_scatter x1, waiting for transfers between devices, on_device(): lax.psum_scatter(weight_terms, 'fsdp', scatter_dimension=0, tiled=True)  30.5 us
    another operation x3, other arithmetic  20.7 us
    reduce_sum x1, other arithmetic, on_device(): kernel_rows.append(jnp.sum(masked * shift_rows(glu_f, offset, 0.0), axis=0))  18.2 us
    slice x4, local copies, waits for them, and re-layouts, shift_rows(): return jnp.concatenate([values[offset:], pad], axis=0)  17.9 us
    slice x8, local copies, waits for them, and re-layouts, shift_rows(): return jnp.concatenate([pad, values[:rows + offset]], axis=0)  13.5 us
    ppermute x10, starting transfers between devices, group_sum(): lax.ppermute(x, axis, [(i, i ^ d << shift) for i in range(size)])  12.8 us
    mul x1, other arithmetic, on_device(): conv = conv * keep  12.6 us
  transfers between devices with their start and end apart: 16, of which 9 were waited for; matrix products, arithmetic and copies ran while one was open for 36% of the time, Pallas kernels for 0%

profile of v9, /device:TPU:0, one launch (start us, length us, event | category | flops | bytes accessed | tf_op | source)
XLA Modules:
  0.0 282.0 jit_solution(5039009094846013424)
XLA Ops:
  7.9 2.9 %copy.37 = bf16[128,8,8,128]{3,0,1,2:T(8,128)(2,1)S(1)} copy(bf16[128,8,8,128]{3,1,2,0:T(8,128)(2,1)} %bitcast.72) | data formatting | bytes 4194304 | tf_op jit(solution)/shard_map/reshape | solution.py:74
  11.9 3.3 %copy.38 = bf16[128,80,128]{2,1,0:T(8,128)(2,1)} copy(bf16[128,80,128]{2,0,1:T(8,128)(2,1)S(1)} %fusion.26) | data formatting | bytes 5242880 | tf_op jit(solution)/shard_map/convert_element_type | solution.py:85
  15.2 11.6 %all-to-all-start = ((bf16[128,80,128]{2,1,0:T(8,128)(2,1)}), bf16[128,80,128]{2,1,0:T(8,128)(2,1)}, u32[]{:S(2)}, u32[]{:S(2)}) async-start(bf16[128,80,128]{2,1,0:T(8,128)(2,1)} %copy.38), calls=%async_computation | async-start | bytes 5242880 | tf_op jit(solution)/shard_map/all_to_all | solution.py:86
  27.9 2.9 %copy.36 = bf16[1024,1024]{0,1:T(8,128)(2,1)S(1)} copy(bf16[1024,1024]{1,0:T(8,128)(2,1)} %param.9) | data formatting | bytes 4194304 | tf_op args[0]
  32.6 31.1 %all-to-all-done = bf16[128,80,128]{2,1,0:T(8,128)(2,1)} async-done(((bf16[128,80,128]{2,1,0:T(8,128)(2,1)}), bf16[128,80,128]{2,1,0:T(8,128)(2,1)}, u32[]{:S(2)}, u32[]{:S(2)}) %all-to-all-start) | async-done | bytes 2621472 | tf_op jit(solution)/shard_map/all_to_all | solution.py:86
  63.6 1.8 slice.187
  65.4 2.0 fusion.43
  67.4 1.7 fusion.29
  69.2 2.7 copy.62
  71.9 7.5 %fusion.38 = f32[1024,2048]{0,1:T(8,128)S(1)} fusion(bf16[1024,2048]{1,0:T(8,128)(2,1)} %all-gather.5.cloned.1.call-done, bf16[1024,1024]{0,1:T(8,128)(2,1)S(1)} %copy.36, f32[1024]{0:T(1024)S(1)} %copy-done.27, f32[1024]{0:T(1024)S(1)} %add_rsqrt_fusion, f32[1024]{0:T(1024)S(1)} %broadcast_multiply_fusion.2), kind=kOutput, calls=%fused_computation.58 | convolution fusion | flops 4300210176 | bytes 14692352 | tf_op jit(solution)/shard_map/dot_general | solution.py:120
  79.4 4.0 %fusion.15 = (f32[1024,1024]{0,1:T(8,128)}, f32[1024,1024]{0,1:T(8,128)S(1)}) fusion(f32[1024,2048]{0,1:T(8,128)S(1)} %fusion.38), kind=kLoop, calls=%fused_computation.19 | loop fusion | flops 6291456 | bytes 16777216 | tf_op jit(solution)/shard_map/div | solution.py:122
  83.9 1.7 fusion.66
  85.6 1.7 fusion.67
  87.2 5.2 %fusion.68 = (f32[1022,1024]{0,1:T(8,128)}, f32[1022,1024]{0,1:T(8,128)}) fusion(f32[1024,1024]{0,1:T(8,128)S(1)} %get-tuple-element.46), kind=kLoop, calls=%fused_computation.114 | loop fusion | bytes 16744448 | tf_op jit(solution)/shard_map/slice | solution.py:16
  92.5 4.7 %fusion.69 = (f32[1023,1024]{0,1:T(8,128)}, f32[1023,1024]{0,1:T(8,128)}) fusion(f32[1024,1024]{0,1:T(8,128)S(1)} %get-tuple-element.46), kind=kLoop, calls=%fused_computation.115 | loop fusion | bytes 16760832 | tf_op jit(solution)/shard_map/slice | solution.py:16
  97.3 12.6 %add_multiply_fusion = f32[1024,1024]{0,1:T(8,128)} fusion(f32[1024,1024]{0,1:T(8,128)S(1)} %get-tuple-element.46, f32[1020,1024]{0,1:T(8,128)S(1)} %get-tuple-element.56, f32[1021,1024]{0,1:T(8,128)S(1)} %get-tuple-element.58, f32[1022,1024]{0,1:T(8,128)} %get-tuple-element.60, f32[1023,1024]{0,1:T(8,128)} %get-tuple-element.62, ...), kind=kLoop, calls=%fused_computation.36 | loop fusion | flops 27262976 | bytes 41934848 | tf_op jit(solution)/shard_map/mul | solution.py:133
  109.9 6.1 %fusion.32 = bf16[1024,1024]{1,0:T(8,128)(2,1)} fusion(f32[1024,1024]{0,1:T(8,128)} %add_multiply_fusion, bf16[128,8,8,128]{3,2,1,0:T(8,128)(2,1)S(1)} %bitcast.73), kind=kOutput, calls=%fused_computation.53 | convolution fusion | flops 2153775104 | bytes 8388608 | tf_op jit(solution)/shard_map/dot_general | solution.py:26
  116.0 1.1 all-gather.3.cloned.1.call-done
  117.1 6.2 %multiply_multiply_fusion = f32[1024,1024]{0,1:T(8,128)S(1)} fusion(f32[1024,1024]{0,1:T(8,128)} %add_multiply_fusion, bf16[1024,1024]{1,0:T(8,128)(2,1)} %all-gather.3.cloned.1.call-done, f32[1024]{0:T(1024)S(1)} %convert_element_type.113, bf16[128,8,8,128]{3,2,1,0:T(8,128)(2,1)S(1)} %bitcast.74), kind=kOutput, calls=%fused_computation.34 | convolution fusion | flops 2156920832 | bytes 12587008 | tf_op jit(solution)/shard_map/dot_general | solution.py:137
  123.3 3.4 %fusion.62 = (f32[1020,1024]{0,1:T(8,128)S(1)}, f32[1020,1024]{0,1:T(8,128)}) fusion(f32[1024,1024]{0,1:T(8,128)S(1)} %multiply_multiply_fusion), kind=kLoop, calls=%fused_computation.108 | loop fusion | bytes 16711680 | tf_op jit(solution)/shard_map/slice | solution.py:15
  126.6 4.6 %fusion.63 = (f32[1021,1024]{0,1:T(8,128)}, f32[1021,1024]{0,1:T(8,128)}) fusion(f32[1024,1024]{0,1:T(8,128)S(1)} %multiply_multiply_fusion), kind=kLoop, calls=%fused_computation.109 | loop fusion | bytes 16728064 | tf_op jit(solution)/shard_map/slice | solution.py:15
  131.3 4.6 %fusion.64 = (f32[1022,1024]{0,1:T(8,128)}, f32[1022,1024]{0,1:T(8,128)}) fusion(f32[1024,1024]{0,1:T(8,128)S(1)} %multiply_multiply_fusion), kind=kLoop, calls=%fused_computation.110 | loop fusion | bytes 16744448 | tf_op jit(solution)/shard_map/slice | solution.py:15
  135.9 5.3 %fusion.65 = (f32[1023,1024]{0,1:T(8,128)}, f32[1023,1024]{0,1:T(8,128)}) fusion(f32[1024,1024]{0,1:T(8,128)S(1)} %multiply_multiply_fusion), kind=kLoop, calls=%fused_computation.111 | loop fusion | bytes 16760832 | tf_op jit(solution)/shard_map/slice | solution.py:15
  141.2 16.6 %multiply_convert_fusion.2 = (bf16[1024,1024]{0,1:T(8,128)(2,1)}, f32[1024,1024]{0,1:T(8,128)}) fusion(f32[1024,1024]{0,1:T(8,128)S(1)} %copy-done.2, f32[1024]{0:T(1024)S(1)} %get-tuple-element.72, f32[1020,1024]{0,1:T(8,128)} %get-tuple-element.48, f32[1024]{0:T(1024)} %bitcast.104, f32[1024]{0:T(1024)S(1)} %get-tuple-element.79, ...), kind=kLoop, calls=%fused_computation.32 | loop fusion | flops 28311552 | bytes 48222208 | tf_op jit(solution)/shard_map/convert.3
  157.9 4.0 %multiply_convert_fusion.1 = bf16[1024,1024]{0,1:T(8,128)(2,1)S(1)} fusion(f32[1024,1024]{0,1:T(8,128)S(1)} %copy-done.2, f32[1024,1024]{0,1:T(8,128)} %get-tuple-element.44, f32[1024,2048]{0,1:T(8,128)S(1)} %bitcast.69), kind=kLoop, calls=%fused_computation.31 | loop fusion | flops 5242880 | bytes 14680064 | tf_op jit(solution)/shard_map/convert.4
  161.9 6.3 %convolution_convert_fusion = bf16[1024,2048]{1,0:T(8,128)(2,1)S(1)} fusion(bf16[1024,1024]{0,1:T(8,128)(2,1)S(1)} %copy-done.8, f32[1024]{0:T(1024)S(1)} %copy-done.28, f32[1024]{0:T(1024)S(1)} %copy-done.26, f32[1024]{0:T(1024)S(1)} %copy-done.23, bf16[1024,1024]{0,1:T(8,128)(2,1)S(1)} %multiply_convert_fusion.1, bf16[1024,1024]{0,1:T(8,128)(2,1)S(1)} %copy-done.10), kind=kOutput, calls=%fused_computation.38 | convolution fusion | flops 4310695936 | bytes 10498048 | tf_op jit(solution)/shard_map/dot_general | solution.py:26
  168.2 2.4 pad_maximum_fusion.1
  170.6 3.2 %pad_maximum_fusion = bf16[1024,3072]{1,0:T(8,128)(2,1)} fusion(bf16[1024,1024]{1,0:T(8,128)(2,1)S(1)} %copy-done.14, bf16[1024,2048]{1,0:T(8,128)(2,1)S(1)} %convolution_convert_fusion), kind=kLoop, calls=%fused_computation | loop fusion | flops 12582912 | bytes 12582912 | tf_op jit(solution)/shard_map/concatenate | solution.py:148
  174.0 18.2 %multiply_reduce_fusion = (f32[1024]{0:T(1024)S(1)}, f32[1024]{0:T(1024)S(1)}, f32[1024]{0:T(1024)S(1)}, f32[1024]{0:T(1024)S(1)}, f32[1024]{0:T(1024)S(1)}, /*i...) fusion(f32[1024,1024]{0,1:T(8,128)} %copy-done.1, f32[1020,1024]{0,1:T(8,128)} %copy-done.4, ...), kind=kLoop, calls=%fused_computation.21 | loop fusion | flops 27253760 | bytes 41930752 | tf_op jit(solution)/shard_map/reduce_sum | solution.py:159
  192.2 9.2 %fusion.11 = (f32[1024]{0:T(1024)S(1)}, f32[1024]{0:T(1024)S(1)}, f32[1024]{0:T(1024)S(1)}, f32[1024,1024]{0,1:T(8,128)}) fusion(bf16[1024,1024]{0,1:T(8,128)(2,1)S(1)} %copy-done.8, f32[1024]{0:T(1024)S(1)} %copy-done.26, f32[1024]{0:T(1024)S(1)} %copy-done.23, f32[1024]{0:T(1024)S(1)} %copy-done.28, bf16[1024,2048]{1,0:T(8,128)(2,1)} %all-gather.5.cloned.1.call-done, ...), kind=kOutput, calls=%fused_computation.14 | convolution fusion | flops 4304401408 | bytes 14704640 | tf_op jit(solution)/shard_map/dot_general | solution.py:161
  201.8 1.0 collective-permute-done.2
  202.9 2.4 collective-permute-start.5
  205.3 0.9 collective-permute-start.4
  206.1 0.9 collective-permute-start.3
  207.0 4.9 %fusion.10 = bf16[1024,1024]{0,1:T(8,128)(2,1)} fusion(bf16[1024,1024]{0,1:T(8,128)(2,1)S(1)} %copy-done.8, f32[1024,1024]{0,1:T(8,128)} %get-tuple-element.88, f32[1024]{0:T(1024)S(1)} %get-tuple-element.89, f32[1024]{0:T(1024)S(1)} %get-tuple-element.90, f32[1024]{0:T(1024)S(1)} %copy-done.28, f32[1024]{0:T(1024)S(1)} %copy-done.26, f32[1024]{0:T(1024)S(1)} %copy-done.23), kind=kLoop, calls=%fused_computation.13 | loop fusion | flops 9437184 | bytes 8409088 | tf_op jit(solution)/shard_map/convert_element_type | solution.py:187
  212.0 3.9 %copy.44 = bf16[1024,1024]{1,0:T(8,128)(2,1)} copy(bf16[1024,1024]{0,1:T(8,128)(2,1)} %fusion.10) | data formatting | bytes 4194304
  216.0 2.4 collective-permute-start.8
  218.4 0.8 collective-permute-start.7
  219.2 0.9 collective-permute-start.6
  220.2 1.4 collective-permute-done.8
  221.5 2.6 collective-permute-done.7
  224.8 3.0 %collective-permute-start.11 = (f32[10,1024]{1,0:T(8,128)S(1)}, f32[10,1024]{1,0:T(8,128)S(1)}, u32[]{:S(2)}, u32[]{:S(2)}) collective-permute-start(f32[10,1024]{1,0:T(8,128)S(1)} %fusion.79), channel_id=1, source_target_pairs={{0,96},{32,64},{64,32},{96,0},{1,97},{33,65},{65,33},{97,1},{2,98}... | collective-permute-start | bytes 122888 | tf_op jit(solution)/shard_map/ppermute | solution.py:53
  229.0 30.5 %reduce-scatter.2.cloned.1.call-done = bf16[32,3072]{1,0:T(8,128)(2,1)} async-done(((bf16[1024,3072]{1,0:T(8,128)(2,1)}), bf16[32,3072]{1,0:T(8,128)(2,1)}) %reduce-scatter.2.cloned.1.call-update) | async-done | bytes 196624 | tf_op jit(solution)/shard_map/reduce_scatter | solution.py:154
  259.5 1.6 collective-permute-start
  261.8 3.6 %collective-permute-done = bf16[32,3072]{1,0:T(8,128)(2,1)S(1)} collective-permute-done((bf16[32,3072]{1,0:T(8,128)(2,1)}, bf16[32,3072]{1,0:T(8,128)(2,1)S(1)}, u32[]{:S(2)}, u32[]{:S(2)}) %collective-permute-start) | collective-permute-done | bytes 196640 | tf_op jit(solution)/shard_map/ppermute | solution.py:174
  265.4 1.0 add_convert_fusion
  266.4 3.2 %collective-permute-start.1 = (bf16[32,3072]{1,0:T(8,128)(2,1)S(1)}, bf16[32,3072]{1,0:T(8,128)(2,1)S(1)}, u32[]{:S(2)}, u32[]{:S(2)}) collective-permute-start(bf16[32,3072]{1,0:T(8,128)(2,1)S(1)} %add_convert_fusion), channel_id=1, source_target_pairs={{0,64},{32,96},{64,0},{96,32},{1,65},{33,97},{65,1},{97,33},{2,66}... | collective-permute-start | bytes 589832 | tf_op jit(solution)/shard_map/ppermute | solution.py:180
  270.2 3.4 %collective-permute-done.1 = bf16[32,3072]{1,0:T(8,128)(2,1)S(1)} collective-permute-done((bf16[32,3072]{1,0:T(8,128)(2,1)S(1)}, bf16[32,3072]{1,0:T(8,128)(2,1)S(1)}, u32[]{:S(2)}, u32[]{:S(2)}) %collective-permute-start.1) | collective-permute-done | bytes 196640 | tf_op jit(solution)/shard_map/ppermute | solution.py:180
  (119 shorter events, 10.1 us)
Async XLA Ops:
  7.2 64.7 %all-gather.5.cloned.1.call-start = ((), (), s32[]{:S(2)}) async-start(), calls=%async_computation.3 | async-start | bytes 4325376 | tf_op jit(solution)/shard_map/all_gather | solution.py:109
  15.2 15.6 %copy-start.29 = (s32[1024]{0:T(1024)S(1)}, s32[1024]{0:T(1024)}, u32[]{:S(2)}) copy-start(s32[1024]{0:T(1024)} %param.13) | copy-start | bytes 12292
  15.2 15.7 %copy-start.31 = (s32[1,4]{1,0:T(1,128)S(1)}, s32[1,4]{1,0:T(1,128)}, u32[]{:S(2)}) copy-start(s32[1,4]{1,0:T(1,128)} %param.12) | copy-start | bytes 52
  15.2 48.5 %all-to-all-start = ((bf16[128,80,128]{2,1,0:T(8,128)(2,1)}), bf16[128,80,128]{2,1,0:T(8,128)(2,1)}, u32[]{:S(2)}, u32[]{:S(2)}) async-start(bf16[128,80,128]{2,1,0:T(8,128)(2,1)} %copy.38), calls=%async_computation | async-start | bytes 5242880 | tf_op jit(solution)/shard_map/all_to_all | solution.py:86
  26.8 90.3 %all-gather.3.cloned.1.call-start = ((), (), s32[]{:S(2)}) async-start(), calls=%async_computation.2 | async-start | bytes 2162688 | tf_op jit(solution)/shard_map/all_gather | solution.py:110
  27.6 4.9 %copy-start.24 = (f32[9,1024]{1,0:T(8,128)S(1)}, f32[9,1024]{1,0:T(8,128)}, u32[]{:S(2)}) copy-start(f32[9,1024]{1,0:T(8,128)} %param.16) | copy-start | bytes 110596
  27.6 231.9 %reduce-scatter.2.cloned.1.call-start = ((), (), s32[]{:S(2)}) async-start(), calls=%async_computation.4 | async-start | bytes 6488064 | tf_op jit(solution)/shard_map/reduce_scatter | solution.py:154
  30.8 41.1 %copy-start.7 = (bf16[1024,1024]{0,1:T(8,128)(2,1)}, bf16[1024,1024]{0,1:T(8,128)(2,1)S(1)}, u32[]{:S(2)}) copy-start(bf16[1024,1024]{0,1:T(8,128)(2,1)S(1)} %copy.36) | copy-start | bytes 6291460
  31.5 40.4 %copy-start.22 = (f32[1024]{0:T(1024)}, f32[1024]{0:T(1024)S(1)}, u32[]{:S(2)}) copy-start(f32[1024]{0:T(1024)S(1)} %broadcast_multiply_fusion.2) | copy-start | bytes 12292
  32.1 39.8 %copy-start.25 = (f32[1024]{0:T(1024)}, f32[1024]{0:T(1024)S(1)}, u32[]{:S(2)}) copy-start(f32[1024]{0:T(1024)S(1)} %add_rsqrt_fusion) | copy-start | bytes 12292
  32.5 64.7 %copy-start.15 = (f32[1,1024]{1,0:T(1,128)}, f32[1,1024]{1,0:T(1,128)S(1)}, u32[]{:S(2)}) copy-start(f32[1,1024]{1,0:T(1,128)S(1)} %get-tuple-element.65) | copy-start | bytes 12292
  32.5 64.6 %copy-start.16 = (f32[1,1024]{1,0:T(1,128)}, f32[1,1024]{1,0:T(1,128)S(1)}, u32[]{:S(2)}) copy-start(f32[1,1024]{1,0:T(1,128)S(1)} %get-tuple-element.66) | copy-start | bytes 12292
  32.5 64.6 %copy-start.17 = (f32[1,1024]{1,0:T(1,128)}, f32[1,1024]{1,0:T(1,128)S(1)}, u32[]{:S(2)}) copy-start(f32[1,1024]{1,0:T(1,128)S(1)} %get-tuple-element.67) | copy-start | bytes 12292
  32.5 64.6 %copy-start.18 = (f32[1,1024]{1,0:T(1,128)}, f32[1,1024]{1,0:T(1,128)S(1)}, u32[]{:S(2)}) copy-start(f32[1,1024]{1,0:T(1,128)S(1)} %get-tuple-element.68) | copy-start | bytes 12292
  32.5 64.6 %copy-start.19 = (f32[1,1024]{1,0:T(1,128)}, f32[1,1024]{1,0:T(1,128)S(1)}, u32[]{:S(2)}) copy-start(f32[1,1024]{1,0:T(1,128)S(1)} %get-tuple-element.69) | copy-start | bytes 12292
  32.6 64.6 %copy-start.20 = (f32[1,1024]{1,0:T(1,128)}, f32[1,1024]{1,0:T(1,128)S(1)}, u32[]{:S(2)}) copy-start(f32[1,1024]{1,0:T(1,128)S(1)} %get-tuple-element.70) | copy-start | bytes 12292
  32.6 64.6 %copy-start.21 = (f32[1,1024]{1,0:T(1,128)}, f32[1,1024]{1,0:T(1,128)S(1)}, u32[]{:S(2)}) copy-start(f32[1,1024]{1,0:T(1,128)S(1)} %get-tuple-element.71) | copy-start | bytes 12292
  67.4 4.4 %copy-start.27 = (f32[1024]{0:T(1024)S(1)}, f32[1024]{0:T(1024)}, u32[]{:S(2)}) copy-start(f32[1024]{0:T(1024)} %param.14) | copy-start | bytes 12292
  79.3 4.5 %copy-start.9 = (f32[1024,2048]{0,1:T(8,128)}, f32[1024,2048]{0,1:T(8,128)S(1)}, u32[]{:S(2)}) copy-start(f32[1024,2048]{0,1:T(8,128)S(1)} %fusion.38) | copy-start | bytes 25165828
  83.9 13.3 %copy-start = (f32[1024,1024]{0,1:T(8,128)}, f32[1024,1024]{0,1:T(8,128)S(1)}, u32[]{:S(2)}) copy-start(f32[1024,1024]{0,1:T(8,128)S(1)} %get-tuple-element.46) | copy-start | bytes 12582916
  85.5 11.7 %copy-start.3 = (f32[1020,1024]{0,1:T(8,128)}, f32[1020,1024]{0,1:T(8,128)S(1)}, u32[]{:S(2)}) copy-start(f32[1020,1024]{0,1:T(8,128)S(1)} %get-tuple-element.55) | copy-start | bytes 12533764
  85.5 11.7 %copy-start.4 = (f32[1020,1024]{0,1:T(8,128)}, f32[1020,1024]{0,1:T(8,128)S(1)}, u32[]{:S(2)}) copy-start(f32[1020,1024]{0,1:T(8,128)S(1)} %get-tuple-element.56) | copy-start | bytes 12533764
  87.2 10.0 %copy-start.5 = (f32[1021,1024]{0,1:T(8,128)}, f32[1021,1024]{0,1:T(8,128)S(1)}, u32[]{:S(2)}) copy-start(f32[1021,1024]{0,1:T(8,128)S(1)} %get-tuple-element.57) | copy-start | bytes 12546052
  87.2 10.0 %copy-start.6 = (f32[1021,1024]{0,1:T(8,128)}, f32[1021,1024]{0,1:T(8,128)S(1)}, u32[]{:S(2)}) copy-start(f32[1021,1024]{0,1:T(8,128)S(1)} %get-tuple-element.58) | copy-start | bytes 12546052
  97.3 12.6 %copy-start.12 = (bf16[128,8,8,128]{3,1,2,0:T(8,128)(2,1)S(1)}, bf16[128,8,8,128]{3,1,2,0:T(8,128)(2,1)}, u32[]{:S(2)}) copy-start(bf16[128,8,8,128]{3,1,2,0:T(8,128)(2,1)} %copy.62) | copy-start | bytes 6291460
  109.9 7.2 %copy-start.13 = (bf16[128,8,8,128]{3,1,2,0:T(8,128)(2,1)S(1)}, bf16[128,8,8,128]{3,1,2,0:T(8,128)(2,1)}, u32[]{:S(2)}) copy-start(bf16[128,8,8,128]{3,1,2,0:T(8,128)(2,1)} %copy.62) | copy-start | bytes 6291460
  123.3 18.0 %copy-start.1 = (f32[1024,1024]{0,1:T(8,128)}, f32[1024,1024]{0,1:T(8,128)S(1)}, u32[]{:S(2)}) copy-start(f32[1024,1024]{0,1:T(8,128)S(1)} %multiply_multiply_fusion) | copy-start | bytes 12582916
  135.9 5.3 %copy-start.2 = (f32[1024,1024]{0,1:T(8,128)S(1)}, f32[1024,1024]{0,1:T(8,128)}, u32[]{:S(2)}) copy-start(f32[1024,1024]{0,1:T(8,128)} %get-tuple-element.45) | copy-start | bytes 12582916
  135.9 21.9 %slice-start = ((s8[8388608]{0:T(1024)(128)(4,1)}), s8[4194304]{0:T(1024)(128)(4,1)S(1)}, s32[]{:S(2)}) async-start(s8[8388608]{0:T(1024)(128)(4,1)} %bitcast.68), calls=%async_computation.5 | async-start | bytes 8388608
  141.2 16.6 %slice-start.1 = ((s8[8388608]{0:T(1024)(128)(4,1)}), s8[4194304]{0:T(1024)(128)(4,1)S(1)}, s32[]{:S(2)}) async-start(s8[8388608]{0:T(1024)(128)(4,1)} %bitcast.68), calls=%async_computation.6 | async-start | bytes 8388608
  157.8 4.0 %copy-start.8 = (bf16[1024,1024]{0,1:T(8,128)(2,1)S(1)}, bf16[1024,1024]{0,1:T(8,128)(2,1)}, u32[]{:S(2)}) copy-start(bf16[1024,1024]{0,1:T(8,128)(2,1)} %copy-done.7) | copy-start | bytes 6291460
  157.8 4.0 %copy-start.10 = (bf16[1024,1024]{0,1:T(8,128)(2,1)S(1)}, bf16[1024,1024]{0,1:T(8,128)(2,1)}, u32[]{:S(2)}) copy-start(bf16[1024,1024]{0,1:T(8,128)(2,1)} %get-tuple-element.43) | copy-start | bytes 6291460
  157.9 4.0 %copy-start.23 = (f32[1024]{0:T(1024)S(1)}, f32[1024]{0:T(1024)}, u32[]{:S(2)}) copy-start(f32[1024]{0:T(1024)} %copy-done.22) | copy-start | bytes 12292
  157.9 4.0 %copy-start.26 = (f32[1024]{0:T(1024)S(1)}, f32[1024]{0:T(1024)}, u32[]{:S(2)}) copy-start(f32[1024]{0:T(1024)} %copy-done.25) | copy-start | bytes 12292
  157.9 4.0 %copy-start.28 = (f32[1024]{0:T(1024)S(1)}, f32[1024]{0:T(1024)}, u32[]{:S(2)}) copy-start(f32[1024]{0:T(1024)} %param.14) | copy-start | bytes 12292
  174.0 18.2 %copy-start.11 = (bf16[1024,2048]{0,1:T(8,128)(2,1)S(1)}, bf16[1024,2048]{0,1:T(8,128)(2,1)}, u32[]{:S(2)}) copy-start(bf16[1024,2048]{0,1:T(8,128)(2,1)} %pad_maximum_fusion.1) | copy-start | bytes 12582916
  201.5 1.3 collective-permute-start.2
  202.9 13.0 %collective-permute-start.5 = (f32[10,1024]{1,0:T(8,128)S(1)}, f32[10,1024]{1,0:T(8,128)S(1)}, u32[]{:S(2)}, u32[]{:S(2)}) collective-permute-start(f32[10,1024]{1,0:T(8,128)S(1)} %bitcast.76), channel_id=1, source_target_pairs={{0,6},{1,7},{2,4},{3,5},{4,2},{5,3},{6,0},{7,1},{8,14},{9,15},{10,... | collective-permute-start | bytes 122888 | tf_op jit(solution)/shard_map/ppermute | solution.py:53
  205.3 10.6 %collective-permute-start.4 = (f32[10,1024]{1,0:T(8,128)S(1)}, f32[10,1024]{1,0:T(8,128)S(1)}, u32[]{:S(2)}, u32[]{:S(2)}) collective-permute-start(f32[10,1024]{1,0:T(8,128)S(1)} %bitcast.77), channel_id=1, source_target_pairs={{0,4},{1,5},{2,6},{3,7},{4,0},{5,1},{6,2},{7,3},{8,12},{9,13},{10,... | collective-permute-start | bytes 122888 | tf_op jit(solution)/shard_map/ppermute | solution.py:53
  206.1 9.8 %collective-permute-start.3 = (f32[10,1024]{1,0:T(8,128)S(1)}, f32[10,1024]{1,0:T(8,128)S(1)}, u32[]{:S(2)}, u32[]{:S(2)}) collective-permute-start(f32[10,1024]{1,0:T(8,128)S(1)} %bitcast.78), channel_id=1, source_target_pairs={{0,2},{1,3},{2,0},{3,1},{4,6},{5,7},{6,4},{7,5},{8,10},{9,11},{10,... | collective-permute-start | bytes 122888 | tf_op jit(solution)/shard_map/ppermute | solution.py:53
  216.0 5.6 %collective-permute-start.8 = (f32[10,1024]{1,0:T(8,128)S(1)}, f32[10,1024]{1,0:T(8,128)S(1)}, u32[]{:S(2)}, u32[]{:S(2)}) collective-permute-start(f32[10,1024]{1,0:T(8,128)S(1)} %fusion.80), channel_id=1, source_target_pairs={{0,24},{1,25},{2,26},{3,27},{4,28},{5,29},{6,30},{7,31},{8,16},{9,... | collective-permute-start | bytes 122888 | tf_op jit(solution)/shard_map/ppermute | solution.py:53
  218.4 5.8 %collective-permute-start.7 = (f32[10,1024]{1,0:T(8,128)S(1)}, f32[10,1024]{1,0:T(8,128)S(1)}, u32[]{:S(2)}, u32[]{:S(2)}) collective-permute-start(f32[10,1024]{1,0:T(8,128)S(1)} %fusion.80), channel_id=1, source_target_pairs={{0,16},{1,17},{2,18},{3,19},{4,20},{5,21},{6,22},{7,23},{8,24},{9,... | collective-permute-start | bytes 122888 | tf_op jit(solution)/shard_map/ppermute | solution.py:53
  219.2 5.5 %collective-permute-start.6 = (f32[10,1024]{1,0:T(8,128)S(1)}, f32[10,1024]{1,0:T(8,128)S(1)}, u32[]{:S(2)}, u32[]{:S(2)}) collective-permute-start(f32[10,1024]{1,0:T(8,128)S(1)} %fusion.80), channel_id=1, source_target_pairs={{0,8},{1,9},{2,10},{3,11},{4,12},{5,13},{6,14},{7,15},{8,0},{9,1},... | collective-permute-start | bytes 122888 | tf_op jit(solution)/shard_map/ppermute | solution.py:53
  224.8 36.3 %collective-permute-start.11 = (f32[10,1024]{1,0:T(8,128)S(1)}, f32[10,1024]{1,0:T(8,128)S(1)}, u32[]{:S(2)}, u32[]{:S(2)}) collective-permute-start(f32[10,1024]{1,0:T(8,128)S(1)} %fusion.79), channel_id=1, source_target_pairs={{0,96},{32,64},{64,32},{96,0},{1,97},{33,65},{65,33},{97,1},{2,98}... | collective-permute-start | bytes 122888 | tf_op jit(solution)/shard_map/ppermute | solution.py:53
  227.8 33.3 %collective-permute-start.10 = (f32[10,1024]{1,0:T(8,128)S(1)}, f32[10,1024]{1,0:T(8,128)S(1)}, u32[]{:S(2)}, u32[]{:S(2)}) collective-permute-start(f32[10,1024]{1,0:T(8,128)S(1)} %fusion.79), channel_id=1, source_target_pairs={{0,64},{32,96},{64,0},{96,32},{1,65},{33,97},{65,1},{97,33},{2,66}... | collective-permute-start | bytes 122888 | tf_op jit(solution)/shard_map/ppermute | solution.py:53
  228.5 32.6 %collective-permute-start.9 = (f32[10,1024]{1,0:T(8,128)S(1)}, f32[10,1024]{1,0:T(8,128)S(1)}, u32[]{:S(2)}, u32[]{:S(2)}) collective-permute-start(f32[10,1024]{1,0:T(8,128)S(1)} %fusion.79), channel_id=1, source_target_pairs={{0,32},{32,0},{64,96},{96,64},{1,33},{33,1},{65,97},{97,65},{2,34}... | collective-permute-start | bytes 122888 | tf_op jit(solution)/shard_map/ppermute | solution.py:53
  259.5 5.9 %collective-permute-start = (bf16[32,3072]{1,0:T(8,128)(2,1)}, bf16[32,3072]{1,0:T(8,128)(2,1)S(1)}, u32[]{:S(2)}, u32[]{:S(2)}) collective-permute-start(bf16[32,3072]{1,0:T(8,128)(2,1)} %reduce-scatter.2.cloned.1.call-done), channel_id=1, source_target_pairs={{0,32},{32,0},{64,96},{96,64},{1,33},{33,1},{65,97},{97,65},{2,34}... | collective-permute-start | bytes 589832 | tf_op jit(solution)/shard_map/ppermute | solution.py:174
  266.4 7.3 %collective-permute-start.1 = (bf16[32,3072]{1,0:T(8,128)(2,1)S(1)}, bf16[32,3072]{1,0:T(8,128)(2,1)S(1)}, u32[]{:S(2)}, u32[]{:S(2)}) collective-permute-start(bf16[32,3072]{1,0:T(8,128)(2,1)S(1)} %add_convert_fusion), channel_id=1, source_target_pairs={{0,64},{32,96},{64,0},{96,32},{1,65},{33,97},{65,1},{97,33},{2,66}... | collective-permute-start | bytes 589832 | tf_op jit(solution)/shard_map/ppermute | solution.py:180
  (2 other events, 6.3 us)
Sparse Core Ops, SparseCore 0:
  10.2 61.4 all-gather.4
  74.0 43.0 all-gather.2
  174.0 85.4 reduce-scatter.1
